TPU v7x, 256 devices: a whole 4x4x8 slice. The times are simulated.
256 devices in a mesh: expert: 64 (over y, z, core), tensor: 4 (over x).
Axes of the slice: x: 4, y: 4, z: 8, core: 2. Of those that a mesh axis runs over, the one named last changes fastest.
Arguments:
- tokens: bfloat16 [8192, 2048], P('expert', 'tensor'), may hold values from -6 to 6
- labels: int32 [8192, 1], P('expert'), may hold values from 0 to 31, as said below
- domain_ids: int32 [8192], P('expert'), may hold values from 0 to 21
- domain_weights: float32 [22], replicated, may hold values from 0.02 to 0.5
- cotangent: bfloat16 [8192, 2048], P('expert', 'tensor'), may hold values from -6 to 6
- gate_weight: bfloat16 [64, 2048, 2048], P('expert', None, 'tensor'), may hold values from -0.125 to 0.125
- up_weight: bfloat16 [64, 2048, 2048], P('expert', None, 'tensor'), may hold values from -0.125 to 0.125
- down_weight: bfloat16 [64, 2048, 2048], P('expert', 'tensor'), may hold values from -0.09375 to 0.09375
Outputs:
- layer_out: bfloat16 [8192, 2048], P('expert', 'tensor')
- input_grad: bfloat16 [8192, 2048], P('expert', 'tensor')
- gate_grad: bfloat16 [64, 2048, 2048], P('expert', None, 'tensor')
- up_grad: bfloat16 [64, 2048, 2048], P('expert', None, 'tensor')
- down_grad: bfloat16 [64, 2048, 2048], P('expert', 'tensor')
Inputs may be any that keep to these rules, and one draw needn't show every extreme that they name: `labels`: among the rows of one device (aligned blocks of 128 rows) no label appears more than 8 times, and every such block has some label exactly 8 times.
All inputs are finite; a program needn't handle non-finite values.
Results may differ from a plain program's by a relative error of at most 0.0058.
Values may be sent and summed in bfloat16 or wider, within the bound.
No kernel may reach another device: no remote copies, remote signals or barrier semaphores. Data moves between devices by JAX's collectives and lax.ppermute only.
A program may use at most 320 MiB of HBM per device.

v0:
```python
import jax
import jax.numpy as jnp
from jax import lax
from jax.sharding import PartitionSpec as P

SPLIT = 2


def partner(value, axis, stride):
    return lax.ppermute(value, axis, [(i, i ^ 1 << stride) for i in range(lax.axis_size(axis))])


def silu_parts(gate_pre):
    squash = jax.nn.sigmoid(gate_pre)
    return (squash, gate_pre * squash)


def body(
    tokens, labels, domain_ids, domain_weights, cotangent, gate_weight, up_weight, down_weight
):
    n_expert = lax.axis_size("expert")
    tok_rows = tokens.shape[0]
    experts_all = n_expert // SPLIT
    capacity = 2 * tok_rows // experts_all
    half_cap = capacity // 2
    parity = lax.axis_index("expert") % 2
    lang_label = labels[:, 0]
    dom_hot = (
        domain_ids[:, None] == jnp.arange(domain_weights.shape[0], dtype=jnp.int32)[None, :]
    ).astype(jnp.float32)
    tok_scale = jnp.sum(dom_hot * domain_weights[None, :], axis=1)
    grad_rows = (tok_scale[:, None] * cotangent.astype(jnp.float32)).astype(jnp.bfloat16)
    lab_hot = (lang_label[:, None] == jnp.arange(experts_all, dtype=jnp.int32)[None, :]).astype(
        jnp.float32
    )
    row_ids = jnp.arange(tok_rows, dtype=jnp.int32)
    earlier = (row_ids[None, :] < row_ids[:, None]).astype(jnp.float32)
    before = jnp.dot(earlier, lab_hot, precision=lax.Precision.HIGHEST)
    slot_pos = jnp.sum(before * lab_hot, axis=1).astype(jnp.int32)
    target_row = lang_label * capacity + slot_pos
    sources = jnp.stack((tokens, grad_rows))
    sources = lax.all_gather(sources, "tensor", axis=2, tiled=True)
    slot_ids = jnp.arange(n_expert * capacity, dtype=jnp.int32)
    dispatch_map = (slot_ids[:, None] // capacity // SPLIT == lang_label[None, :]) & (
        slot_ids[:, None] % capacity == slot_pos[None, :]
    )
    dispatch_map = dispatch_map.astype(jnp.bfloat16)
    outbound = jnp.einsum(
        "rt,ktw->krw", dispatch_map, sources, preferred_element_type=jnp.float32
    ).astype(jnp.bfloat16)
    outbound = outbound.reshape(2, n_expert, capacity, sources.shape[2])
    arrived = lax.all_to_all(outbound, "expert", split_axis=1, concat_axis=1, tiled=True)
    rows_all = n_expert * capacity
    feat_width = arrived.shape[3]
    routed = arrived[0].reshape(rows_all, feat_width)
    routed_grad = arrived[1].reshape(rows_all, feat_width)
    w_gate = gate_weight[0]
    w_up = up_weight[0]
    w_down = down_weight[0]
    contract_rows = (((0,), (0,)), ((), ()))
    contract_cols = (((1,), (1,)), ((), ()))
    gate_pre = jnp.dot(routed, w_gate, preferred_element_type=jnp.float32)
    up_pre = jnp.dot(routed, w_up, preferred_element_type=jnp.float32)
    squash, activated = silu_parts(gate_pre)
    hidden = (activated * up_pre).astype(jnp.bfloat16)
    out_part = jnp.dot(hidden, w_down, preferred_element_type=jnp.float32)
    grad_hidden = lax.dot_general(
        routed_grad, w_down, contract_cols, preferred_element_type=jnp.float32
    )
    grad_gate_pre = (grad_hidden * up_pre * squash * (1.0 + gate_pre * (1.0 - squash))).astype(
        jnp.bfloat16
    )
    grad_up_pre = (grad_hidden * activated).astype(jnp.bfloat16)
    gate_grad = lax.dot_general(
        routed, grad_gate_pre, contract_rows, preferred_element_type=jnp.float32
    ).astype(jnp.bfloat16)[None]
    up_grad = lax.dot_general(
        routed, grad_up_pre, contract_rows, preferred_element_type=jnp.float32
    ).astype(jnp.bfloat16)[None]
    down_grad = lax.dot_general(
        hidden, routed_grad, contract_rows, preferred_element_type=jnp.float32
    ).astype(jnp.bfloat16)[None]
    input_part = lax.dot_general(
        grad_gate_pre, w_gate, contract_cols, preferred_element_type=jnp.float32
    ) + lax.dot_general(grad_up_pre, w_up, contract_cols, preferred_element_type=jnp.float32)
    out_part = out_part.reshape(n_expert, capacity, feat_width)
    input_part = input_part.reshape(n_expert, capacity, feat_width)
    out_share, input_share = (
        lax.psum_scatter(out_part, "tensor", scatter_dimension=2, tiled=True),
        lax.psum_scatter(input_part, "tensor", scatter_dimension=2, tiled=True),
    )
    partial_value = jnp.stack((out_share, input_share))
    kept = jnp.where(parity == 0, partial_value[:, :, :half_cap], partial_value[:, :, half_cap:])
    handed = jnp.where(parity == 0, partial_value[:, :, half_cap:], partial_value[:, :, :half_cap])
    summed = kept + partner(handed, "expert", 0)
    going_back = summed.astype(jnp.bfloat16)
    returned = lax.all_to_all(going_back, "expert", split_axis=1, concat_axis=1, tiled=True)
    home_ids = jnp.arange(n_expert * half_cap, dtype=jnp.int32)
    home_map = (home_ids[:, None] == target_row[None, :]).astype(jnp.bfloat16)
    flat_back = returned.reshape(2, n_expert * half_cap, returned.shape[3])
    gathered_home = jnp.einsum(
        "rt,krw->ktw", home_map, flat_back, preferred_element_type=jnp.float32
    ).astype(jnp.bfloat16)
    return (gathered_home[0], gathered_home[1], gate_grad, up_grad, down_grad)


def solution(mesh):
    return jax.shard_map(
        body,
        mesh=mesh,
        in_specs=(
            P("expert", "tensor"),
            P("expert", None),
            P("expert"),
            P(),
            P("expert", "tensor"),
            P("expert", None, "tensor"),
            P("expert", None, "tensor"),
            P("expert", "tensor", None),
        ),
        out_specs=(
            P("expert", "tensor"),
            P("expert", "tensor"),
            P("expert", None, "tensor"),
            P("expert", None, "tensor"),
            P("expert", "tensor", None),
        ),
        check_vma=False,
    )
```

profile of v0, /device:TPU:1, one launch (start us, length us, event | category | flops | bytes accessed | tf_op | source)
XLA Modules:
  0.0 302.7 jit_solution(17173675187760145169)
XLA Ops:
  7.2 0.9 select_reduce_fusion
  8.1 1.0 fusion.24
  9.1 1.6 pad_maximum_fusion.1
  10.8 0.9 fusion.15
  11.7 28.7 %all-gather.2.cloned.1.call-done = bf16[2,128,2048]{2,1,0:T(8,128)(2,1)} async-done(((bf16[2,128,512]{2,1,0:T(8,128)(2,1)}), bf16[2,128,2048]{2,1,0:T(8,128)(2,1)}) %all-gather.2.cloned.1.call-update) | async-done | bytes 1048592 | tf_op jit(solution)/shard_map/all_gather | solution.py:42
  40.4 2.5 convert_bitcast_fusion
  43.5 107.7 %all_to_all.10 = bf16[2,64,8,2048]{3,2,0,1:T(8,128)(2,1)S(1)} all-to-all(bf16[2,64,8,2048]{3,2,0,1:T(8,128)(2,1)S(1)} %copy.27), channel_id=1, replica_groups=mesh['expert'=64,'tensor'=4] {'expert'}, dimensions={1} | all-to-all | bytes 8388608 | tf_op jit(solution)/shard_map/all_to_all | solution.py:52
  151.3 1.2 fusion.12
  152.5 1.9 copy-done.5
  154.4 1.3 fusion.5
  155.7 1.6 multiply_convert_fusion.2
  157.3 1.3 fusion.10
  158.7 3.3 %add_bitcast_fusion = f32[64,8,2048]{2,1,0:T(8,128)} fusion(f32[512,2048]{1,0:T(8,128)S(1)} %fusion.10, bf16[512,512]{1,0:T(8,128)(2,1)S(1)} %get-tuple-element.27, bf16[1,2048,512]{2,1,0:T(8,128)(2,1)S(1)} %copy-done), kind=kOutput, calls=%fused_computation | convolution fusion | flops 1074790400 | bytes 11010048 | tf_op jit(solution)/shard_map/dot_general | solution.py:85
  162.0 4.8 %fusion.3 = f32[64,8,2048]{2,1,0:T(8,128)} fusion(bf16[1,512,2048]{2,1,0:T(8,128)(2,1)} %param.15, bf16[512,512]{1,0:T(8,128)(2,1)S(1)} %get-tuple-element.25), kind=kOutput, calls=%fused_computation.12 | convolution fusion | flops 1073741824 | bytes 6815744 | tf_op jit(solution)/shard_map/dot_general | solution.py:66
  166.9 40.1 %reduce-scatter.5.cloned.1.call-done = f32[64,8,512]{2,1,0:T(8,128)} async-done(((f32[64,8,2048]{2,1,0:T(8,128)}), f32[64,8,512]{2,1,0:T(8,128)}) %reduce-scatter.5.cloned.1.call-update) | async-done | bytes 1048592 | tf_op jit(solution)/shard_map/reduce_scatter | solution.py:90
  207.0 51.8 %reduce-scatter.3.cloned.1.call-done = f32[64,8,512]{2,1,0:T(8,128)} async-done(((f32[64,8,2048]{2,1,0:T(8,128)}), f32[64,8,512]{2,1,0:T(8,128)}) %reduce-scatter.3.cloned.1.call-update) | async-done | bytes 1048592 | tf_op jit(solution)/shard_map/reduce_scatter | solution.py:89
  258.8 2.8 broadcast_select_fusion
  262.4 2.3 collective-permute-done
  265.1 1.0 copy.28
  266.1 10.4 %all-to-all-start.1 = ((bf16[2,64,4,512]{3,2,0,1:T(4,128)(2,1)}), bf16[2,64,4,512]{3,2,0,1:T(4,128)(2,1)S(1)}, u32[]{:S(2)}, u32[]{:S(2)}) async-start(bf16[2,64,4,512]{3,2,0,1:T(4,128)(2,1)} %copy.28), calls=%async_computation.3 | async-start | bytes 1048576 | tf_op jit(solution)/shard_map/all_to_all | solution.py:97
  276.5 4.5 %fusion.2 = bf16[1,512,2048]{2,1,0:T(8,128)(2,1)} fusion(bf16[512,512]{1,0:T(8,128)(2,1)} %copy-done.9, bf16[2,64,8,2048]{3,2,0,1:T(8,128)(2,1)} %copy-done.1), kind=kOutput, calls=%fused_computation.7 | convolution fusion | flops 1074790400 | bytes 4718592 | tf_op jit(solution)/shard_map/dot_general | solution.py:80
  281.0 2.6 fusion
  283.7 2.6 fusion.1
  286.3 7.5 %all-to-all-done.1 = bf16[2,64,4,512]{3,2,0,1:T(4,128)(2,1)S(1)} async-done(((bf16[2,64,4,512]{3,2,0,1:T(4,128)(2,1)}), bf16[2,64,4,512]{3,2,0,1:T(4,128)(2,1)S(1)}, u32[]{:S(2)}, u32[]{:S(2)}) %all-to-all-start.1) | async-done | bytes 524320 | tf_op jit(solution)/shard_map/all_to_all | solution.py:97
  (42 shorter events, 4.3 us)
Async XLA Ops:
  7.2 148.5 %copy-start = (bf16[1,2048,512]{2,1,0:T(8,128)(2,1)S(1)}, bf16[1,2048,512]{2,1,0:T(8,128)(2,1)}, u32[]{:S(2)}) copy-start(bf16[1,2048,512]{2,1,0:T(8,128)(2,1)} %param.14) | copy-start | bytes 6291460
  7.2 33.2 %all-gather.2.cloned.1.call-start = ((), (), s32[]{:S(2)}) async-start(), calls=%async_computation.4 | async-start | bytes 1310720 | tf_op jit(solution)/shard_map/all_gather | solution.py:42
  10.8 196.2 %reduce-scatter.5.cloned.1.call-start = ((), (), s32[]{:S(2)}) async-start(), calls=%async_computation.6 | async-start | bytes 5242880 | tf_op jit(solution)/shard_map/reduce_scatter | solution.py:90
  43.5 107.7 %copy-start.6 = (bf16[1,2048,512]{2,1,0:T(8,128)(2,1)S(1)}, bf16[1,2048,512]{2,1,0:T(8,128)(2,1)}, u32[]{:S(2)}) copy-start(bf16[1,2048,512]{2,1,0:T(8,128)(2,1)} %param.13) | copy-start | bytes 6291460
  151.2 4.4 %copy-start.1 = (bf16[2,64,8,2048]{3,2,0,1:T(8,128)(2,1)}, bf16[2,64,8,2048]{3,2,0,1:T(8,128)(2,1)S(1)}, u32[]{:S(2)}) copy-start(bf16[2,64,8,2048]{3,2,0,1:T(8,128)(2,1)S(1)} %all_to_all.10) | copy-start | bytes 12582916
  151.2 3.1 %copy-start.5 = (bf16[1,512,2048]{2,1,0:T(8,128)(2,1)S(1)}, bf16[1,512,2048]{2,1,0:T(8,128)(2,1)}, u32[]{:S(2)}) copy-start(bf16[1,512,2048]{2,1,0:T(8,128)(2,1)} %param.15) | copy-start | bytes 6291460
  157.3 1.3 copy-start.7
  157.3 1.3 copy-start.10
  157.3 4.7 %copy-start.9 = (bf16[512,512]{1,0:T(8,128)(2,1)}, bf16[512,512]{1,0:T(8,128)(2,1)S(1)}, u32[]{:S(2)}) copy-start(bf16[512,512]{1,0:T(8,128)(2,1)S(1)} %get-tuple-element.25) | copy-start | bytes 1572868
  161.9 96.9 %reduce-scatter.3.cloned.1.call-start = ((), (), s32[]{:S(2)}) async-start(), calls=%async_computation.5 | async-start | bytes 5242880 | tf_op jit(solution)/shard_map/reduce_scatter | solution.py:89
  207.0 57.7 %copy-start.3 = (f32[64,8,512]{2,1,0:T(8,128)S(1)}, f32[64,8,512]{2,1,0:T(8,128)}, u32[]{:S(2)}) copy-start(f32[64,8,512]{2,1,0:T(8,128)} %reduce-scatter.5.cloned.1.call-done) | copy-start | bytes 3145732
  258.8 5.8 %copy-start.4 = (f32[64,8,512]{2,1,0:T(8,128)S(1)}, f32[64,8,512]{2,1,0:T(8,128)}, u32[]{:S(2)}) copy-start(f32[64,8,512]{2,1,0:T(8,128)} %reduce-scatter.3.cloned.1.call-done) | copy-start | bytes 3145732
  261.6 14.8 %copy-start.12 = (s32[128,1]{0,1:T(1,128)S(1)}, s32[128,1]{0,1:T(1,128)}, u32[]{:S(2)}) copy-start(s32[128,1]{0,1:T(1,128)} %param.9) | copy-start | bytes 1540
  261.7 3.0 collective-permute-start
  266.1 27.7 %all-to-all-start.1 = ((bf16[2,64,4,512]{3,2,0,1:T(4,128)(2,1)}), bf16[2,64,4,512]{3,2,0,1:T(4,128)(2,1)S(1)}, u32[]{:S(2)}, u32[]{:S(2)}) async-start(bf16[2,64,4,512]{3,2,0,1:T(4,128)(2,1)} %copy.28), calls=%async_computation.3 | async-start | bytes 1048576 | tf_op jit(solution)/shard_map/all_to_all | solution.py:97
  276.5 4.5 %copy-start.2 = (bf16[2,64,8,2048]{3,2,0,1:T(8,128)(2,1)S(1)}, bf16[2,64,8,2048]{3,2,0,1:T(8,128)(2,1)}, u32[]{:S(2)}) copy-start(bf16[2,64,8,2048]{3,2,0,1:T(8,128)(2,1)} %copy-done.1) | copy-start | bytes 12582916
  276.5 4.5 %copy-start.8 = (bf16[512,512]{1,0:T(8,128)(2,1)S(1)}, bf16[512,512]{1,0:T(8,128)(2,1)}, u32[]{:S(2)}) copy-start(bf16[512,512]{1,0:T(8,128)(2,1)} %copy-done.7) | copy-start | bytes 1572868
  281.0 2.6 copy-start.11
Sparse Core Ops, SparseCore 0:
  10.9 29.4 all-gather.1
  162.1 44.8 reduce-scatter.4
  209.7 49.0 reduce-scatter.2
where the time goes:
time: 303 us
  waiting for transfers between devices  130 us (43%)
  blocking collectives  108 us (36%)
  matrix products  27 us (9%)
  between operations  14 us (5%)
  starting transfers between devices  11.2 us (4%)
  other arithmetic  6.76 us (2%)
  local copies, waits for them, and re-layouts  5.46 us (2%)
    all_to_all x1, blocking collectives, body(): lax.all_to_all(outbound, 'expert', split_axis=1, concat_axis=1, tiled=True)  108 us
    reduce_scatter x1, waiting for transfers between devices, body(): lax.psum_scatter(out_part, 'tensor', scatter_dimension=2, tiled=True)  51.8 us
    reduce_scatter x1, waiting for transfers between devices, body(): lax.psum_scatter(input_part, 'tensor', scatter_dimension=2, tiled=True)  40.1 us
    all_gather x1, waiting for transfers between devices, body(): sources = lax.all_gather(sources, 'tensor', axis=2, tiled=True)  28.7 us
    all_to_all x1, starting transfers between devices, body(): lax.all_to_all(going_back, 'expert', split_axis=1, concat_axis=1, tiled=T...  10.4 us
    all_to_all x1, waiting for transfers between devices, body(): lax.all_to_all(going_back, 'expert', split_axis=1, concat_axis=1, tiled=T...  7.52 us
  transfers between devices with their start and end apart: 5, of which 5 were waited for; matrix products, arithmetic and copies ran while one was open for 5% of the time, Pallas kernels for 0%

commit v1 on v0

--- a/solution.py
+++ b/solution.py
@@ -10,6 +10,11 @@
     return lax.ppermute(value, axis, [(i, i ^ 1 << stride) for i in range(lax.axis_size(axis))])
 
 
+def shifted(value, axis, step):
+    size = lax.axis_size(axis)
+    return lax.ppermute(value, axis, [(i, (i + step) % size) for i in range(size)])
+
+
 def silu_parts(gate_pre):
     squash = jax.nn.sigmoid(gate_pre)
     return (squash, gate_pre * squash)
@@ -19,11 +24,13 @@
     tokens, labels, domain_ids, domain_weights, cotangent, gate_weight, up_weight, down_weight
 ):
     n_expert = lax.axis_size("expert")
+    n_tensor = lax.axis_size("tensor")
     tok_rows = tokens.shape[0]
+    feat_slice = tokens.shape[1]
     experts_all = n_expert // SPLIT
-    capacity = 2 * tok_rows // experts_all
-    half_cap = capacity // 2
-    parity = lax.axis_index("expert") % 2
+    capacity = SPLIT * tok_rows // experts_all
+    half_cap = capacity // SPLIT
+    t_idx = lax.axis_index("tensor")
     lang_label = labels[:, 0]
     dom_hot = (
         domain_ids[:, None] == jnp.arange(domain_weights.shape[0], dtype=jnp.int32)[None, :]
@@ -38,22 +45,24 @@
     before = jnp.dot(earlier, lab_hot, precision=lax.Precision.HIGHEST)
     slot_pos = jnp.sum(before * lab_hot, axis=1).astype(jnp.int32)
     target_row = lang_label * capacity + slot_pos
+    rows_out = n_expert * half_cap
     sources = jnp.stack((tokens, grad_rows))
-    sources = lax.all_gather(sources, "tensor", axis=2, tiled=True)
-    slot_ids = jnp.arange(n_expert * capacity, dtype=jnp.int32)
-    dispatch_map = (slot_ids[:, None] // capacity // SPLIT == lang_label[None, :]) & (
-        slot_ids[:, None] % capacity == slot_pos[None, :]
-    )
-    dispatch_map = dispatch_map.astype(jnp.bfloat16)
+    dispatch_map = (
+        jnp.arange(rows_out, dtype=jnp.int32)[:, None] == target_row[None, :]
+    ).astype(jnp.bfloat16)
     outbound = jnp.einsum(
         "rt,ktw->krw", dispatch_map, sources, preferred_element_type=jnp.float32
     ).astype(jnp.bfloat16)
-    outbound = outbound.reshape(2, n_expert, capacity, sources.shape[2])
+    outbound = outbound.reshape(2, n_expert, half_cap, feat_slice)
     arrived = lax.all_to_all(outbound, "expert", split_axis=1, concat_axis=1, tiled=True)
-    rows_all = n_expert * capacity
-    feat_width = arrived.shape[3]
-    routed = arrived[0].reshape(rows_all, feat_width)
-    routed_grad = arrived[1].reshape(rows_all, feat_width)
+    pieces = [arrived] + [shifted(arrived, "tensor", k) for k in range(1, n_tensor)]
+    reversed_pieces = jnp.stack([pieces[(-m) % n_tensor] for m in range(n_tensor)])
+    ordered = jnp.roll(reversed_pieces, t_idx, axis=0)
+    own_rows = jnp.moveaxis(ordered, 0, 3).reshape(2, rows_out, n_tensor * feat_slice)
+    other_rows = partner(own_rows, "expert", 0)
+    routed_both = jnp.concatenate((own_rows, other_rows), axis=1)
+    routed = routed_both[0]
+    routed_grad = routed_both[1]
     w_gate = gate_weight[0]
     w_up = up_weight[0]
     w_down = down_weight[0]
@@ -83,21 +92,19 @@
     input_part = lax.dot_general(
         grad_gate_pre, w_gate, contract_cols, preferred_element_type=jnp.float32
     ) + lax.dot_general(grad_up_pre, w_up, contract_cols, preferred_element_type=jnp.float32)
-    out_part = out_part.reshape(n_expert, capacity, feat_width)
-    input_part = input_part.reshape(n_expert, capacity, feat_width)
-    out_share, input_share = (
-        lax.psum_scatter(out_part, "tensor", scatter_dimension=2, tiled=True),
-        lax.psum_scatter(input_part, "tensor", scatter_dimension=2, tiled=True),
-    )
-    partial_value = jnp.stack((out_share, input_share))
-    kept = jnp.where(parity == 0, partial_value[:, :, :half_cap], partial_value[:, :, half_cap:])
-    handed = jnp.where(parity == 0, partial_value[:, :, half_cap:], partial_value[:, :, :half_cap])
-    summed = kept + partner(handed, "expert", 0)
-    going_back = summed.astype(jnp.bfloat16)
+    partial_value = jnp.stack((out_part, input_part))
+    core_sum = partial_value[:, :rows_out] + partner(partial_value[:, rows_out:], "expert", 0)
+    chunks = core_sum.reshape(2, rows_out, n_tensor, feat_slice)
+    acc = lax.dynamic_index_in_dim(chunks, t_idx, axis=2, keepdims=False)
+    for k in range(1, n_tensor):
+        sent = lax.dynamic_index_in_dim(chunks, (t_idx + k) % n_tensor, axis=2, keepdims=False)
+        acc = acc + shifted(sent, "tensor", k)
+    going_back = acc.astype(jnp.bfloat16).reshape(2, n_expert, half_cap, feat_slice)
     returned = lax.all_to_all(going_back, "expert", split_axis=1, concat_axis=1, tiled=True)
-    home_ids = jnp.arange(n_expert * half_cap, dtype=jnp.int32)
-    home_map = (home_ids[:, None] == target_row[None, :]).astype(jnp.bfloat16)
-    flat_back = returned.reshape(2, n_expert * half_cap, returned.shape[3])
+    flat_back = returned.reshape(2, rows_out, feat_slice)
+    home_map = (
+        jnp.arange(rows_out, dtype=jnp.int32)[:, None] == target_row[None, :]
+    ).astype(jnp.bfloat16)
     gathered_home = jnp.einsum(
         "rt,krw->ktw", home_map, flat_back, preferred_element_type=jnp.float32
     ).astype(jnp.bfloat16)

time: 303 us -> 202 us (0.67)
  blocking collectives: 108 us -> 30.3 us
  waiting for transfers between devices: 130 us -> 89.6 us
  local copies, waits for them, and re-layouts: 5.46 us -> 36.3 us
  between operations: 14 us -> 0.96 us
  matrix products: 27 us -> 20.3 us
  other arithmetic: 6.76 us -> 12.2 us
    reduce_scatter x2 -> x0, waiting for transfers between devices: 92 us -> none  [the longest x1 51.8 us: body(): lax.psum_scatter(out_part, 'tensor', scatter_dimension=2, tiled=True)]
    all_to_all x1, blocking collectives: 108 us -> 30.3 us  [body(): lax.all_to_all(outbound, 'expert', split_axis=1, concat_axis=1, tiled=True)]
    ppermute x0 -> x6, waiting for transfers between devices: none -> 72.6 us  [shifted(): lax.ppermute(value, axis, [(i, (i + step) % size) for i in range(size)])]
    all_gather x1 -> x0, waiting for transfers between devices: 28.7 us -> none  [body(): sources = lax.all_gather(sources, 'tensor', axis=2, tiled=True)]
    dynamic_slice x0 -> x1, local copies, waits for them, and re-layouts: none -> 10.6 us  [body(): acc = lax.dynamic_index_in_dim(chunks, t_idx, axis=2, keepdims=False)]
    reshape x1 -> x4, local copies, waits for them, and re-layouts: 0.58 us -> 10.8 us  [the longest x1 6.09 us: body(): chunks = core_sum.reshape(2, rows_out, n_tensor, feat_slice)]
    ppermute x1 -> x2, waiting for transfers between devices: 2.29 us -> 9.26 us  [partner(): lax.ppermute(value, axis, [(i, i ^ 1 << stride) for i in range(lax.axis_s...]
    add x0 -> x1, other arithmetic: none -> 6.48 us  [body(): partial_value[:, :rows_out]]
  transfers between devices with their start and end apart: 5 -> 9, of which waited for: 5 -> 8; matrix products, arithmetic and copies ran while one was open for 5% -> 6% of each run, Pallas kernels for 0% -> 0%
where the time goes in v1:
time: 202 us
  waiting for transfers between devices  89.6 us (44%)
  local copies, waits for them, and re-layouts  36.3 us (18%)
  blocking collectives  30.3 us (15%)
  matrix products  20.3 us (10%)
  starting transfers between devices  12.3 us (6%)
  other arithmetic  12.2 us (6%)
    ppermute x6, waiting for transfers between devices, shifted(): lax.ppermute(value, axis, [(i, (i + step) % size) for i in range(size)])  72.6 us
    all_to_all x1, blocking collectives, body(): lax.all_to_all(outbound, 'expert', split_axis=1, concat_axis=1, tiled=True)  30.3 us
    dynamic_slice x1, local copies, waits for them, and re-layouts, body(): acc = lax.dynamic_index_in_dim(chunks, t_idx, axis=2, keepdims=False)  10.6 us
    ppermute x2, waiting for transfers between devices, partner(): lax.ppermute(value, axis, [(i, i ^ 1 << stride) for i in range(lax.axis_s...  9.26 us
    unnamed x37, local copies, waits for them, and re-layouts  9.14 us
    all_to_all x1, waiting for transfers between devices, body(): lax.all_to_all(going_back, 'expert', split_axis=1, concat_axis=1, tiled=T...  7.68 us
    add x1, other arithmetic, body(): partial_value[:, :rows_out]  6.48 us
    all_to_all x1, starting transfers between devices, body(): lax.all_to_all(going_back, 'expert', split_axis=1, concat_axis=1, tiled=T...  6.12 us
  transfers between devices with their start and end apart: 9, of which 8 were waited for; matrix products, arithmetic and copies ran while one was open for 6% of the time, Pallas kernels for 0%

profile of v1, /device:TPU:1, one launch (start us, length us, event | category | flops | bytes accessed | tf_op | source)
XLA Modules:
  0.0 201.9 jit_solution(12338603505528669869)
XLA Ops:
  5.6 30.3 %all_to_all.10 = bf16[2,64,4,512]{3,2,0,1:T(4,128)(2,1)S(1)} all-to-all(bf16[2,64,4,512]{3,2,0,1:T(4,128)(2,1)S(1)} %copy.45), channel_id=1, replica_groups=mesh['expert'=64,'tensor'=4] {'expert'}, dimensions={1} | all-to-all | bytes 1048576 | tf_op jit(solution)/shard_map/all_to_all | solution.py:57
  36.8 2.5 %collective-permute-start = (bf16[2,64,4,512]{3,1,2,0:T(8,128)(2,1)}, bf16[2,64,4,512]{3,1,2,0:T(8,128)(2,1)S(1)}, u32[]{:S(2)}, u32[]{:S(2)}) collective-permute-start(bf16[2,64,4,512]{3,1,2,0:T(8,128)(2,1)} %copy.46), channel_id=1, source_target_pairs={{0,3},{1,0},{2,1},{3,2},{4,7},{5,4},{6,5},{7,6},{8,11},{9,8},{10,9... | collective-permute-start | bytes 1572872 | tf_op jit(solution)/shard_map/ppermute | solution.py:15
  40.6 21.1 %collective-permute-done = bf16[2,64,4,512]{3,1,2,0:T(8,128)(2,1)S(1)} collective-permute-done((bf16[2,64,4,512]{3,1,2,0:T(8,128)(2,1)}, bf16[2,64,4,512]{3,1,2,0:T(8,128)(2,1)S(1)}, u32[]{:S(2)}, u32[]{:S(2)}) %collective-permute-start) | collective-permute-done | bytes 524320 | tf_op jit(solution)/shard_map/ppermute | solution.py:15
  62.8 3.2 %collective-permute-done.2 = bf16[2,64,4,512]{3,1,2,0:T(8,128)(2,1)S(1)} collective-permute-done((bf16[2,64,4,512]{3,1,2,0:T(8,128)(2,1)}, bf16[2,64,4,512]{3,1,2,0:T(8,128)(2,1)S(1)}, u32[]{:S(2)}, u32[]{:S(2)}) %collective-permute-start.2) | collective-permute-done | bytes 524320 | tf_op jit(solution)/shard_map/ppermute | solution.py:15
  67.7 3.0 %copy.50 = bf16[2,64,4,4,512]{4,3,2,1,0:T(4,128)(2,1)} copy(bf16[2,64,4,4,512]{4,1,2,0,3:T(8,128)(2,1)S(1)} %dynamic-slice_bitcast_fusion) | data formatting | bytes 4194304 | tf_op jit(solution)/shard_map/transpose | solution.py:61
  70.7 4.4 %reshape.38 = bf16[2,256,2048]{2,1,0:T(8,128)(2,1)} reshape(bf16[2,64,4,4,512]{4,3,2,1,0:T(4,128)(2,1)} %copy.50) | data formatting | bytes 4194304 | tf_op jit(solution)/shard_map/reshape | solution.py:61
  75.6 1.9 constant_dynamic-update-slice_fusion.1
  77.5 2.1 %collective-permute-done.3 = bf16[2,256,2048]{2,1,0:T(8,128)(2,1)S(1)} collective-permute-done((bf16[2,256,2048]{2,1,0:T(8,128)(2,1)}, bf16[2,256,2048]{2,1,0:T(8,128)(2,1)S(1)}, u32[]{:S(2)}, u32[]{:S(2)}) %collective-permute-start.3) | collective-permute-done | bytes 2097184 | tf_op jit(solution)/shard_map/ppermute | solution.py:10
  81.1 1.8 copy-done.4
  84.3 1.6 multiply_convert_fusion.2
  88.6 1.4 add_bitcast_fusion
  90.6 2.8 %pad_maximum_fusion = f32[2,256,2048]{2,1,0:T(8,128)} fusion(f32[1,512,2048]{2,1,0:T(8,128)S(1)} %add_bitcast_fusion, f32[1,512,2048]{2,1,0:T(8,128)S(1)} %convolution_bitcast_fusion), kind=kLoop, calls=%fused_computation.4 | loop fusion | flops 1048576 | bytes 12582912 | tf_op jit(solution)/shard_map/stack | solution.py:95
  94.2 7.1 %collective-permute-done.4 = f32[2,256,2048]{2,1,0:T(8,128)} collective-permute-done((f32[2,256,2048]{2,1,0:T(8,128)}, f32[2,256,2048]{2,1,0:T(8,128)}, u32[]{:S(2)}, u32[]{:S(2)}) %collective-permute-start.4) | collective-permute-done | bytes 4194336 | tf_op jit(solution)/shard_map/ppermute | solution.py:10
  101.3 6.5 %fusion.1 = f32[2,256,2048]{2,1,0:T(8,128)} fusion(f32[2,256,2048]{2,1,0:T(8,128)} %collective-permute-done.4, f32[1,512,2048]{2,1,0:T(8,128)} %copy-done.3, f32[1,512,2048]{2,1,0:T(8,128)} %copy-done.2), kind=kLoop, calls=%fused_computation.3 | loop fusion | flops 2097152 | bytes 16777216 | tf_op jit(solution)/shard_map/add | solution.py:96
  107.8 6.1 %reshape.39 = f32[2,256,4,512]{3,2,1,0:T(4,128)} reshape(f32[2,256,2048]{2,1,0:T(8,128)} %fusion.1) | data formatting | bytes 8388608 | tf_op jit(solution)/shard_map/reshape | solution.py:97
  113.9 10.6 %constant_dynamic-slice_fusion.3 = (f32[2,256,1,512]{3,2,1,0:T(1,128)S(1)}, f32[2,256,1,512]{3,2,1,0:T(1,128)S(1)}, f32[2,256,1,512]{3,2,1,0:T(1,128)S(1)}, f32[2,256,1,512]{3,2,1,0:T(1,128)S(1)}) fusion(f32[2,256,4,512]{3,2,1,0:T(4,128)} %reshape.39, s32[]{:T(128)S(6)} %select_n.42, s32[]{:T(128)S(6)} %select_n.48, s32[]{:T(128)S(6)} %select_n.46, ...), kind=kLoop, calls=%fused_computation.74 | loop fusion | bytes 8388624 | tf_op jit(solution)/shard_map/jit(dynamic_index_in_dim)/dynamic_slice | solution.py:98
  126.4 22.6 %collective-permute-done.7 = f32[2,256,512]{2,1,0:T(8,128)S(1)} collective-permute-done((f32[2,256,512]{2,1,0:T(8,128)S(1)}, f32[2,256,512]{2,1,0:T(8,128)S(1)}, u32[]{:S(2)}, u32[]{:S(2)}) %collective-permute-start.7) | collective-permute-done | bytes 1048608 | tf_op jit(solution)/shard_map/ppermute | solution.py:15
  148.9 2.3 %collective-permute-done.6 = f32[2,256,512]{2,1,0:T(8,128)S(1)} collective-permute-done((f32[2,256,512]{2,1,0:T(8,128)S(1)}, f32[2,256,512]{2,1,0:T(8,128)S(1)}, u32[]{:S(2)}, u32[]{:S(2)}) %collective-permute-start.6) | collective-permute-done | bytes 1048608 | tf_op jit(solution)/shard_map/ppermute | solution.py:15
  151.2 23.5 %collective-permute-done.5 = f32[2,256,512]{2,1,0:T(8,128)S(1)} collective-permute-done((f32[2,256,512]{2,1,0:T(8,128)S(1)}, f32[2,256,512]{2,1,0:T(8,128)S(1)}, u32[]{:S(2)}, u32[]{:S(2)}) %collective-permute-start.5) | collective-permute-done | bytes 1048608 | tf_op jit(solution)/shard_map/ppermute | solution.py:15
  176.5 6.1 %all-to-all-start.1 = ((bf16[2,64,4,512]{3,0,2,1:T(2,128)(2,1)}), bf16[2,64,4,512]{3,0,2,1:T(2,128)(2,1)S(1)}, u32[]{:S(2)}, u32[]{:S(2)}) async-start(bf16[2,64,4,512]{3,0,2,1:T(2,128)(2,1)} %bitcast.18), calls=%async_computation.1 | async-start | bytes 1048576 | tf_op jit(solution)/shard_map/all_to_all | solution.py:103
  182.7 4.3 %fusion.4 = bf16[1,512,2048]{2,1,0:T(8,128)(2,1)} fusion(bf16[512,512]{1,0:T(8,128)(2,1)S(1)} %copy-done.9, bf16[2,512,2048]{2,1,0:T(8,128)(2,1)} %copy-done.6), kind=kOutput, calls=%fused_computation.12 | convolution fusion | flops 1074790400 | bytes 4718592 | tf_op jit(solution)/shard_map/dot_general | solution.py:89
  187.0 2.6 %fusion.2 = bf16[1,2048,512]{2,1,0:T(8,128)(2,1)} fusion(bf16[512,512]{1,0:T(8,128)(2,1)S(1)} %get-tuple-element.35, bf16[2,512,2048]{2,1,0:T(8,128)(2,1)S(1)} %copy-done.7), kind=kOutput, calls=%fused_computation.10 | convolution fusion | flops 1074790400 | bytes 4718592 | tf_op jit(solution)/shard_map/dot_general | solution.py:83
  189.7 2.6 %fusion.3 = bf16[1,2048,512]{2,1,0:T(8,128)(2,1)} fusion(bf16[512,512]{1,0:T(8,128)(2,1)S(1)} %copy-done.11, bf16[2,512,2048]{2,1,0:T(8,128)(2,1)S(1)} %copy-done.7), kind=kOutput, calls=%fused_computation.11 | convolution fusion | flops 1074790400 | bytes 4718592 | tf_op jit(solution)/shard_map/dot_general | solution.py:86
  192.3 7.7 %all-to-all-done.1 = bf16[2,64,4,512]{3,0,2,1:T(2,128)(2,1)S(1)} async-done(((bf16[2,64,4,512]{3,0,2,1:T(2,128)(2,1)}), bf16[2,64,4,512]{3,0,2,1:T(2,128)(2,1)S(1)}, u32[]{:S(2)}, u32[]{:S(2)}) %all-to-all-start.1) | async-done | bytes 524320 | tf_op jit(solution)/shard_map/all_to_all | solution.py:103
  (62 shorter events, 22.9 us)
Async XLA Ops:
  0.6 83.6 %copy-start = (bf16[1,2048,512]{2,1,0:T(8,128)(2,1)S(1)}, bf16[1,2048,512]{2,1,0:T(8,128)(2,1)}, u32[]{:S(2)}) copy-start(bf16[1,2048,512]{2,1,0:T(8,128)(2,1)} %param.14) | copy-start | bytes 6291460
  36.8 24.9 %collective-permute-start = (bf16[2,64,4,512]{3,1,2,0:T(8,128)(2,1)}, bf16[2,64,4,512]{3,1,2,0:T(8,128)(2,1)S(1)}, u32[]{:S(2)}, u32[]{:S(2)}) collective-permute-start(bf16[2,64,4,512]{3,1,2,0:T(8,128)(2,1)} %copy.46), channel_id=1, source_target_pairs={{0,3},{1,0},{2,1},{3,2},{4,7},{5,4},{6,5},{7,6},{8,11},{9,8},{10,9... | collective-permute-start | bytes 1572872 | tf_op jit(solution)/shard_map/ppermute | solution.py:15
  39.3 22.5 %collective-permute-start.1 = (bf16[2,64,4,512]{3,1,2,0:T(8,128)(2,1)}, bf16[2,64,4,512]{3,1,2,0:T(8,128)(2,1)}, u32[]{:S(2)}, u32[]{:S(2)}) collective-permute-start(bf16[2,64,4,512]{3,1,2,0:T(8,128)(2,1)} %copy.46), channel_id=1, source_target_pairs={{0,2},{1,3},{2,0},{3,1},{4,6},{5,7},{6,4},{7,5},{8,10},{9,11},{10,... | collective-permute-start | bytes 1572872 | tf_op jit(solution)/shard_map/ppermute | solution.py:15
  39.8 26.3 %collective-permute-start.2 = (bf16[2,64,4,512]{3,1,2,0:T(8,128)(2,1)}, bf16[2,64,4,512]{3,1,2,0:T(8,128)(2,1)S(1)}, u32[]{:S(2)}, u32[]{:S(2)}) collective-permute-start(bf16[2,64,4,512]{3,1,2,0:T(8,128)(2,1)} %copy.46), channel_id=1, source_target_pairs={{0,1},{1,2},{2,3},{3,0},{4,5},{5,6},{6,7},{7,4},{8,9},{9,10},{10,1... | collective-permute-start | bytes 1572872 | tf_op jit(solution)/shard_map/ppermute | solution.py:15
  75.1 4.7 %copy-start.5 = (bf16[1,2048,512]{2,1,0:T(8,128)(2,1)S(1)}, bf16[1,2048,512]{2,1,0:T(8,128)(2,1)}, u32[]{:S(2)}) copy-start(bf16[1,2048,512]{2,1,0:T(8,128)(2,1)} %param.13) | copy-start | bytes 6291460
  75.1 4.5 %collective-permute-start.3 = (bf16[2,256,2048]{2,1,0:T(8,128)(2,1)}, bf16[2,256,2048]{2,1,0:T(8,128)(2,1)S(1)}, u32[]{:S(2)}, u32[]{:S(2)}) collective-permute-start(bf16[2,256,2048]{2,1,0:T(8,128)(2,1)} %reshape.38), channel_id=1, source_target_pairs={{0,4},{4,0},{8,12},{12,8},{16,20},{20,16},{24,28},{28,24},{32,36},... | collective-permute-start | bytes 6291464 | tf_op jit(solution)/shard_map/ppermute | solution.py:10
  79.8 4.4 %copy-start.6 = (bf16[2,512,2048]{2,1,0:T(8,128)(2,1)}, bf16[2,512,2048]{2,1,0:T(8,128)(2,1)S(1)}, u32[]{:S(2)}) copy-start(bf16[2,512,2048]{2,1,0:T(8,128)(2,1)S(1)} %constant_dynamic-update-slice_fusion) | copy-start | bytes 12582916
  79.9 3.1 %copy-start.4 = (bf16[1,512,2048]{2,1,0:T(8,128)(2,1)S(1)}, bf16[1,512,2048]{2,1,0:T(8,128)(2,1)}, u32[]{:S(2)}) copy-start(bf16[1,512,2048]{2,1,0:T(8,128)(2,1)} %param.15) | copy-start | bytes 6291460
  85.9 1.3 copy-start.8
  85.9 2.6 %copy-start.10 = (bf16[512,512]{1,0:T(8,128)(2,1)}, bf16[512,512]{1,0:T(8,128)(2,1)S(1)}, u32[]{:S(2)}) copy-start(bf16[512,512]{1,0:T(8,128)(2,1)S(1)} %get-tuple-element.36) | copy-start | bytes 1572868
  88.6 2.0 copy-start.3
  90.6 3.2 %copy-start.2 = (f32[1,512,2048]{2,1,0:T(8,128)}, f32[1,512,2048]{2,1,0:T(8,128)S(1)}, u32[]{:S(2)}) copy-start(f32[1,512,2048]{2,1,0:T(8,128)S(1)} %add_bitcast_fusion) | copy-start | bytes 12582916
  93.8 7.5 %collective-permute-start.4 = (f32[2,256,2048]{2,1,0:T(8,128)}, f32[2,256,2048]{2,1,0:T(8,128)}, u32[]{:S(2)}, u32[]{:S(2)}) collective-permute-start(f32[2,256,2048]{2,1,0:T(8,128)} %pad_maximum_fusion), channel_id=1, source_target_pairs={{0,4},{4,0},{8,12},{12,8},{16,20},{20,16},{24,28},{28,24},{32,36},... | collective-permute-start | bytes 12582920 | tf_op jit(solution)/shard_map/ppermute | solution.py:10
  124.5 24.5 %collective-permute-start.7 = (f32[2,256,512]{2,1,0:T(8,128)S(1)}, f32[2,256,512]{2,1,0:T(8,128)S(1)}, u32[]{:S(2)}, u32[]{:S(2)}) collective-permute-start(f32[2,256,512]{2,1,0:T(8,128)S(1)} %bitcast.95), channel_id=1, source_target_pairs={{0,3},{1,0},{2,1},{3,2},{4,7},{5,4},{6,5},{7,6},{8,11},{9,8},{10,9... | collective-permute-start | bytes 3145736 | tf_op jit(solution)/shard_map/ppermute | solution.py:15
  125.5 25.7 %collective-permute-start.6 = (f32[2,256,512]{2,1,0:T(8,128)S(1)}, f32[2,256,512]{2,1,0:T(8,128)S(1)}, u32[]{:S(2)}, u32[]{:S(2)}) collective-permute-start(f32[2,256,512]{2,1,0:T(8,128)S(1)} %bitcast.96), channel_id=1, source_target_pairs={{0,2},{1,3},{2,0},{3,1},{4,6},{5,7},{6,4},{7,5},{8,10},{9,11},{10,... | collective-permute-start | bytes 3145736 | tf_op jit(solution)/shard_map/ppermute | solution.py:15
  126.0 56.7 %copy-start.9 = (bf16[512,512]{1,0:T(8,128)(2,1)S(1)}, bf16[512,512]{1,0:T(8,128)(2,1)}, u32[]{:S(2)}) copy-start(bf16[512,512]{1,0:T(8,128)(2,1)} %copy-done.8) | copy-start | bytes 1572868
  126.0 48.7 %collective-permute-start.5 = (f32[2,256,512]{2,1,0:T(8,128)S(1)}, f32[2,256,512]{2,1,0:T(8,128)S(1)}, u32[]{:S(2)}, u32[]{:S(2)}) collective-permute-start(f32[2,256,512]{2,1,0:T(8,128)S(1)} %bitcast.97), channel_id=1, source_target_pairs={{0,1},{1,2},{2,3},{3,0},{4,5},{5,6},{6,7},{7,4},{8,9},{9,10},{10,1... | collective-permute-start | bytes 3145736 | tf_op jit(solution)/shard_map/ppermute | solution.py:15
  176.5 23.4 %all-to-all-start.1 = ((bf16[2,64,4,512]{3,0,2,1:T(2,128)(2,1)}), bf16[2,64,4,512]{3,0,2,1:T(2,128)(2,1)S(1)}, u32[]{:S(2)}, u32[]{:S(2)}) async-start(bf16[2,64,4,512]{3,0,2,1:T(2,128)(2,1)} %bitcast.18), calls=%async_computation.1 | async-start | bytes 1048576 | tf_op jit(solution)/shard_map/all_to_all | solution.py:103
  182.7 4.4 %copy-start.7 = (bf16[2,512,2048]{2,1,0:T(8,128)(2,1)S(1)}, bf16[2,512,2048]{2,1,0:T(8,128)(2,1)}, u32[]{:S(2)}) copy-start(bf16[2,512,2048]{2,1,0:T(8,128)(2,1)} %copy-done.6) | copy-start | bytes 12582916
  187.0 2.6 %copy-start.11 = (bf16[512,512]{1,0:T(8,128)(2,1)S(1)}, bf16[512,512]{1,0:T(8,128)(2,1)}, u32[]{:S(2)}) copy-start(bf16[512,512]{1,0:T(8,128)(2,1)} %copy-done.10) | copy-start | bytes 1572868
  187.0 14.9 %copy-start.1 = (bf16[1,2048,512]{2,1,0:T(8,128)(2,1)S(1)}, bf16[1,2048,512]{2,1,0:T(8,128)(2,1)}, u32[]{:S(2)}) copy-start(bf16[1,2048,512]{2,1,0:T(8,128)(2,1)} %param.14) | copy-start | bytes 6291460

commit v2 on v1

--- a/solution.py
+++ b/solution.py
@@ -55,50 +55,88 @@
     ).astype(jnp.bfloat16)
     outbound = outbound.reshape(2, n_expert, half_cap, feat_slice)
     arrived = lax.all_to_all(outbound, "expert", split_axis=1, concat_axis=1, tiled=True)
-    pieces = [arrived] + [shifted(arrived, "tensor", k) for k in range(1, n_tensor)]
-    reversed_pieces = jnp.stack([pieces[(-m) % n_tensor] for m in range(n_tensor)])
-    ordered = jnp.roll(reversed_pieces, t_idx, axis=0)
-    own_rows = jnp.moveaxis(ordered, 0, 3).reshape(2, rows_out, n_tensor * feat_slice)
-    other_rows = partner(own_rows, "expert", 0)
-    routed_both = jnp.concatenate((own_rows, other_rows), axis=1)
-    routed = routed_both[0]
-    routed_grad = routed_both[1]
+    pieces = [arrived.reshape(2, rows_out, feat_slice)]
+    pieces += [shifted(pieces[0], "tensor", k) for k in range(1, n_tensor)]
+    blocks = [jnp.concatenate((p, partner(p, "expert", 0)), axis=1) for p in pieces]
+    src_off = [((t_idx - k) % n_tensor) * feat_slice for k in range(n_tensor)]
     w_gate = gate_weight[0]
     w_up = up_weight[0]
     w_down = down_weight[0]
     contract_rows = (((0,), (0,)), ((), ()))
     contract_cols = (((1,), (1,)), ((), ()))
-    gate_pre = jnp.dot(routed, w_gate, preferred_element_type=jnp.float32)
-    up_pre = jnp.dot(routed, w_up, preferred_element_type=jnp.float32)
+
+    def rows_of(w, off):
+        return lax.dynamic_slice_in_dim(w, off, feat_slice, axis=0)
+
+    def cols_of(w, off):
+        return lax.dynamic_slice_in_dim(w, off, feat_slice, axis=1)
+
+    def block_sum(terms):
+        total = terms[0]
+        for term in terms[1:]:
+            total = total + term
+        return total
+
+    gate_pre = block_sum(
+        [
+            jnp.dot(b[0], rows_of(w_gate, o), preferred_element_type=jnp.float32)
+            for b, o in zip(blocks, src_off)
+        ]
+    )
+    up_pre = block_sum(
+        [
+            jnp.dot(b[0], rows_of(w_up, o), preferred_element_type=jnp.float32)
+            for b, o in zip(blocks, src_off)
+        ]
+    )
+    grad_hidden = block_sum(
+        [
+            lax.dot_general(
+                b[1], cols_of(w_down, o), contract_cols, preferred_element_type=jnp.float32
+            )
+            for b, o in zip(blocks, src_off)
+        ]
+    )
     squash, activated = silu_parts(gate_pre)
     hidden = (activated * up_pre).astype(jnp.bfloat16)
-    out_part = jnp.dot(hidden, w_down, preferred_element_type=jnp.float32)
-    grad_hidden = lax.dot_general(
-        routed_grad, w_down, contract_cols, preferred_element_type=jnp.float32
-    )
     grad_gate_pre = (grad_hidden * up_pre * squash * (1.0 + gate_pre * (1.0 - squash))).astype(
         jnp.bfloat16
     )
     grad_up_pre = (grad_hidden * activated).astype(jnp.bfloat16)
-    gate_grad = lax.dot_general(
-        routed, grad_gate_pre, contract_rows, preferred_element_type=jnp.float32
-    ).astype(jnp.bfloat16)[None]
-    up_grad = lax.dot_general(
-        routed, grad_up_pre, contract_rows, preferred_element_type=jnp.float32
-    ).astype(jnp.bfloat16)[None]
-    down_grad = lax.dot_general(
-        hidden, routed_grad, contract_rows, preferred_element_type=jnp.float32
-    ).astype(jnp.bfloat16)[None]
-    input_part = lax.dot_general(
-        grad_gate_pre, w_gate, contract_cols, preferred_element_type=jnp.float32
-    ) + lax.dot_general(grad_up_pre, w_up, contract_cols, preferred_element_type=jnp.float32)
-    partial_value = jnp.stack((out_part, input_part))
-    core_sum = partial_value[:, :rows_out] + partner(partial_value[:, rows_out:], "expert", 0)
-    chunks = core_sum.reshape(2, rows_out, n_tensor, feat_slice)
-    acc = lax.dynamic_index_in_dim(chunks, t_idx, axis=2, keepdims=False)
-    for k in range(1, n_tensor):
-        sent = lax.dynamic_index_in_dim(chunks, (t_idx + k) % n_tensor, axis=2, keepdims=False)
-        acc = acc + shifted(sent, "tensor", k)
+    gate_grad = jnp.zeros(w_gate.shape, jnp.bfloat16)
+    up_grad = jnp.zeros(w_up.shape, jnp.bfloat16)
+    down_grad = jnp.zeros(w_down.shape, jnp.bfloat16)
+    for b, o in zip(blocks, src_off):
+        gate_piece = lax.dot_general(
+            b[0], grad_gate_pre, contract_rows, preferred_element_type=jnp.float32
+        ).astype(jnp.bfloat16)
+        up_piece = lax.dot_general(
+            b[0], grad_up_pre, contract_rows, preferred_element_type=jnp.float32
+        ).astype(jnp.bfloat16)
+        down_piece = lax.dot_general(
+            hidden, b[1], contract_rows, preferred_element_type=jnp.float32
+        ).astype(jnp.bfloat16)
+        gate_grad = lax.dynamic_update_slice_in_dim(gate_grad, gate_piece, o, axis=0)
+        up_grad = lax.dynamic_update_slice_in_dim(up_grad, up_piece, o, axis=0)
+        down_grad = lax.dynamic_update_slice_in_dim(down_grad, down_piece, o, axis=1)
+    gate_grad = gate_grad[None]
+    up_grad = up_grad[None]
+    down_grad = down_grad[None]
+    acc = None
+    for m in range(n_tensor):
+        off = ((t_idx + m) % n_tensor) * feat_slice
+        out_m = jnp.dot(hidden, cols_of(w_down, off), preferred_element_type=jnp.float32)
+        in_m = lax.dot_general(
+            grad_gate_pre, rows_of(w_gate, off), contract_cols, preferred_element_type=jnp.float32
+        ) + lax.dot_general(
+            grad_up_pre, rows_of(w_up, off), contract_cols, preferred_element_type=jnp.float32
+        )
+        part_m = jnp.stack((out_m, in_m))
+        core_m = part_m[:, :rows_out] + partner(part_m[:, rows_out:], "expert", 0)
+        if m == 0:
+            acc = core_m
+        else:
+            acc = acc + shifted(core_m.astype(jnp.bfloat16), "tensor", m).astype(jnp.float32)
     going_back = acc.astype(jnp.bfloat16).reshape(2, n_expert, half_cap, feat_slice)
     returned = lax.all_to_all(going_back, "expert", split_axis=1, concat_axis=1, tiled=True)
     flat_back = returned.reshape(2, rows_out, feat_slice)

time: 202 us -> 144 us (0.71)
  waiting for transfers between devices: 89.6 us -> 42.5 us
  local copies, waits for them, and re-layouts: 36.3 us -> 14 us
  starting transfers between devices: 12.3 us -> 20.7 us
  matrix products: 20.3 us -> 23.8 us
    ppermute x6, waiting for transfers between devices: 72.6 us -> 31.8 us  [shifted(): lax.ppermute(value, axis, [(i, (i + step) % size) for i in range(size)])]
    dynamic_slice x1 -> x0, local copies, waits for them, and re-layouts: 10.6 us -> none  [body(): acc = lax.dynamic_index_in_dim(chunks, t_idx, axis=2, keepdims=False)]
    ppermute x2 -> x8, waiting for transfers between devices: 9.26 us -> 0.02 us  [partner(): lax.ppermute(value, axis, [(i, i ^ 1 << stride) for i in range(lax.axis_s...]
    reshape x2 -> x1, local copies, waits for them, and re-layouts: 10.5 us -> 1.35 us  [body(): acc.astype(jnp.bfloat16).reshape(2, n_expert, half_cap, feat_slice)]
    concatenate x0 -> x1, other arithmetic: none -> 7.63 us  [body(): jnp.concatenate((p, partner(p, 'expert', 0)), axis=1)]
    add x1 -> x0, other arithmetic: 6.48 us -> none  [body(): partial_value[:, :rows_out]]
    unnamed x37 -> x31, local copies, waits for them, and re-layouts: 9.14 us -> 4.37 us
    slice x0 -> x3, local copies, waits for them, and re-layouts: none -> 4.51 us  [body(): b[1]]
  transfers between devices with their start and end apart: 9 -> 15, of which waited for: 8 -> 5; matrix products, arithmetic and copies ran while one was open for 6% -> 18% of each run, Pallas kernels for 0% -> 0%
where the time goes in v2:
time: 144 us
  waiting for transfers between devices  42.5 us (30%)
  blocking collectives  30.3 us (21%)
  matrix products  23.8 us (17%)
  starting transfers between devices  20.7 us (14%)
  local copies, waits for them, and re-layouts  14 us (10%)
  other arithmetic  11.5 us (8%)
    ppermute x6, waiting for transfers between devices, shifted(): lax.ppermute(value, axis, [(i, (i + step) % size) for i in range(size)])  31.8 us
    all_to_all x1, blocking collectives, body(): lax.all_to_all(outbound, 'expert', split_axis=1, concat_axis=1, tiled=True)  30.3 us
    all_to_all x1, waiting for transfers between devices, body(): lax.all_to_all(going_back, 'expert', split_axis=1, concat_axis=1, tiled=T...  10.7 us
    ppermute x6, starting transfers between devices, shifted(): lax.ppermute(value, axis, [(i, (i + step) % size) for i in range(size)])  8.6 us
    all_to_all x1, starting transfers between devices, body(): lax.all_to_all(going_back, 'expert', split_axis=1, concat_axis=1, tiled=T...  7.7 us
    concatenate x1, other arithmetic, body(): jnp.concatenate((p, partner(p, 'expert', 0)), axis=1)  7.63 us
    dot_general x4, matrix products, body(): lax.dot_general(b[0], grad_gate_pre, contract_rows, preferred_element_typ...  5.05 us
    slice x3, local copies, waits for them, and re-layouts, body(): b[1]  4.51 us
  transfers between devices with their start and end apart: 15, of which 5 were waited for; matrix products, arithmetic and copies ran while one was open for 18% of the time, Pallas kernels for 0%

profile of v2, /device:TPU:1, one launch (start us, length us, event | category | flops | bytes accessed | tf_op | source)
XLA Modules:
  0.0 144.0 jit_solution(16930033031463386924)
XLA Ops:
  4.0 1.2 fusion.4
  5.6 30.3 %all_to_all.10 = bf16[2,64,4,512]{3,2,0,1:T(4,128)(2,1)S(1)} all-to-all(bf16[2,64,4,512]{3,2,0,1:T(4,128)(2,1)S(1)} %copy.37), channel_id=1, replica_groups=mesh['expert'=64,'tensor'=4] {'expert'}, dimensions={1} | all-to-all | bytes 1048576 | tf_op jit(solution)/shard_map/all_to_all | solution.py:57
  36.7 1.2 collective-permute-start.1
  37.9 2.4 %collective-permute-start.3 = (bf16[2,256,512]{2,0,1:T(2,128)(2,1)S(1)}, bf16[2,256,512]{2,0,1:T(2,128)(2,1)S(1)}, u32[]{:S(2)}, u32[]{:S(2)}) collective-permute-start(bf16[2,256,512]{2,0,1:T(2,128)(2,1)S(1)} %bitcast.240), channel_id=1, source_target_pairs={{0,2},{1,3},{2,0},{3,1},{4,6},{5,7},{6,4},{7,5},{8,10},{9,11},{10,... | collective-permute-start | bytes 1572872 | tf_op jit(solution)/shard_map/ppermute | solution.py:15
  40.3 1.2 collective-permute-start.5
  41.5 7.6 %pad_maximum_fusion.4 = (bf16[1,512,512]{2,0,1:T(2,128)(2,1)S(1)}, bf16[1,512,512]{2,0,1:T(2,128)(2,1)S(1)}) fusion(bf16[2,256,512]{2,0,1:T(2,128)(2,1)S(1)} %collective-permute-done, bf16[2,256,512]{2,0,1:T(2,128)(2,1)S(1)} %bitcast.242), kind=kLoop, calls=%fused_computation.90 | loop fusion | flops 2097152 | bytes 2097152 | tf_op jit(solution)/shard_map/concatenate | solution.py:60
  51.2 1.1 collective-permute-start.2
  52.7 10.7 %collective-permute-done.3 = bf16[2,256,512]{2,0,1:T(2,128)(2,1)S(1)} collective-permute-done((bf16[2,256,512]{2,0,1:T(2,128)(2,1)S(1)}, bf16[2,256,512]{2,0,1:T(2,128)(2,1)S(1)}, u32[]{:S(2)}, u32[]{:S(2)}) %collective-permute-start.3) | collective-permute-done | bytes 524320 | tf_op jit(solution)/shard_map/ppermute | solution.py:15
  66.4 1.5 %fusion.172 = (bf16[1,512,512]{2,0,1:T(2,128)(2,1)S(1)}, bf16[1,512,512]{2,0,1:T(2,128)(2,1)S(1)}) fusion(bf16[2,512,512]{2,0,1:T(2,128)(2,1)S(1)} %constant_dynamic-update-slice_fusion), kind=kLoop, calls=%fused_computation.235 | loop fusion | bytes 2097152 | tf_op jit(solution)/shard_map/slice | solution.py:95
  68.3 1.5 %fusion.171 = (bf16[1,512,512]{2,0,1:T(2,128)(2,1)S(1)}, bf16[1,512,512]{2,0,1:T(2,128)(2,1)S(1)}) fusion(bf16[2,512,512]{2,0,1:T(2,128)(2,1)S(1)} %constant_dynamic-update-slice_fusion.2), kind=kLoop, calls=%fused_computation.234 | loop fusion | bytes 2097152 | tf_op jit(solution)/shard_map/slice | solution.py:95
  70.2 1.5 %fusion.170 = (bf16[1,512,512]{2,0,1:T(2,128)(2,1)S(1)}, bf16[1,512,512]{2,0,1:T(2,128)(2,1)S(1)}) fusion(bf16[2,512,512]{2,0,1:T(2,128)(2,1)S(1)} %constant_dynamic-update-slice_fusion.4), kind=kLoop, calls=%fused_computation.233 | loop fusion | bytes 2097152 | tf_op jit(solution)/shard_map/slice | solution.py:95
  88.5 2.2 %collective-permute-start.11 = (bf16[2,256,512]{2,1,0:T(8,128)(2,1)S(1)}, bf16[2,256,512]{2,1,0:T(8,128)(2,1)S(1)}, u32[]{:S(2)}, u32[]{:S(2)}) collective-permute-start(bf16[2,256,512]{2,1,0:T(8,128)(2,1)S(1)} %fusion.36), channel_id=1, source_target_pairs={{0,2},{1,3},{2,0},{3,1},{4,6},{5,7},{6,4},{7,5},{8,10},{9,11},{10,... | collective-permute-start | bytes 1572872 | tf_op jit(solution)/shard_map/ppermute | solution.py:15
  91.0 1.4 collective-permute-start.13
  93.3 9.0 %collective-permute-done.9 = bf16[2,256,512]{2,1,0:T(8,128)(2,1)S(1)} collective-permute-done((bf16[2,256,512]{2,1,0:T(8,128)(2,1)S(1)}, bf16[2,256,512]{2,1,0:T(8,128)(2,1)S(1)}, u32[]{:S(2)}, u32[]{:S(2)}) %collective-permute-start.9) | collective-permute-done | bytes 524320 | tf_op jit(solution)/shard_map/ppermute | solution.py:15
  102.3 11.4 %collective-permute-done.11 = bf16[2,256,512]{2,1,0:T(8,128)(2,1)S(1)} collective-permute-done((bf16[2,256,512]{2,1,0:T(8,128)(2,1)S(1)}, bf16[2,256,512]{2,1,0:T(8,128)(2,1)S(1)}, u32[]{:S(2)}, u32[]{:S(2)}) %collective-permute-start.11) | collective-permute-done | bytes 524320 | tf_op jit(solution)/shard_map/ppermute | solution.py:15
  114.7 1.3 copy.43
  116.0 7.7 %all-to-all-start.1 = ((bf16[2,64,4,512]{3,0,2,1:T(2,128)(2,1)}), bf16[2,64,4,512]{3,0,2,1:T(2,128)(2,1)}, u32[]{:S(2)}, u32[]{:S(2)}) async-start(bf16[2,64,4,512]{3,0,2,1:T(2,128)(2,1)} %bitcast.237), calls=%async_computation.1 | async-start | bytes 1048576 | tf_op jit(solution)/shard_map/all_to_all | solution.py:141
  123.8 1.5 %broadcast_in_dim.43.clone = bf16[1,2048,512]{2,1,0:T(8,128)(2,1)} broadcast(bf16[]{:T(256)} %constant.102.clone.1), dimensions={} | broadcast | bytes 2097154 | tf_op jit(solution)/shard_map/broadcast_in_dim | solution.py:122
  125.2 1.3 fusion.6
  126.5 1.3 fusion.8
  127.7 1.3 fusion.10
  129.0 1.3 fusion.12
  130.3 10.7 %all-to-all-done.1 = bf16[2,64,4,512]{3,0,2,1:T(2,128)(2,1)} async-done(((bf16[2,64,4,512]{3,0,2,1:T(2,128)(2,1)}), bf16[2,64,4,512]{3,0,2,1:T(2,128)(2,1)}, u32[]{:S(2)}, u32[]{:S(2)}) %all-to-all-start.1) | async-done | bytes 524320 | tf_op jit(solution)/shard_map/all_to_all | solution.py:141
  141.0 1.4 fusion.29
  (103 shorter events, 30.8 us)
Async XLA Ops:
  0.6 48.6 %copy-start = (bf16[1,2048,512]{2,1,0:T(8,128)(2,1)S(1)}, bf16[1,2048,512]{2,1,0:T(8,128)(2,1)}, u32[]{:S(2)}) copy-start(bf16[1,2048,512]{2,1,0:T(8,128)(2,1)} %param.14) | copy-start | bytes 6291460
  36.3 5.2 %collective-permute-start = (bf16[2,256,512]{2,0,1:T(2,128)(2,1)S(1)}, bf16[2,256,512]{2,0,1:T(2,128)(2,1)S(1)}, u32[]{:S(2)}, u32[]{:S(2)}) collective-permute-start(bf16[2,256,512]{2,0,1:T(2,128)(2,1)S(1)} %bitcast.238), channel_id=1, source_target_pairs={{0,4},{4,0},{8,12},{12,8},{16,20},{20,16},{24,28},{28,24},{32,36},... | collective-permute-start | bytes 1572872 | tf_op jit(solution)/shard_map/ppermute | solution.py:10
  36.7 14.5 %collective-permute-start.1 = (bf16[2,256,512]{2,0,1:T(2,128)(2,1)S(1)}, bf16[2,256,512]{2,0,1:T(2,128)(2,1)S(1)}, u32[]{:S(2)}, u32[]{:S(2)}) collective-permute-start(bf16[2,256,512]{2,0,1:T(2,128)(2,1)S(1)} %bitcast.239), channel_id=1, source_target_pairs={{0,1},{1,2},{2,3},{3,0},{4,5},{5,6},{6,7},{7,4},{8,9},{9,10},{10,1... | collective-permute-start | bytes 1572872 | tf_op jit(solution)/shard_map/ppermute | solution.py:15
  37.9 25.5 %collective-permute-start.3 = (bf16[2,256,512]{2,0,1:T(2,128)(2,1)S(1)}, bf16[2,256,512]{2,0,1:T(2,128)(2,1)S(1)}, u32[]{:S(2)}, u32[]{:S(2)}) collective-permute-start(bf16[2,256,512]{2,0,1:T(2,128)(2,1)S(1)} %bitcast.240), channel_id=1, source_target_pairs={{0,2},{1,3},{2,0},{3,1},{4,6},{5,7},{6,4},{7,5},{8,10},{9,11},{10,... | collective-permute-start | bytes 1572872 | tf_op jit(solution)/shard_map/ppermute | solution.py:15
  40.3 25.0 %collective-permute-start.5 = (bf16[2,256,512]{2,0,1:T(2,128)(2,1)S(1)}, bf16[2,256,512]{2,0,1:T(2,128)(2,1)S(1)}, u32[]{:S(2)}, u32[]{:S(2)}) collective-permute-start(bf16[2,256,512]{2,0,1:T(2,128)(2,1)S(1)} %bitcast.241), channel_id=1, source_target_pairs={{0,3},{1,0},{2,1},{3,2},{4,7},{5,4},{6,5},{7,6},{8,11},{9,8},{10,9... | collective-permute-start | bytes 1572872 | tf_op jit(solution)/shard_map/ppermute | solution.py:15
  50.7 14.1 %copy-start.2 = (bf16[1,512,2048]{2,1,0:T(8,128)(2,1)S(1)}, bf16[1,512,2048]{2,1,0:T(8,128)(2,1)}, u32[]{:S(2)}) copy-start(bf16[1,512,2048]{2,1,0:T(8,128)(2,1)} %param.15) | copy-start | bytes 6291460
  51.2 14.8 %collective-permute-start.2 = (bf16[2,256,512]{2,0,1:T(2,128)(2,1)S(1)}, bf16[2,256,512]{2,0,1:T(2,128)(2,1)S(1)}, u32[]{:S(2)}, u32[]{:S(2)}) collective-permute-start(bf16[2,256,512]{2,0,1:T(2,128)(2,1)S(1)} %collective-permute-done.1), channel_id=1, source_target_pairs={{0,4},{4,0},{8,12},{12,8},{16,20},{20,16},{24,28},{28,24},{32,36},... | collective-permute-start | bytes 1572872 | tf_op jit(solution)/shard_map/ppermute | solution.py:10
  63.4 4.5 %collective-permute-start.4 = (bf16[2,256,512]{2,0,1:T(2,128)(2,1)S(1)}, bf16[2,256,512]{2,0,1:T(2,128)(2,1)S(1)}, u32[]{:S(2)}, u32[]{:S(2)}) collective-permute-start(bf16[2,256,512]{2,0,1:T(2,128)(2,1)S(1)} %collective-permute-done.3), channel_id=1, source_target_pairs={{0,4},{4,0},{8,12},{12,8},{16,20},{20,16},{24,28},{28,24},{32,36},... | collective-permute-start | bytes 1572872 | tf_op jit(solution)/shard_map/ppermute | solution.py:10
  65.7 4.1 %collective-permute-start.6 = (bf16[2,256,512]{2,0,1:T(2,128)(2,1)S(1)}, bf16[2,256,512]{2,0,1:T(2,128)(2,1)S(1)}, u32[]{:S(2)}, u32[]{:S(2)}) collective-permute-start(bf16[2,256,512]{2,0,1:T(2,128)(2,1)S(1)} %collective-permute-done.5), channel_id=1, source_target_pairs={{0,4},{4,0},{8,12},{12,8},{16,20},{20,16},{24,28},{28,24},{32,36},... | collective-permute-start | bytes 1572872 | tf_op jit(solution)/shard_map/ppermute | solution.py:10
  71.9 15.2 %copy-start.5 = (bf16[1,512,512]{2,1,0:T(8,128)(2,1)}, bf16[1,512,512]{2,1,0:T(8,128)(2,1)S(1)}, u32[]{:S(2)}) copy-start(bf16[1,512,512]{2,1,0:T(8,128)(2,1)S(1)} %copy.45) | copy-start | bytes 1572868
  72.0 20.3 %copy-start.3 = (bf16[1,512,512]{2,1,0:T(8,128)(2,1)}, bf16[1,512,512]{2,1,0:T(8,128)(2,1)S(1)}, u32[]{:S(2)}) copy-start(bf16[1,512,512]{2,1,0:T(8,128)(2,1)S(1)} %copy.46) | copy-start | bytes 1572868
  73.9 18.9 %copy-start.9 = (bf16[1,512,512]{2,1,0:T(8,128)(2,1)}, bf16[1,512,512]{2,1,0:T(8,128)(2,1)S(1)}, u32[]{:S(2)}) copy-start(bf16[1,512,512]{2,1,0:T(8,128)(2,1)S(1)} %copy.47) | copy-start | bytes 1572868
  82.2 5.5 %collective-permute-start.8 = (f32[2,256,512]{2,1,0:T(8,128)S(1)}, f32[2,256,512]{2,1,0:T(8,128)S(1)}, u32[]{:S(2)}, u32[]{:S(2)}) collective-permute-start(f32[2,256,512]{2,1,0:T(8,128)S(1)} %pad_maximum_fusion.2), channel_id=1, source_target_pairs={{0,4},{4,0},{8,12},{12,8},{16,20},{20,16},{24,28},{28,24},{32,36},... | collective-permute-start | bytes 3145736 | tf_op jit(solution)/shard_map/ppermute | solution.py:10
  83.3 4.9 %collective-permute-start.10 = (f32[2,256,512]{2,1,0:T(8,128)S(1)}, f32[2,256,512]{2,1,0:T(8,128)S(1)}, u32[]{:S(2)}, u32[]{:S(2)}) collective-permute-start(f32[2,256,512]{2,1,0:T(8,128)S(1)} %pad_maximum_fusion.1), channel_id=1, source_target_pairs={{0,4},{4,0},{8,12},{12,8},{16,20},{20,16},{24,28},{28,24},{32,36},... | collective-permute-start | bytes 3145736 | tf_op jit(solution)/shard_map/ppermute | solution.py:10
  84.2 6.5 %collective-permute-start.12 = (f32[2,256,512]{2,1,0:T(8,128)S(1)}, f32[2,256,512]{2,1,0:T(8,128)S(1)}, u32[]{:S(2)}, u32[]{:S(2)}) collective-permute-start(f32[2,256,512]{2,1,0:T(8,128)S(1)} %pad_maximum_fusion), channel_id=1, source_target_pairs={{0,4},{4,0},{8,12},{12,8},{16,20},{20,16},{24,28},{28,24},{32,36},... | collective-permute-start | bytes 3145736 | tf_op jit(solution)/shard_map/ppermute | solution.py:10
  85.3 8.0 %collective-permute-start.7 = (f32[2,256,512]{2,1,0:T(8,128)S(1)}, f32[2,256,512]{2,1,0:T(8,128)S(1)}, u32[]{:S(2)}, u32[]{:S(2)}) collective-permute-start(f32[2,256,512]{2,1,0:T(8,128)S(1)} %pad_maximum_fusion.3), channel_id=1, source_target_pairs={{0,4},{4,0},{8,12},{12,8},{16,20},{20,16},{24,28},{28,24},{32,36},... | collective-permute-start | bytes 3145736 | tf_op jit(solution)/shard_map/ppermute | solution.py:10
  88.0 14.3 %collective-permute-start.9 = (bf16[2,256,512]{2,1,0:T(8,128)(2,1)S(1)}, bf16[2,256,512]{2,1,0:T(8,128)(2,1)S(1)}, u32[]{:S(2)}, u32[]{:S(2)}) collective-permute-start(bf16[2,256,512]{2,1,0:T(8,128)(2,1)S(1)} %fusion.39), channel_id=1, source_target_pairs={{0,1},{1,2},{2,3},{3,0},{4,5},{5,6},{6,7},{7,4},{8,9},{9,10},{10,1... | collective-permute-start | bytes 1572872 | tf_op jit(solution)/shard_map/ppermute | solution.py:15
  88.5 25.2 %collective-permute-start.11 = (bf16[2,256,512]{2,1,0:T(8,128)(2,1)S(1)}, bf16[2,256,512]{2,1,0:T(8,128)(2,1)S(1)}, u32[]{:S(2)}, u32[]{:S(2)}) collective-permute-start(bf16[2,256,512]{2,1,0:T(8,128)(2,1)S(1)} %fusion.36), channel_id=1, source_target_pairs={{0,2},{1,3},{2,0},{3,1},{4,6},{5,7},{6,4},{7,5},{8,10},{9,11},{10,... | collective-permute-start | bytes 1572872 | tf_op jit(solution)/shard_map/ppermute | solution.py:15
  91.0 23.3 %collective-permute-start.13 = (bf16[2,256,512]{2,1,0:T(8,128)(2,1)S(1)}, bf16[2,256,512]{2,1,0:T(8,128)(2,1)S(1)}, u32[]{:S(2)}, u32[]{:S(2)}) collective-permute-start(bf16[2,256,512]{2,1,0:T(8,128)(2,1)S(1)} %fusion.33), channel_id=1, source_target_pairs={{0,3},{1,0},{2,1},{3,2},{4,7},{5,4},{6,5},{7,6},{8,11},{9,8},{10,9... | collective-permute-start | bytes 1572872 | tf_op jit(solution)/shard_map/ppermute | solution.py:15
  93.3 21.4 %copy-start.8 = (bf16[1,2048,512]{2,1,0:T(8,128)(2,1)}, bf16[1,2048,512]{2,1,0:T(8,128)(2,1)S(1)}, u32[]{:S(2)}) copy-start(bf16[1,2048,512]{2,1,0:T(8,128)(2,1)S(1)} %fusion.20) | copy-start | bytes 6291460
  116.0 24.9 %all-to-all-start.1 = ((bf16[2,64,4,512]{3,0,2,1:T(2,128)(2,1)}), bf16[2,64,4,512]{3,0,2,1:T(2,128)(2,1)}, u32[]{:S(2)}, u32[]{:S(2)}) async-start(bf16[2,64,4,512]{3,0,2,1:T(2,128)(2,1)} %bitcast.237), calls=%async_computation.1 | async-start | bytes 1048576 | tf_op jit(solution)/shard_map/all_to_all | solution.py:141
  123.7 2.7 %copy-start.6 = (bf16[1,512,512]{2,1,0:T(8,128)(2,1)S(1)}, bf16[1,512,512]{2,1,0:T(8,128)(2,1)}, u32[]{:S(2)}) copy-start(bf16[1,512,512]{2,1,0:T(8,128)(2,1)} %copy-done.5) | copy-start | bytes 1572868
  125.2 2.5 %copy-start.4 = (bf16[1,512,512]{2,1,0:T(8,128)(2,1)S(1)}, bf16[1,512,512]{2,1,0:T(8,128)(2,1)}, u32[]{:S(2)}) copy-start(bf16[1,512,512]{2,1,0:T(8,128)(2,1)} %copy-done.3) | copy-start | bytes 1572868
  126.5 2.5 %copy-start.10 = (bf16[1,512,512]{2,1,0:T(8,128)(2,1)S(1)}, bf16[1,512,512]{2,1,0:T(8,128)(2,1)}, u32[]{:S(2)}) copy-start(bf16[1,512,512]{2,1,0:T(8,128)(2,1)} %copy-done.9) | copy-start | bytes 1572868
  (2 other events, 2.9 us)

commit v3 on v2

--- a/solution.py
+++ b/solution.py
@@ -57,7 +57,7 @@
     arrived = lax.all_to_all(outbound, "expert", split_axis=1, concat_axis=1, tiled=True)
     pieces = [arrived.reshape(2, rows_out, feat_slice)]
     pieces += [shifted(pieces[0], "tensor", k) for k in range(1, n_tensor)]
-    blocks = [jnp.concatenate((p, partner(p, "expert", 0)), axis=1) for p in pieces]
+    groups = [pieces, [partner(p, "expert", 0) for p in pieces]]
     src_off = [((t_idx - k) % n_tensor) * feat_slice for k in range(n_tensor)]
     w_gate = gate_weight[0]
     w_up = up_weight[0]
@@ -77,44 +77,81 @@
             total = total + term
         return total
 
-    gate_pre = block_sum(
-        [
-            jnp.dot(b[0], rows_of(w_gate, o), preferred_element_type=jnp.float32)
-            for b, o in zip(blocks, src_off)
-        ]
-    )
-    up_pre = block_sum(
-        [
-            jnp.dot(b[0], rows_of(w_up, o), preferred_element_type=jnp.float32)
-            for b, o in zip(blocks, src_off)
-        ]
-    )
-    grad_hidden = block_sum(
-        [
-            lax.dot_general(
-                b[1], cols_of(w_down, o), contract_cols, preferred_element_type=jnp.float32
-            )
-            for b, o in zip(blocks, src_off)
-        ]
-    )
-    squash, activated = silu_parts(gate_pre)
-    hidden = (activated * up_pre).astype(jnp.bfloat16)
-    grad_gate_pre = (grad_hidden * up_pre * squash * (1.0 + gate_pre * (1.0 - squash))).astype(
-        jnp.bfloat16
-    )
-    grad_up_pre = (grad_hidden * activated).astype(jnp.bfloat16)
+    acts = []
+    for blocks in groups:
+        gate_pre = block_sum(
+            [
+                jnp.dot(b[0], rows_of(w_gate, o), preferred_element_type=jnp.float32)
+                for b, o in zip(blocks, src_off)
+            ]
+        )
+        up_pre = block_sum(
+            [
+                jnp.dot(b[0], rows_of(w_up, o), preferred_element_type=jnp.float32)
+                for b, o in zip(blocks, src_off)
+            ]
+        )
+        grad_hidden = block_sum(
+            [
+                lax.dot_general(
+                    b[1], cols_of(w_down, o), contract_cols, preferred_element_type=jnp.float32
+                )
+                for b, o in zip(blocks, src_off)
+            ]
+        )
+        squash, activated = silu_parts(gate_pre)
+        hidden = (activated * up_pre).astype(jnp.bfloat16)
+        grad_gate_pre = (
+            grad_hidden * up_pre * squash * (1.0 + gate_pre * (1.0 - squash))
+        ).astype(jnp.bfloat16)
+        grad_up_pre = (grad_hidden * activated).astype(jnp.bfloat16)
+        acts.append((hidden, grad_gate_pre, grad_up_pre))
+
+    def partials(act, off):
+        hidden, grad_gate_pre, grad_up_pre = act
+        out_m = jnp.dot(hidden, cols_of(w_down, off), preferred_element_type=jnp.float32)
+        in_m = lax.dot_general(
+            grad_gate_pre, rows_of(w_gate, off), contract_cols, preferred_element_type=jnp.float32
+        ) + lax.dot_general(
+            grad_up_pre, rows_of(w_up, off), contract_cols, preferred_element_type=jnp.float32
+        )
+        return jnp.stack((out_m, in_m))
+
+    acc = None
+    for m in range(n_tensor):
+        off = ((t_idx + m) % n_tensor) * feat_slice
+        core_m = partials(acts[0], off) + partner(partials(acts[1], off), "expert", 0)
+        if m == 0:
+            acc = core_m
+        else:
+            acc = acc + shifted(core_m.astype(jnp.bfloat16), "tensor", m).astype(jnp.float32)
     gate_grad = jnp.zeros(w_gate.shape, jnp.bfloat16)
     up_grad = jnp.zeros(w_up.shape, jnp.bfloat16)
     down_grad = jnp.zeros(w_down.shape, jnp.bfloat16)
-    for b, o in zip(blocks, src_off):
-        gate_piece = lax.dot_general(
-            b[0], grad_gate_pre, contract_rows, preferred_element_type=jnp.float32
+    for k, o in enumerate(src_off):
+        gate_piece = block_sum(
+            [
+                lax.dot_general(
+                    g[k][0], a[1], contract_rows, preferred_element_type=jnp.float32
+                )
+                for g, a in zip(groups, acts)
+            ]
         ).astype(jnp.bfloat16)
-        up_piece = lax.dot_general(
-            b[0], grad_up_pre, contract_rows, preferred_element_type=jnp.float32
+        up_piece = block_sum(
+            [
+                lax.dot_general(
+                    g[k][0], a[2], contract_rows, preferred_element_type=jnp.float32
+                )
+                for g, a in zip(groups, acts)
+            ]
         ).astype(jnp.bfloat16)
-        down_piece = lax.dot_general(
-            hidden, b[1], contract_rows, preferred_element_type=jnp.float32
+        down_piece = block_sum(
+            [
+                lax.dot_general(
+                    a[0], g[k][1], contract_rows, preferred_element_type=jnp.float32
+                )
+                for g, a in zip(groups, acts)
+            ]
         ).astype(jnp.bfloat16)
         gate_grad = lax.dynamic_update_slice_in_dim(gate_grad, gate_piece, o, axis=0)
         up_grad = lax.dynamic_update_slice_in_dim(up_grad, up_piece, o, axis=0)
@@ -122,21 +159,6 @@
     gate_grad = gate_grad[None]
     up_grad = up_grad[None]
     down_grad = down_grad[None]
-    acc = None
-    for m in range(n_tensor):
-        off = ((t_idx + m) % n_tensor) * feat_slice
-        out_m = jnp.dot(hidden, cols_of(w_down, off), preferred_element_type=jnp.float32)
-        in_m = lax.dot_general(
-            grad_gate_pre, rows_of(w_gate, off), contract_cols, preferred_element_type=jnp.float32
-        ) + lax.dot_general(
-            grad_up_pre, rows_of(w_up, off), contract_cols, preferred_element_type=jnp.float32
-        )
-        part_m = jnp.stack((out_m, in_m))
-        core_m = part_m[:, :rows_out] + partner(part_m[:, rows_out:], "expert", 0)
-        if m == 0:
-            acc = core_m
-        else:
-            acc = acc + shifted(core_m.astype(jnp.bfloat16), "tensor", m).astype(jnp.float32)
     going_back = acc.astype(jnp.bfloat16).reshape(2, n_expert, half_cap, feat_slice)
     returned = lax.all_to_all(going_back, "expert", split_axis=1, concat_axis=1, tiled=True)
     flat_back = returned.reshape(2, rows_out, feat_slice)

time: 144 us -> 161 us (1.12)
  blocking collectives: 30.3 us -> 0 us
  starting transfers between devices: 20.7 us -> 38.5 us
  waiting for transfers between devices: 42.5 us -> 59.2 us
  matrix products: 23.8 us -> 37.4 us
  other arithmetic: 11.5 us -> 3.92 us
  local copies, waits for them, and re-layouts: 14 us -> 19.5 us
    all_to_all x1 -> x0, blocking collectives: 30.3 us -> none  [body(): lax.all_to_all(outbound, 'expert', split_axis=1, concat_axis=1, tiled=True)]
    all_to_all x0 -> x1, waiting for transfers between devices: none -> 17.2 us  [body(): lax.all_to_all(outbound, 'expert', split_axis=1, concat_axis=1, tiled=True)]
    all_to_all x0 -> x1, starting transfers between devices: none -> 13.2 us  [body(): lax.all_to_all(outbound, 'expert', split_axis=1, concat_axis=1, tiled=True)]
    dot_general x24 -> x48, matrix products: 14.3 us -> 22.8 us  [the longest x8 9.67 us: body(): lax.dot_general(g[k][0], a[1], contract_rows, preferred_element_type=jnp....]
    concatenate x1 -> x0, other arithmetic: 7.63 us -> none  [body(): jnp.concatenate((p, partner(p, 'expert', 0)), axis=1)]
    slice x3 -> x8, local copies, waits for them, and re-layouts: 4.51 us -> 10.1 us  [body(): b[1]]
    ppermute x8, starting transfers between devices: 4.41 us -> 9.39 us  [partner(): lax.ppermute(value, axis, [(i, i ^ 1 << stride) for i in range(lax.axis_s...]
    dot_general x4 -> x8, matrix products: 1.76 us -> 4.29 us  [body(): jnp.dot(b[0], rows_of(w_gate, o), preferred_element_type=jnp.float32)]
  transfers between devices with their start and end apart: 15 -> 16, of which waited for: 5 -> 6; matrix products, arithmetic and copies ran while one was open for 18% -> 18% of each run, Pallas kernels for 0% -> 0%
where the time goes in v3:
time: 161 us; the launch traced here: 160 us
  waiting for transfers between devices  59.2 us (37%)
  starting transfers between devices  38.5 us (24%)
  matrix products  37.4 us (23%)
  local copies, waits for them, and re-layouts  19.5 us (12%)
  other arithmetic  3.92 us (2%)
    ppermute x6, waiting for transfers between devices, shifted(): lax.ppermute(value, axis, [(i, (i + step) % size) for i in range(size)])  30.8 us
    all_to_all x1, waiting for transfers between devices, body(): lax.all_to_all(outbound, 'expert', split_axis=1, concat_axis=1, tiled=True)  17.2 us
    all_to_all x1, starting transfers between devices, body(): lax.all_to_all(outbound, 'expert', split_axis=1, concat_axis=1, tiled=True)  13.2 us
    all_to_all x1, waiting for transfers between devices, body(): lax.all_to_all(going_back, 'expert', split_axis=1, concat_axis=1, tiled=T...  11.2 us
    slice x8, local copies, waits for them, and re-layouts, body(): b[1]  10.1 us
    dot_general x8, matrix products, body(): lax.dot_general(g[k][0], a[1], contract_rows, preferred_element_type=jnp....  9.67 us
    ppermute x8, starting transfers between devices, partner(): lax.ppermute(value, axis, [(i, i ^ 1 << stride) for i in range(lax.axis_s...  9.39 us
    ppermute x6, starting transfers between devices, shifted(): lax.ppermute(value, axis, [(i, (i + step) % size) for i in range(size)])  9.02 us
  transfers between devices with their start and end apart: 16, of which 6 were waited for; matrix products, arithmetic and copies ran while one was open for 18% of the time, Pallas kernels for 0%

profile of v3, /device:TPU:1, one launch (start us, length us, event | category | flops | bytes accessed | tf_op | source)
XLA Modules:
  0.0 160.1 jit_solution(13589958200872128715)
XLA Ops:
  6.4 13.2 %all-to-all-start = ((bf16[2,64,4,512]{3,2,0,1:T(4,128)(2,1)}), bf16[2,64,4,512]{3,2,0,1:T(4,128)(2,1)S(1)}, u32[]{:S(2)}, u32[]{:S(2)}) async-start(bf16[2,64,4,512]{3,2,0,1:T(4,128)(2,1)} %copy.37), calls=%async_computation | async-start | bytes 1048576 | tf_op jit(solution)/shard_map/all_to_all | solution.py:57
  19.6 17.2 %all-to-all-done = bf16[2,64,4,512]{3,2,0,1:T(4,128)(2,1)S(1)} async-done(((bf16[2,64,4,512]{3,2,0,1:T(4,128)(2,1)}), bf16[2,64,4,512]{3,2,0,1:T(4,128)(2,1)S(1)}, u32[]{:S(2)}, u32[]{:S(2)}) %all-to-all-start) | async-done | bytes 524320 | tf_op jit(solution)/shard_map/all_to_all | solution.py:57
  39.3 1.5 collective-permute-start.2
  40.7 1.5 collective-permute-start.1
  44.4 2.1 %fusion.126 = f32[256,512]{1,0:T(8,128)} fusion(bf16[256,512]{1,0:T(8,128)(2,1)S(1)} %squeeze.39, bf16[1,2048,512]{2,1,0:T(8,128)(2,1)} %param.13, s32[]{:T(128)S(6)} %select_n.48), kind=kOutput, calls=%fused_computation.177 | convolution fusion | flops 134217728 | bytes 1310724 | tf_op jit(solution)/shard_map/dot_general | solution.py:84
  47.9 1.5 fusion.95
  49.4 3.1 %collective-permute-done.2 = bf16[2,256,512]{2,0,1:T(2,128)(2,1)} collective-permute-done((bf16[2,256,512]{2,0,1:T(2,128)(2,1)}, bf16[2,256,512]{2,0,1:T(2,128)(2,1)}, u32[]{:S(2)}, u32[]{:S(2)}) %collective-permute-start.2) | collective-permute-done | bytes 524320 | tf_op jit(solution)/shard_map/ppermute | solution.py:15
  52.5 2.1 %fusion.306 = (bf16[1,256,512]{2,0,1:T(2,128)(2,1)S(1)}, bf16[1,256,512]{2,0,1:T(2,128)(2,1)S(1)}) fusion(bf16[2,256,512]{2,0,1:T(2,128)(2,1)} %collective-permute-done.2), kind=kLoop, calls=%fused_computation.372 | loop fusion | bytes 1048576 | tf_op jit(solution)/shard_map/slice | solution.py:97
  55.7 2.1 %fusion.309 = (bf16[1,256,512]{2,0,1:T(2,128)(2,1)S(1)}, bf16[1,256,512]{2,0,1:T(2,128)(2,1)S(1)}) fusion(bf16[2,256,512]{2,0,1:T(2,128)(2,1)} %collective-permute-done.3), kind=kLoop, calls=%fused_computation.375 | loop fusion | bytes 1048576 | tf_op jit(solution)/shard_map/slice | solution.py:97
  58.8 6.2 %collective-permute-done.1 = bf16[2,256,512]{2,0,1:T(2,128)(2,1)} collective-permute-done((bf16[2,256,512]{2,0,1:T(2,128)(2,1)}, bf16[2,256,512]{2,0,1:T(2,128)(2,1)}, u32[]{:S(2)}, u32[]{:S(2)}) %collective-permute-start.1) | collective-permute-done | bytes 524320 | tf_op jit(solution)/shard_map/ppermute | solution.py:15
  65.0 2.1 %fusion.303 = (bf16[1,256,512]{2,0,1:T(2,128)(2,1)S(1)}, bf16[1,256,512]{2,0,1:T(2,128)(2,1)S(1)}) fusion(bf16[2,256,512]{2,0,1:T(2,128)(2,1)} %collective-permute-done.1), kind=kLoop, calls=%fused_computation.369 | loop fusion | bytes 1048576 | tf_op jit(solution)/shard_map/slice | solution.py:97
  72.3 1.3 fusion.311
  73.6 1.3 fusion.229
  79.3 6.1 %collective-permute-start.4 = (bf16[2,256,512]{2,0,1:T(2,128)(2,1)S(1)}, bf16[2,256,512]{2,0,1:T(2,128)(2,1)S(1)}, u32[]{:S(2)}, u32[]{:S(2)}) collective-permute-start(bf16[2,256,512]{2,0,1:T(2,128)(2,1)S(1)} %collective-permute-done), channel_id=1, source_target_pairs={{0,4},{4,0},{8,12},{12,8},{16,20},{20,16},{24,28},{28,24},{32,36},... | collective-permute-start | bytes 1572872 | tf_op jit(solution)/shard_map/ppermute | solution.py:10
  86.0 1.3 fusion.223
  87.3 1.3 fusion.217
  103.9 4.6 %collective-permute-start.11 = (bf16[2,256,512]{2,1,0:T(8,128)(2,1)S(1)}, bf16[2,256,512]{2,1,0:T(8,128)(2,1)S(1)}, u32[]{:S(2)}, u32[]{:S(2)}) collective-permute-start(bf16[2,256,512]{2,1,0:T(8,128)(2,1)S(1)} %fusion.58), channel_id=1, source_target_pairs={{0,2},{1,3},{2,0},{3,1},{4,6},{5,7},{6,4},{7,5},{8,10},{9,11},{10,... | collective-permute-start | bytes 1572872 | tf_op jit(solution)/shard_map/ppermute | solution.py:15
  109.6 9.5 %collective-permute-done.9 = bf16[2,256,512]{2,1,0:T(8,128)(2,1)S(1)} collective-permute-done((bf16[2,256,512]{2,1,0:T(8,128)(2,1)S(1)}, bf16[2,256,512]{2,1,0:T(8,128)(2,1)S(1)}, u32[]{:S(2)}, u32[]{:S(2)}) %collective-permute-start.9) | collective-permute-done | bytes 524320 | tf_op jit(solution)/shard_map/ppermute | solution.py:15
  119.1 12.1 %collective-permute-done.11 = bf16[2,256,512]{2,1,0:T(8,128)(2,1)S(1)} collective-permute-done((bf16[2,256,512]{2,1,0:T(8,128)(2,1)S(1)}, bf16[2,256,512]{2,1,0:T(8,128)(2,1)S(1)}, u32[]{:S(2)}, u32[]{:S(2)}) %collective-permute-start.11) | collective-permute-done | bytes 524320 | tf_op jit(solution)/shard_map/ppermute | solution.py:15
  131.6 1.4 copy.43
  132.9 6.9 %all-to-all-start.1 = ((bf16[2,64,4,512]{3,0,2,1:T(2,128)(2,1)}), bf16[2,64,4,512]{3,0,2,1:T(2,128)(2,1)}, u32[]{:S(2)}, u32[]{:S(2)}) async-start(bf16[2,64,4,512]{3,0,2,1:T(2,128)(2,1)} %bitcast.381), calls=%async_computation.1 | async-start | bytes 1048576 | tf_op jit(solution)/shard_map/all_to_all | solution.py:163
  139.9 1.5 broadcast_in_dim.43.clone
  146.0 11.2 %all-to-all-done.1 = bf16[2,64,4,512]{3,0,2,1:T(2,128)(2,1)} async-done(((bf16[2,64,4,512]{3,0,2,1:T(2,128)(2,1)}), bf16[2,64,4,512]{3,0,2,1:T(2,128)(2,1)}, u32[]{:S(2)}, u32[]{:S(2)}) %all-to-all-start.1) | async-done | bytes 524320 | tf_op jit(solution)/shard_map/all_to_all | solution.py:163
  157.1 1.4 fusion.51
  (141 shorter events, 46.2 us)
Async XLA Ops:
  0.6 46.9 %copy-start = (bf16[1,2048,512]{2,1,0:T(8,128)(2,1)S(1)}, bf16[1,2048,512]{2,1,0:T(8,128)(2,1)}, u32[]{:S(2)}) copy-start(bf16[1,2048,512]{2,1,0:T(8,128)(2,1)} %param.14) | copy-start | bytes 6291460
  6.4 30.5 %all-to-all-start = ((bf16[2,64,4,512]{3,2,0,1:T(4,128)(2,1)}), bf16[2,64,4,512]{3,2,0,1:T(4,128)(2,1)S(1)}, u32[]{:S(2)}, u32[]{:S(2)}) async-start(bf16[2,64,4,512]{3,2,0,1:T(4,128)(2,1)} %copy.37), calls=%async_computation | async-start | bytes 1048576 | tf_op jit(solution)/shard_map/all_to_all | solution.py:57
  38.0 16.9 %collective-permute-start = (bf16[2,256,512]{2,0,1:T(2,128)(2,1)}, bf16[2,256,512]{2,0,1:T(2,128)(2,1)S(1)}, u32[]{:S(2)}, u32[]{:S(2)}) collective-permute-start(bf16[2,256,512]{2,0,1:T(2,128)(2,1)} %bitcast.6), channel_id=1, source_target_pairs={{0,1},{1,2},{2,3},{3,0},{4,5},{5,6},{6,7},{7,4},{8,9},{9,10},{10,1... | collective-permute-start | bytes 1572872 | tf_op jit(solution)/shard_map/ppermute | solution.py:15
  39.3 13.2 %collective-permute-start.2 = (bf16[2,256,512]{2,0,1:T(2,128)(2,1)}, bf16[2,256,512]{2,0,1:T(2,128)(2,1)}, u32[]{:S(2)}, u32[]{:S(2)}) collective-permute-start(bf16[2,256,512]{2,0,1:T(2,128)(2,1)} %bitcast.6), channel_id=1, source_target_pairs={{0,3},{1,0},{2,1},{3,2},{4,7},{5,4},{6,5},{7,6},{8,11},{9,8},{10,9... | collective-permute-start | bytes 1572872 | tf_op jit(solution)/shard_map/ppermute | solution.py:15
  40.7 24.3 %collective-permute-start.1 = (bf16[2,256,512]{2,0,1:T(2,128)(2,1)}, bf16[2,256,512]{2,0,1:T(2,128)(2,1)}, u32[]{:S(2)}, u32[]{:S(2)}) collective-permute-start(bf16[2,256,512]{2,0,1:T(2,128)(2,1)} %bitcast.6), channel_id=1, source_target_pairs={{0,2},{1,3},{2,0},{3,1},{4,6},{5,7},{6,4},{7,5},{8,10},{9,11},{10,... | collective-permute-start | bytes 1572872 | tf_op jit(solution)/shard_map/ppermute | solution.py:15
  42.3 13.4 %collective-permute-start.3 = (bf16[2,256,512]{2,0,1:T(2,128)(2,1)}, bf16[2,256,512]{2,0,1:T(2,128)(2,1)}, u32[]{:S(2)}, u32[]{:S(2)}) collective-permute-start(bf16[2,256,512]{2,0,1:T(2,128)(2,1)} %bitcast.6), channel_id=1, source_target_pairs={{0,4},{4,0},{8,12},{12,8},{16,20},{20,16},{24,28},{28,24},{32,36},... | collective-permute-start | bytes 1572872 | tf_op jit(solution)/shard_map/ppermute | solution.py:10
  47.9 6.8 %copy-start.1 = (bf16[1,2048,512]{2,1,0:T(8,128)(2,1)S(1)}, bf16[1,2048,512]{2,1,0:T(8,128)(2,1)}, u32[]{:S(2)}) copy-start(bf16[1,2048,512]{2,1,0:T(8,128)(2,1)} %param.13) | copy-start | bytes 6291460
  58.5 8.6 %copy-start.2 = (bf16[1,512,2048]{2,1,0:T(8,128)(2,1)S(1)}, bf16[1,512,2048]{2,1,0:T(8,128)(2,1)}, u32[]{:S(2)}) copy-start(bf16[1,512,2048]{2,1,0:T(8,128)(2,1)} %param.15) | copy-start | bytes 6291460
  58.8 8.7 %copy-start.9 = (f32[256,512]{1,0:T(8,128)S(1)}, f32[256,512]{1,0:T(8,128)}, u32[]{:S(2)}) copy-start(f32[256,512]{1,0:T(8,128)} %fusion.126) | copy-start | bytes 1572868
  79.3 10.0 %collective-permute-start.4 = (bf16[2,256,512]{2,0,1:T(2,128)(2,1)S(1)}, bf16[2,256,512]{2,0,1:T(2,128)(2,1)S(1)}, u32[]{:S(2)}, u32[]{:S(2)}) collective-permute-start(bf16[2,256,512]{2,0,1:T(2,128)(2,1)S(1)} %collective-permute-done), channel_id=1, source_target_pairs={{0,4},{4,0},{8,12},{12,8},{16,20},{20,16},{24,28},{28,24},{32,36},... | collective-permute-start | bytes 1572872 | tf_op jit(solution)/shard_map/ppermute | solution.py:10
  85.4 3.1 %collective-permute-start.6 = (bf16[2,256,512]{2,0,1:T(2,128)(2,1)}, bf16[2,256,512]{2,0,1:T(2,128)(2,1)S(1)}, u32[]{:S(2)}, u32[]{:S(2)}) collective-permute-start(bf16[2,256,512]{2,0,1:T(2,128)(2,1)} %collective-permute-done.2), channel_id=1, source_target_pairs={{0,4},{4,0},{8,12},{12,8},{16,20},{20,16},{24,28},{28,24},{32,36},... | collective-permute-start | bytes 1572872 | tf_op jit(solution)/shard_map/ppermute | solution.py:10
  85.8 5.3 %collective-permute-start.5 = (bf16[2,256,512]{2,0,1:T(2,128)(2,1)}, bf16[2,256,512]{2,0,1:T(2,128)(2,1)S(1)}, u32[]{:S(2)}, u32[]{:S(2)}) collective-permute-start(bf16[2,256,512]{2,0,1:T(2,128)(2,1)} %collective-permute-done.1), channel_id=1, source_target_pairs={{0,4},{4,0},{8,12},{12,8},{16,20},{20,16},{24,28},{28,24},{32,36},... | collective-permute-start | bytes 1572872 | tf_op jit(solution)/shard_map/ppermute | solution.py:10
  97.2 6.1 %collective-permute-start.8 = (f32[2,256,512]{2,1,0:T(8,128)S(1)}, f32[2,256,512]{2,1,0:T(8,128)S(1)}, u32[]{:S(2)}, u32[]{:S(2)}) collective-permute-start(f32[2,256,512]{2,1,0:T(8,128)S(1)} %pad_maximum_fusion.1), channel_id=1, source_target_pairs={{0,4},{4,0},{8,12},{12,8},{16,20},{20,16},{24,28},{28,24},{32,36},... | collective-permute-start | bytes 3145736 | tf_op jit(solution)/shard_map/ppermute | solution.py:10
  98.0 5.7 %collective-permute-start.10 = (f32[2,256,512]{2,1,0:T(8,128)S(1)}, f32[2,256,512]{2,1,0:T(8,128)S(1)}, u32[]{:S(2)}, u32[]{:S(2)}) collective-permute-start(f32[2,256,512]{2,1,0:T(8,128)S(1)} %pad_maximum_fusion.2), channel_id=1, source_target_pairs={{0,4},{4,0},{8,12},{12,8},{16,20},{20,16},{24,28},{28,24},{32,36},... | collective-permute-start | bytes 3145736 | tf_op jit(solution)/shard_map/ppermute | solution.py:10
  98.7 9.9 %collective-permute-start.12 = (f32[2,256,512]{2,1,0:T(8,128)S(1)}, f32[2,256,512]{2,1,0:T(8,128)S(1)}, u32[]{:S(2)}, u32[]{:S(2)}) collective-permute-start(f32[2,256,512]{2,1,0:T(8,128)S(1)} %pad_maximum_fusion.3), channel_id=1, source_target_pairs={{0,4},{4,0},{8,12},{12,8},{16,20},{20,16},{24,28},{28,24},{32,36},... | collective-permute-start | bytes 3145736 | tf_op jit(solution)/shard_map/ppermute | solution.py:10
  99.5 10.1 %collective-permute-start.7 = (f32[2,256,512]{2,1,0:T(8,128)S(1)}, f32[2,256,512]{2,1,0:T(8,128)S(1)}, u32[]{:S(2)}, u32[]{:S(2)}) collective-permute-start(f32[2,256,512]{2,1,0:T(8,128)S(1)} %pad_maximum_fusion), channel_id=1, source_target_pairs={{0,4},{4,0},{8,12},{12,8},{16,20},{20,16},{24,28},{28,24},{32,36},... | collective-permute-start | bytes 3145736 | tf_op jit(solution)/shard_map/ppermute | solution.py:10
  103.6 15.5 %collective-permute-start.9 = (bf16[2,256,512]{2,1,0:T(8,128)(2,1)S(1)}, bf16[2,256,512]{2,1,0:T(8,128)(2,1)S(1)}, u32[]{:S(2)}, u32[]{:S(2)}) collective-permute-start(bf16[2,256,512]{2,1,0:T(8,128)(2,1)S(1)} %fusion.57), channel_id=1, source_target_pairs={{0,1},{1,2},{2,3},{3,0},{4,5},{5,6},{6,7},{7,4},{8,9},{9,10},{10,1... | collective-permute-start | bytes 1572872 | tf_op jit(solution)/shard_map/ppermute | solution.py:15
  103.9 27.3 %collective-permute-start.11 = (bf16[2,256,512]{2,1,0:T(8,128)(2,1)S(1)}, bf16[2,256,512]{2,1,0:T(8,128)(2,1)S(1)}, u32[]{:S(2)}, u32[]{:S(2)}) collective-permute-start(bf16[2,256,512]{2,1,0:T(8,128)(2,1)S(1)} %fusion.58), channel_id=1, source_target_pairs={{0,2},{1,3},{2,0},{3,1},{4,6},{5,7},{6,4},{7,5},{8,10},{9,11},{10,... | collective-permute-start | bytes 1572872 | tf_op jit(solution)/shard_map/ppermute | solution.py:15
  108.8 22.3 %collective-permute-start.13 = (bf16[2,256,512]{2,1,0:T(8,128)(2,1)S(1)}, bf16[2,256,512]{2,1,0:T(8,128)(2,1)S(1)}, u32[]{:S(2)}, u32[]{:S(2)}) collective-permute-start(bf16[2,256,512]{2,1,0:T(8,128)(2,1)S(1)} %fusion.59), channel_id=1, source_target_pairs={{0,3},{1,0},{2,1},{3,2},{4,7},{5,4},{6,5},{7,6},{8,11},{9,8},{10,9... | collective-permute-start | bytes 1572872 | tf_op jit(solution)/shard_map/ppermute | solution.py:15
  109.6 22.0 %copy-start.8 = (bf16[1,2048,512]{2,1,0:T(8,128)(2,1)}, bf16[1,2048,512]{2,1,0:T(8,128)(2,1)S(1)}, u32[]{:S(2)}) copy-start(bf16[1,2048,512]{2,1,0:T(8,128)(2,1)S(1)} %fusion.22) | copy-start | bytes 6291460
  132.9 24.2 %all-to-all-start.1 = ((bf16[2,64,4,512]{3,0,2,1:T(2,128)(2,1)}), bf16[2,64,4,512]{3,0,2,1:T(2,128)(2,1)}, u32[]{:S(2)}, u32[]{:S(2)}) async-start(bf16[2,64,4,512]{3,0,2,1:T(2,128)(2,1)} %bitcast.381), calls=%async_computation.1 | async-start | bytes 1048576 | tf_op jit(solution)/shard_map/all_to_all | solution.py:163
  139.9 2.7 %copy-start.3 = (f32[512,512]{1,0:T(8,128)S(1)}, f32[512,512]{1,0:T(8,128)}, u32[]{:S(2)}) copy-start(f32[512,512]{1,0:T(8,128)} %fusion.229) | copy-start | bytes 3145732
  141.5 2.2 %copy-start.6 = (f32[512,512]{1,0:T(8,128)S(1)}, f32[512,512]{1,0:T(8,128)}, u32[]{:S(2)}) copy-start(f32[512,512]{1,0:T(8,128)} %fusion.223) | copy-start | bytes 3145732
  142.6 2.2 %copy-start.5 = (f32[512,512]{1,0:T(8,128)S(1)}, f32[512,512]{1,0:T(8,128)}, u32[]{:S(2)}) copy-start(f32[512,512]{1,0:T(8,128)} %fusion.217) | copy-start | bytes 3145732
  (2 other events, 2.9 us)

commit v4 on v2

--- a/solution.py
+++ b/solution.py
@@ -57,7 +57,10 @@
     arrived = lax.all_to_all(outbound, "expert", split_axis=1, concat_axis=1, tiled=True)
     pieces = [arrived.reshape(2, rows_out, feat_slice)]
     pieces += [shifted(pieces[0], "tensor", k) for k in range(1, n_tensor)]
-    blocks = [jnp.concatenate((p, partner(p, "expert", 0)), axis=1) for p in pieces]
+    blocks = []
+    for p in pieces:
+        q = partner(p, "expert", 0)
+        blocks.append([jnp.concatenate((p[i], q[i]), axis=0) for i in range(2)])
     src_off = [((t_idx - k) % n_tensor) * feat_slice for k in range(n_tensor)]
     w_gate = gate_weight[0]
     w_up = up_weight[0]

time: 144 us -> 146 us (1.014)
  other arithmetic: 11.5 us -> 3.97 us
  local copies, waits for them, and re-layouts: 14 us -> 20.4 us
  waiting for transfers between devices: 42.5 us -> 45.5 us
  starting transfers between devices: 20.7 us -> 18.8 us
  matrix products: 23.8 us -> 25.6 us
    concatenate x1 -> x0, other arithmetic: 7.63 us -> none  [body(): jnp.concatenate((p, partner(p, 'expert', 0)), axis=1)]
    slice x3 -> x8, local copies, waits for them, and re-layouts: 4.51 us -> 10.2 us  [body(): blocks.append([jnp.concatenate((p[i], q[i]), axis=0) for i in range(2)])]
    ppermute x6, waiting for transfers between devices: 31.8 us -> 37.1 us  [shifted(): lax.ppermute(value, axis, [(i, (i + step) % size) for i in range(size)])]
    all_to_all x1, waiting for transfers between devices: 10.7 us -> 8.37 us  [body(): lax.all_to_all(going_back, 'expert', split_axis=1, concat_axis=1, tiled=T...]
    dot_general x4, matrix products: 1.87 us -> 3.75 us  [body(): lax.dot_general(b[0], grad_up_pre, contract_rows, preferred_element_type=...]
    ppermute x6, starting transfers between devices: 8.6 us -> 7.08 us  [shifted(): lax.ppermute(value, axis, [(i, (i + step) % size) for i in range(size)])]
    unnamed x31 -> x51, local copies, waits for them, and re-layouts: 4.37 us -> 4.43 us
  transfers between devices with their start and end apart: 15 -> 15, of which waited for: 5 -> 5; matrix products, arithmetic and copies ran while one was open for 18% -> 20% of each run, Pallas kernels for 0% -> 0%
where the time goes in v4:
time: 146 us
  waiting for transfers between devices  45.5 us (31%)
  blocking collectives  30.3 us (21%)
  matrix products  25.6 us (18%)
  local copies, waits for them, and re-layouts  20.4 us (14%)
  starting transfers between devices  18.8 us (13%)
  other arithmetic  3.97 us (3%)
    ppermute x6, waiting for transfers between devices, shifted(): lax.ppermute(value, axis, [(i, (i + step) % size) for i in range(size)])  37.1 us
    all_to_all x1, blocking collectives, body(): lax.all_to_all(outbound, 'expert', split_axis=1, concat_axis=1, tiled=True)  30.3 us
    slice x8, local copies, waits for them, and re-layouts, body(): blocks.append([jnp.concatenate((p[i], q[i]), axis=0) for i in range(2)])  10.2 us
    all_to_all x1, waiting for transfers between devices, body(): lax.all_to_all(going_back, 'expert', split_axis=1, concat_axis=1, tiled=T...  8.37 us
    all_to_all x1, starting transfers between devices, body(): lax.all_to_all(going_back, 'expert', split_axis=1, concat_axis=1, tiled=T...  7.49 us
    ppermute x6, starting transfers between devices, shifted(): lax.ppermute(value, axis, [(i, (i + step) % size) for i in range(size)])  7.08 us
    dot_general x4, matrix products, body(): lax.dot_general(b[0], grad_gate_pre, contract_rows, preferred_element_typ...  5.03 us
    unnamed x51, local copies, waits for them, and re-layouts  4.43 us
  transfers between devices with their start and end apart: 15, of which 5 were waited for; matrix products, arithmetic and copies ran while one was open for 20% of the time, Pallas kernels for 0%

profile of v4, /device:TPU:1, one launch (start us, length us, event | category | flops | bytes accessed | tf_op | source)
XLA Modules:
  0.0 145.9 jit_solution(6199737927758783681)
XLA Ops:
  4.0 1.2 fusion.4
  5.6 30.3 %all_to_all.10 = bf16[2,64,4,512]{3,2,0,1:T(4,128)(2,1)S(1)} all-to-all(bf16[2,64,4,512]{3,2,0,1:T(4,128)(2,1)S(1)} %copy.58), channel_id=1, replica_groups=mesh['expert'=64,'tensor'=4] {'expert'}, dimensions={1} | all-to-all | bytes 1048576 | tf_op jit(solution)/shard_map/all_to_all | solution.py:57
  35.8 1.2 copy.59
  37.4 1.2 collective-permute-start.1
  38.6 2.4 %collective-permute-start.3 = (bf16[2,256,512]{2,0,1:T(2,128)(2,1)}, bf16[2,256,512]{2,0,1:T(2,128)(2,1)}, u32[]{:S(2)}, u32[]{:S(2)}) collective-permute-start(bf16[2,256,512]{2,0,1:T(2,128)(2,1)} %bitcast.5), channel_id=1, source_target_pairs={{0,2},{1,3},{2,0},{3,1},{4,6},{5,7},{6,4},{7,5},{8,10},{9,11},{10,... | collective-permute-start | bytes 1572872 | tf_op jit(solution)/shard_map/ppermute | solution.py:15
  41.0 1.2 collective-permute-start.5
  45.5 6.7 %collective-permute-done.1 = bf16[2,256,512]{2,0,1:T(2,128)(2,1)} collective-permute-done((bf16[2,256,512]{2,0,1:T(2,128)(2,1)}, bf16[2,256,512]{2,0,1:T(2,128)(2,1)}, u32[]{:S(2)}, u32[]{:S(2)}) %collective-permute-start.1) | collective-permute-done | bytes 524320 | tf_op jit(solution)/shard_map/ppermute | solution.py:15
  53.2 2.1 %fusion.150 = (bf16[1,256,512]{2,0,1:T(2,128)(2,1)S(1)}, bf16[1,256,512]{2,0,1:T(2,128)(2,1)S(1)}) fusion(bf16[2,256,512]{2,0,1:T(2,128)(2,1)} %collective-permute-done.1), kind=kLoop, calls=%fused_computation.227 | loop fusion | bytes 1048576 | tf_op jit(solution)/shard_map/slice | solution.py:63
  55.5 9.0 %collective-permute-done.3 = bf16[2,256,512]{2,0,1:T(2,128)(2,1)} collective-permute-done((bf16[2,256,512]{2,0,1:T(2,128)(2,1)}, bf16[2,256,512]{2,0,1:T(2,128)(2,1)}, u32[]{:S(2)}, u32[]{:S(2)}) %collective-permute-start.3) | collective-permute-done | bytes 524320 | tf_op jit(solution)/shard_map/ppermute | solution.py:15
  64.5 2.1 %fusion.148 = (bf16[1,256,512]{2,0,1:T(2,128)(2,1)S(1)}, bf16[1,256,512]{2,0,1:T(2,128)(2,1)S(1)}) fusion(bf16[2,256,512]{2,0,1:T(2,128)(2,1)} %collective-permute-done.3), kind=kLoop, calls=%fused_computation.225 | loop fusion | bytes 1048576 | tf_op jit(solution)/shard_map/slice | solution.py:63
  68.8 1.1 collective-permute-start.4
  70.1 2.2 %fusion.146 = (bf16[1,256,512]{2,0,1:T(2,128)(2,1)S(1)}, bf16[1,256,512]{2,0,1:T(2,128)(2,1)S(1)}) fusion(bf16[2,256,512]{2,0,1:T(2,128)(2,1)} %collective-permute-done.5), kind=kLoop, calls=%fused_computation.223 | loop fusion | bytes 1048576 | tf_op jit(solution)/shard_map/slice | solution.py:63
  91.8 1.6 %collective-permute-start.13 = (bf16[2,256,512]{2,1,0:T(8,128)(2,1)S(1)}, bf16[2,256,512]{2,1,0:T(8,128)(2,1)S(1)}, u32[]{:S(2)}, u32[]{:S(2)}) collective-permute-start(bf16[2,256,512]{2,1,0:T(8,128)(2,1)S(1)} %fusion.33), channel_id=1, source_target_pairs={{0,3},{1,0},{2,1},{3,2},{4,7},{5,4},{6,5},{7,6},{8,11},{9,8},{10,9... | collective-permute-start | bytes 1572872 | tf_op jit(solution)/shard_map/ppermute | solution.py:15
  95.1 20.7 %collective-permute-done.9 = bf16[2,256,512]{2,1,0:T(8,128)(2,1)S(1)} collective-permute-done((bf16[2,256,512]{2,1,0:T(8,128)(2,1)S(1)}, bf16[2,256,512]{2,1,0:T(8,128)(2,1)S(1)}, u32[]{:S(2)}, u32[]{:S(2)}) %collective-permute-start.9) | collective-permute-done | bytes 524320 | tf_op jit(solution)/shard_map/ppermute | solution.py:15
  116.9 1.4 copy.64
  118.2 7.5 %all-to-all-start.1 = ((bf16[2,64,4,512]{3,0,2,1:T(2,128)(2,1)}), bf16[2,64,4,512]{3,0,2,1:T(2,128)(2,1)}, u32[]{:S(2)}, u32[]{:S(2)}) async-start(bf16[2,64,4,512]{3,0,2,1:T(2,128)(2,1)} %bitcast.211), calls=%async_computation.1 | async-start | bytes 1048576 | tf_op jit(solution)/shard_map/all_to_all | solution.py:144
  125.7 2.3 %fusion.20 = bf16[1,2048,512]{2,1,0:T(8,128)(2,1)} fusion(bf16[1,2048,512]{2,1,0:T(8,128)(2,1)} %copy-done.14, s32[]{:T(128)S(6)} %select_n.90, bf16[512,512]{1,0:T(8,128)(2,1)S(1)} %get-tuple-element.47, bf16[256,512]{1,0:T(8,128)(2,1)} %copy-done.19, bf16[256,512]{1,0:T(8,128)(2,1)} %copy-done.17), kind=kOutput, calls=%fused_computation.58 | convolution fusion | flops 269746176 | bytes 1572868 | tf_op jit(solution)/shard_map/dot_general | solution.py:116
  128.1 1.5 broadcast_in_dim.43.clone
  129.5 1.3 fusion.6
  130.8 1.3 fusion.8
  132.1 1.3 fusion.10
  133.3 1.3 fusion.12
  134.6 8.4 %all-to-all-done.1 = bf16[2,64,4,512]{3,0,2,1:T(2,128)(2,1)} async-done(((bf16[2,64,4,512]{3,0,2,1:T(2,128)(2,1)}), bf16[2,64,4,512]{3,0,2,1:T(2,128)(2,1)}, u32[]{:S(2)}, u32[]{:S(2)}) %all-to-all-start.1) | async-done | bytes 524320 | tf_op jit(solution)/shard_map/all_to_all | solution.py:144
  143.0 1.4 fusion.29
  (126 shorter events, 34.2 us)
Async XLA Ops:
  0.6 44.4 %copy-start = (bf16[1,2048,512]{2,1,0:T(8,128)(2,1)S(1)}, bf16[1,2048,512]{2,1,0:T(8,128)(2,1)}, u32[]{:S(2)}) copy-start(bf16[1,2048,512]{2,1,0:T(8,128)(2,1)} %param.14) | copy-start | bytes 6291460
  37.1 7.1 %collective-permute-start = (bf16[2,256,512]{2,0,1:T(2,128)(2,1)}, bf16[2,256,512]{2,0,1:T(2,128)(2,1)S(1)}, u32[]{:S(2)}, u32[]{:S(2)}) collective-permute-start(bf16[2,256,512]{2,0,1:T(2,128)(2,1)} %bitcast.5), channel_id=1, source_target_pairs={{0,4},{4,0},{8,12},{12,8},{16,20},{20,16},{24,28},{28,24},{32,36},... | collective-permute-start | bytes 1572872 | tf_op jit(solution)/shard_map/ppermute | solution.py:10
  37.4 14.9 %collective-permute-start.1 = (bf16[2,256,512]{2,0,1:T(2,128)(2,1)}, bf16[2,256,512]{2,0,1:T(2,128)(2,1)}, u32[]{:S(2)}, u32[]{:S(2)}) collective-permute-start(bf16[2,256,512]{2,0,1:T(2,128)(2,1)} %bitcast.5), channel_id=1, source_target_pairs={{0,1},{1,2},{2,3},{3,0},{4,5},{5,6},{6,7},{7,4},{8,9},{9,10},{10,1... | collective-permute-start | bytes 1572872 | tf_op jit(solution)/shard_map/ppermute | solution.py:15
  38.6 25.9 %collective-permute-start.3 = (bf16[2,256,512]{2,0,1:T(2,128)(2,1)}, bf16[2,256,512]{2,0,1:T(2,128)(2,1)}, u32[]{:S(2)}, u32[]{:S(2)}) collective-permute-start(bf16[2,256,512]{2,0,1:T(2,128)(2,1)} %bitcast.5), channel_id=1, source_target_pairs={{0,2},{1,3},{2,0},{3,1},{4,6},{5,7},{6,4},{7,5},{8,10},{9,11},{10,... | collective-permute-start | bytes 1572872 | tf_op jit(solution)/shard_map/ppermute | solution.py:15
  41.0 28.8 %collective-permute-start.5 = (bf16[2,256,512]{2,0,1:T(2,128)(2,1)}, bf16[2,256,512]{2,0,1:T(2,128)(2,1)}, u32[]{:S(2)}, u32[]{:S(2)}) collective-permute-start(bf16[2,256,512]{2,0,1:T(2,128)(2,1)} %bitcast.5), channel_id=1, source_target_pairs={{0,3},{1,0},{2,1},{3,2},{4,7},{5,4},{6,5},{7,6},{8,11},{9,8},{10,9... | collective-permute-start | bytes 1572872 | tf_op jit(solution)/shard_map/ppermute | solution.py:15
  44.2 23.1 %copy-start.15 = (bf16[256,512]{1,0:T(8,128)(2,1)}, bf16[256,512]{1,0:T(8,128)(2,1)S(1)}, u32[]{:S(2)}) copy-start(bf16[256,512]{1,0:T(8,128)(2,1)S(1)} %squeeze.69) | copy-start | bytes 786436
  45.1 48.5 %copy-start.3 = (bf16[256,512]{1,0:T(8,128)(2,1)}, bf16[256,512]{1,0:T(8,128)(2,1)S(1)}, u32[]{:S(2)}) copy-start(bf16[256,512]{1,0:T(8,128)(2,1)S(1)} %get-tuple-element.67) | copy-start | bytes 786436
  52.3 20.2 %collective-permute-start.2 = (bf16[2,256,512]{2,0,1:T(2,128)(2,1)}, bf16[2,256,512]{2,0,1:T(2,128)(2,1)S(1)}, u32[]{:S(2)}, u32[]{:S(2)}) collective-permute-start(bf16[2,256,512]{2,0,1:T(2,128)(2,1)} %collective-permute-done.1), channel_id=1, source_target_pairs={{0,4},{4,0},{8,12},{12,8},{16,20},{20,16},{24,28},{28,24},{32,36},... | collective-permute-start | bytes 1572872 | tf_op jit(solution)/shard_map/ppermute | solution.py:10
  55.3 11.3 %copy-start.1 = (bf16[1,2048,512]{2,1,0:T(8,128)(2,1)S(1)}, bf16[1,2048,512]{2,1,0:T(8,128)(2,1)}, u32[]{:S(2)}) copy-start(bf16[1,2048,512]{2,1,0:T(8,128)(2,1)} %param.13) | copy-start | bytes 6291460
  55.5 38.6 %copy-start.5 = (bf16[256,512]{1,0:T(8,128)(2,1)}, bf16[256,512]{1,0:T(8,128)(2,1)S(1)}, u32[]{:S(2)}) copy-start(bf16[256,512]{1,0:T(8,128)(2,1)S(1)} %get-tuple-element.71) | copy-start | bytes 786436
  67.2 27.4 %copy-start.7 = (bf16[256,512]{1,0:T(8,128)(2,1)}, bf16[256,512]{1,0:T(8,128)(2,1)S(1)}, u32[]{:S(2)}) copy-start(bf16[256,512]{1,0:T(8,128)(2,1)S(1)} %get-tuple-element.75) | copy-start | bytes 786436
  68.8 5.5 %collective-permute-start.4 = (bf16[2,256,512]{2,0,1:T(2,128)(2,1)}, bf16[2,256,512]{2,0,1:T(2,128)(2,1)S(1)}, u32[]{:S(2)}, u32[]{:S(2)}) collective-permute-start(bf16[2,256,512]{2,0,1:T(2,128)(2,1)} %collective-permute-done.3), channel_id=1, source_target_pairs={{0,4},{4,0},{8,12},{12,8},{16,20},{20,16},{24,28},{28,24},{32,36},... | collective-permute-start | bytes 1572872 | tf_op jit(solution)/shard_map/ppermute | solution.py:10
  69.9 6.2 %collective-permute-start.6 = (bf16[2,256,512]{2,0,1:T(2,128)(2,1)}, bf16[2,256,512]{2,0,1:T(2,128)(2,1)S(1)}, u32[]{:S(2)}, u32[]{:S(2)}) collective-permute-start(bf16[2,256,512]{2,0,1:T(2,128)(2,1)} %collective-permute-done.5), channel_id=1, source_target_pairs={{0,4},{4,0},{8,12},{12,8},{16,20},{20,16},{24,28},{28,24},{32,36},... | collective-permute-start | bytes 1572872 | tf_op jit(solution)/shard_map/ppermute | solution.py:10
  73.3 20.8 %copy-start.9 = (bf16[256,512]{1,0:T(8,128)(2,1)}, bf16[256,512]{1,0:T(8,128)(2,1)S(1)}, u32[]{:S(2)}) copy-start(bf16[256,512]{1,0:T(8,128)(2,1)S(1)} %get-tuple-element.69) | copy-start | bytes 786436
  75.1 19.5 %copy-start.11 = (bf16[256,512]{1,0:T(8,128)(2,1)}, bf16[256,512]{1,0:T(8,128)(2,1)S(1)}, u32[]{:S(2)}) copy-start(bf16[256,512]{1,0:T(8,128)(2,1)S(1)} %get-tuple-element.73) | copy-start | bytes 786436
  84.5 5.2 %collective-permute-start.8 = (f32[2,256,512]{2,1,0:T(8,128)S(1)}, f32[2,256,512]{2,1,0:T(8,128)S(1)}, u32[]{:S(2)}, u32[]{:S(2)}) collective-permute-start(f32[2,256,512]{2,1,0:T(8,128)S(1)} %pad_maximum_fusion.2), channel_id=1, source_target_pairs={{0,4},{4,0},{8,12},{12,8},{16,20},{20,16},{24,28},{28,24},{32,36},... | collective-permute-start | bytes 3145736 | tf_op jit(solution)/shard_map/ppermute | solution.py:10
  85.4 4.7 %collective-permute-start.10 = (f32[2,256,512]{2,1,0:T(8,128)S(1)}, f32[2,256,512]{2,1,0:T(8,128)S(1)}, u32[]{:S(2)}, u32[]{:S(2)}) collective-permute-start(f32[2,256,512]{2,1,0:T(8,128)S(1)} %pad_maximum_fusion.1), channel_id=1, source_target_pairs={{0,4},{4,0},{8,12},{12,8},{16,20},{20,16},{24,28},{28,24},{32,36},... | collective-permute-start | bytes 3145736 | tf_op jit(solution)/shard_map/ppermute | solution.py:10
  86.4 5.2 %collective-permute-start.12 = (f32[2,256,512]{2,1,0:T(8,128)S(1)}, f32[2,256,512]{2,1,0:T(8,128)S(1)}, u32[]{:S(2)}, u32[]{:S(2)}) collective-permute-start(f32[2,256,512]{2,1,0:T(8,128)S(1)} %pad_maximum_fusion), channel_id=1, source_target_pairs={{0,4},{4,0},{8,12},{12,8},{16,20},{20,16},{24,28},{28,24},{32,36},... | collective-permute-start | bytes 3145736 | tf_op jit(solution)/shard_map/ppermute | solution.py:10
  88.4 6.7 %collective-permute-start.7 = (f32[2,256,512]{2,1,0:T(8,128)S(1)}, f32[2,256,512]{2,1,0:T(8,128)S(1)}, u32[]{:S(2)}, u32[]{:S(2)}) collective-permute-start(f32[2,256,512]{2,1,0:T(8,128)S(1)} %pad_maximum_fusion.3), channel_id=1, source_target_pairs={{0,4},{4,0},{8,12},{12,8},{16,20},{20,16},{24,28},{28,24},{32,36},... | collective-permute-start | bytes 3145736 | tf_op jit(solution)/shard_map/ppermute | solution.py:10
  90.0 25.8 %collective-permute-start.9 = (bf16[2,256,512]{2,1,0:T(8,128)(2,1)S(1)}, bf16[2,256,512]{2,1,0:T(8,128)(2,1)S(1)}, u32[]{:S(2)}, u32[]{:S(2)}) collective-permute-start(bf16[2,256,512]{2,1,0:T(8,128)(2,1)S(1)} %fusion.39), channel_id=1, source_target_pairs={{0,1},{1,2},{2,3},{3,0},{4,5},{5,6},{6,7},{7,4},{8,9},{9,10},{10,1... | collective-permute-start | bytes 1572872 | tf_op jit(solution)/shard_map/ppermute | solution.py:15
  91.0 24.8 %collective-permute-start.11 = (bf16[2,256,512]{2,1,0:T(8,128)(2,1)S(1)}, bf16[2,256,512]{2,1,0:T(8,128)(2,1)S(1)}, u32[]{:S(2)}, u32[]{:S(2)}) collective-permute-start(bf16[2,256,512]{2,1,0:T(8,128)(2,1)S(1)} %fusion.36), channel_id=1, source_target_pairs={{0,2},{1,3},{2,0},{3,1},{4,6},{5,7},{6,4},{7,5},{8,10},{9,11},{10,... | collective-permute-start | bytes 1572872 | tf_op jit(solution)/shard_map/ppermute | solution.py:15
  91.8 24.7 %collective-permute-start.13 = (bf16[2,256,512]{2,1,0:T(8,128)(2,1)S(1)}, bf16[2,256,512]{2,1,0:T(8,128)(2,1)S(1)}, u32[]{:S(2)}, u32[]{:S(2)}) collective-permute-start(bf16[2,256,512]{2,1,0:T(8,128)(2,1)S(1)} %fusion.33), channel_id=1, source_target_pairs={{0,3},{1,0},{2,1},{3,2},{4,7},{5,4},{6,5},{7,6},{8,11},{9,8},{10,9... | collective-permute-start | bytes 1572872 | tf_op jit(solution)/shard_map/ppermute | solution.py:15
  95.1 21.8 %copy-start.14 = (bf16[1,2048,512]{2,1,0:T(8,128)(2,1)}, bf16[1,2048,512]{2,1,0:T(8,128)(2,1)S(1)}, u32[]{:S(2)}) copy-start(bf16[1,2048,512]{2,1,0:T(8,128)(2,1)S(1)} %fusion.18) | copy-start | bytes 6291460
  118.2 24.7 %all-to-all-start.1 = ((bf16[2,64,4,512]{3,0,2,1:T(2,128)(2,1)}), bf16[2,64,4,512]{3,0,2,1:T(2,128)(2,1)}, u32[]{:S(2)}, u32[]{:S(2)}) async-start(bf16[2,64,4,512]{3,0,2,1:T(2,128)(2,1)} %bitcast.211), calls=%async_computation.1 | async-start | bytes 1048576 | tf_op jit(solution)/shard_map/all_to_all | solution.py:144
  (12 other events, 31.7 us)

commit v5 on v2

--- a/solution.py
+++ b/solution.py
@@ -13,6 +13,10 @@
 def shifted(value, axis, step):
     size = lax.axis_size(axis)
     return lax.ppermute(value, axis, [(i, (i + step) % size) for i in range(size)])
+
+
+def ring_send(value, step):
+    return shifted(value, "tensor", step)
 
 
 def silu_parts(gate_pre):
@@ -55,9 +59,14 @@
     ).astype(jnp.bfloat16)
     outbound = outbound.reshape(2, n_expert, half_cap, feat_slice)
     arrived = lax.all_to_all(outbound, "expert", split_axis=1, concat_axis=1, tiled=True)
-    pieces = [arrived.reshape(2, rows_out, feat_slice)]
-    pieces += [shifted(pieces[0], "tensor", k) for k in range(1, n_tensor)]
-    blocks = [jnp.concatenate((p, partner(p, "expert", 0)), axis=1) for p in pieces]
+    flat_in = arrived.reshape(2, rows_out, feat_slice)
+    blocks = [[], []]
+    for i in range(2):
+        own = flat_in[i]
+        for k in range(n_tensor):
+            p = own if k == 0 else ring_send(own, k)
+            blocks[i].append(jnp.concatenate((p, partner(p, "expert", 0)), axis=0))
+    blocks = list(zip(blocks[0], blocks[1]))
     src_off = [((t_idx - k) % n_tensor) * feat_slice for k in range(n_tensor)]
     w_gate = gate_weight[0]
     w_up = up_weight[0]
@@ -122,21 +131,28 @@
     gate_grad = gate_grad[None]
     up_grad = up_grad[None]
     down_grad = down_grad[None]
-    acc = None
-    for m in range(n_tensor):
-        off = ((t_idx + m) % n_tensor) * feat_slice
-        out_m = jnp.dot(hidden, cols_of(w_down, off), preferred_element_type=jnp.float32)
-        in_m = lax.dot_general(
+    def out_partial(off):
+        return jnp.dot(hidden, cols_of(w_down, off), preferred_element_type=jnp.float32)
+
+    def in_partial(off):
+        return lax.dot_general(
             grad_gate_pre, rows_of(w_gate, off), contract_cols, preferred_element_type=jnp.float32
         ) + lax.dot_general(
             grad_up_pre, rows_of(w_up, off), contract_cols, preferred_element_type=jnp.float32
         )
-        part_m = jnp.stack((out_m, in_m))
-        core_m = part_m[:, :rows_out] + partner(part_m[:, rows_out:], "expert", 0)
-        if m == 0:
-            acc = core_m
-        else:
-            acc = acc + shifted(core_m.astype(jnp.bfloat16), "tensor", m).astype(jnp.float32)
+
+    sums = []
+    for partial_of in (out_partial, in_partial):
+        acc = None
+        for m in range(n_tensor):
+            part_m = partial_of(((t_idx + m) % n_tensor) * feat_slice)
+            core_m = part_m[:rows_out] + partner(part_m[rows_out:], "expert", 0)
+            if m == 0:
+                acc = core_m
+            else:
+                acc = acc + ring_send(core_m.astype(jnp.bfloat16), m).astype(jnp.float32)
+        sums.append(acc)
+    acc = jnp.stack(sums)
     going_back = acc.astype(jnp.bfloat16).reshape(2, n_expert, half_cap, feat_slice)
     returned = lax.all_to_all(going_back, "expert", split_axis=1, concat_axis=1, tiled=True)
     flat_back = returned.reshape(2, rows_out, feat_slice)

time: 144 us -> 154 us (1.069)
  starting transfers between devices: 20.7 us -> 38.1 us
  local copies, waits for them, and re-layouts: 14 us -> 8.96 us
  waiting for transfers between devices: 42.5 us -> 38.3 us
  matrix products: 23.8 us -> 26.9 us
  other arithmetic: 11.5 us -> 9.91 us
    ppermute x6 -> x12, starting transfers between devices: 8.6 us -> 19.6 us  [shifted(): lax.ppermute(value, axis, [(i, (i + step) % size) for i in range(size)])]
    concatenate x1 -> x0, other arithmetic: 7.63 us -> none  [body(): jnp.concatenate((p, partner(p, 'expert', 0)), axis=1)]
    ppermute x8 -> x16, starting transfers between devices: 4.41 us -> 11.8 us  [partner(): lax.ppermute(value, axis, [(i, i ^ 1 << stride) for i in range(lax.axis_s...]
    another operation x4 -> x3, other arithmetic: 0.28 us -> 4.88 us  [the longest x1 3.09 us: body(): acc = jnp.stack(sums)]
    ppermute x6 -> x12, waiting for transfers between devices: 31.8 us -> 27.3 us  [shifted(): lax.ppermute(value, axis, [(i, (i + step) % size) for i in range(size)])]
    dot_general x4, matrix products: 1.87 us -> 5.05 us  [body(): lax.dot_general(b[0], grad_up_pre, contract_rows, preferred_element_type=...]
    slice x3 -> x9, local copies, waits for them, and re-layouts: 4.51 us -> 1.4 us  [the longest x8 1.21 us: body(): core_m = part_m[:rows_out] + partner(part_m[rows_out:], 'expert', 0)]
    unnamed x31 -> x32, local copies, waits for them, and re-layouts: 4.37 us -> 1.93 us
  transfers between devices with their start and end apart: 15 -> 29, of which waited for: 5 -> 9; matrix products, arithmetic and copies ran while one was open for 18% -> 17% of each run, Pallas kernels for 0% -> 0%
where the time goes in v5:
time: 154 us
  waiting for transfers between devices  38.3 us (25%)
  starting transfers between devices  38.1 us (25%)
  blocking collectives  30.3 us (20%)
  matrix products  26.9 us (17%)
  other arithmetic  9.91 us (6%)
  local copies, waits for them, and re-layouts  8.96 us (6%)
    all_to_all x1, blocking collectives, body(): lax.all_to_all(outbound, 'expert', split_axis=1, concat_axis=1, tiled=True)  30.3 us
    ppermute x12, waiting for transfers between devices, shifted(): lax.ppermute(value, axis, [(i, (i + step) % size) for i in range(size)])  27.3 us
    ppermute x12, starting transfers between devices, shifted(): lax.ppermute(value, axis, [(i, (i + step) % size) for i in range(size)])  19.6 us
    ppermute x16, starting transfers between devices, partner(): lax.ppermute(value, axis, [(i, i ^ 1 << stride) for i in range(lax.axis_s...  11.8 us
    all_to_all x1, waiting for transfers between devices, body(): lax.all_to_all(going_back, 'expert', split_axis=1, concat_axis=1, tiled=T...  10.7 us
    all_to_all x1, starting transfers between devices, body(): lax.all_to_all(going_back, 'expert', split_axis=1, concat_axis=1, tiled=T...  6.69 us
    dot_general x4, matrix products, body(): lax.dot_general(b[0], grad_up_pre, contract_rows, preferred_element_type=...  5.05 us
    dot_general x4, matrix products, body(): lax.dot_general(b[0], grad_gate_pre, contract_rows, preferred_element_typ...  5.02 us
  transfers between devices with their start and end apart: 29, of which 9 were waited for; matrix products, arithmetic and copies ran while one was open for 17% of the time, Pallas kernels for 0%

profile of v5, /device:TPU:1, one launch (start us, length us, event | category | flops | bytes accessed | tf_op | source)
XLA Modules:
  0.0 153.7 jit_solution(16189450252736751963)
XLA Ops:
  5.6 30.3 %all_to_all.10 = bf16[2,64,4,512]{3,2,0,1:T(4,128)(2,1)S(1)} all-to-all(bf16[2,64,4,512]{3,2,0,1:T(4,128)(2,1)S(1)} %copy.27), channel_id=1, replica_groups=mesh['expert'=64,'tensor'=4] {'expert'}, dimensions={1} | all-to-all | bytes 1048576 | tf_op jit(solution)/shard_map/all_to_all | solution.py:61
  37.5 1.5 %collective-permute-start.5 = (bf16[256,512]{1,0:T(8,128)(2,1)S(1)}, bf16[256,512]{1,0:T(8,128)(2,1)S(1)}, u32[]{:S(2)}, u32[]{:S(2)}) collective-permute-start(bf16[256,512]{1,0:T(8,128)(2,1)S(1)} %squeeze.19), channel_id=1, source_target_pairs={{0,3},{1,0},{2,1},{3,2},{4,7},{5,4},{6,5},{7,6},{8,11},{9,8},{10,9... | collective-permute-start | bytes 786440 | tf_op jit(solution)/shard_map/ppermute | solution.py:15
  39.0 1.5 collective-permute-start.3
  40.8 2.4 %collective-permute-start.19 = (bf16[256,512]{1,0:T(8,128)(2,1)S(1)}, bf16[256,512]{1,0:T(8,128)(2,1)S(1)}, u32[]{:S(2)}, u32[]{:S(2)}) collective-permute-start(bf16[256,512]{1,0:T(8,128)(2,1)S(1)} %squeeze.20), channel_id=1, source_target_pairs={{0,3},{1,0},{2,1},{3,2},{4,7},{5,4},{6,5},{7,6},{8,11},{9,8},{10,9... | collective-permute-start | bytes 786440 | tf_op jit(solution)/shard_map/ppermute | solution.py:15
  43.3 1.7 %collective-permute-done.15 = bf16[256,512]{1,0:T(8,128)(2,1)S(1)} collective-permute-done((bf16[256,512]{1,0:T(8,128)(2,1)S(1)}, bf16[256,512]{1,0:T(8,128)(2,1)S(1)}, u32[]{:S(2)}, u32[]{:S(2)}) %collective-permute-start.15) | collective-permute-done | bytes 262176 | tf_op jit(solution)/shard_map/ppermute | solution.py:15
  45.0 2.4 %collective-permute-start = (bf16[256,512]{1,0:T(8,128)(2,1)S(1)}, bf16[256,512]{1,0:T(8,128)(2,1)S(1)}, u32[]{:S(2)}, u32[]{:S(2)}) collective-permute-start(bf16[256,512]{1,0:T(8,128)(2,1)S(1)} %squeeze.19), channel_id=1, source_target_pairs={{0,4},{4,0},{8,12},{12,8},{16,20},{20,16},{24,28},{28,24},{32,36},... | collective-permute-start | bytes 786440 | tf_op jit(solution)/shard_map/ppermute | solution.py:10
  47.4 8.7 %collective-permute-done.19 = bf16[256,512]{1,0:T(8,128)(2,1)S(1)} collective-permute-done((bf16[256,512]{1,0:T(8,128)(2,1)S(1)}, bf16[256,512]{1,0:T(8,128)(2,1)S(1)}, u32[]{:S(2)}, u32[]{:S(2)}) %collective-permute-start.19) | collective-permute-done | bytes 262176 | tf_op jit(solution)/shard_map/ppermute | solution.py:15
  56.1 2.5 %collective-permute-start.17 = (bf16[256,512]{1,0:T(8,128)(2,1)S(1)}, bf16[256,512]{1,0:T(8,128)(2,1)S(1)}, u32[]{:S(2)}, u32[]{:S(2)}) collective-permute-start(bf16[256,512]{1,0:T(8,128)(2,1)S(1)} %squeeze.20), channel_id=1, source_target_pairs={{0,2},{1,3},{2,0},{3,1},{4,6},{5,7},{6,4},{7,5},{8,10},{9,11},{10,... | collective-permute-start | bytes 786440 | tf_op jit(solution)/shard_map/ppermute | solution.py:15
  58.6 1.8 %collective-permute-start.14 = (bf16[256,512]{1,0:T(8,128)(2,1)S(1)}, bf16[256,512]{1,0:T(8,128)(2,1)S(1)}, u32[]{:S(2)}, u32[]{:S(2)}) collective-permute-start(bf16[256,512]{1,0:T(8,128)(2,1)S(1)} %squeeze.20), channel_id=1, source_target_pairs={{0,4},{4,0},{8,12},{12,8},{16,20},{20,16},{24,28},{28,24},{32,36},... | collective-permute-start | bytes 786440 | tf_op jit(solution)/shard_map/ppermute | solution.py:10
  61.8 2.1 %collective-permute-done.17 = bf16[256,512]{1,0:T(8,128)(2,1)S(1)} collective-permute-done((bf16[256,512]{1,0:T(8,128)(2,1)S(1)}, bf16[256,512]{1,0:T(8,128)(2,1)S(1)}, u32[]{:S(2)}, u32[]{:S(2)}) %collective-permute-start.17) | collective-permute-done | bytes 262176 | tf_op jit(solution)/shard_map/ppermute | solution.py:15
  63.9 2.4 %collective-permute-start.20 = (bf16[256,512]{1,0:T(8,128)(2,1)S(1)}, bf16[256,512]{1,0:T(8,128)(2,1)S(1)}, u32[]{:S(2)}, u32[]{:S(2)}) collective-permute-start(bf16[256,512]{1,0:T(8,128)(2,1)S(1)} %collective-permute-done.19), channel_id=1, source_target_pairs={{0,4},{4,0},{8,12},{12,8},{16,20},{20,16},{24,28},{28,24},{32,36},... | collective-permute-start | bytes 786440 | tf_op jit(solution)/shard_map/ppermute | solution.py:10
  81.1 1.6 %broadcast_in_dim.43.clone = bf16[1,2048,512]{2,1,0:T(8,128)(2,1)} broadcast(bf16[]{:T(256)} %constant.110.clone.1), dimensions={} | broadcast | bytes 2097154 | tf_op jit(solution)/shard_map/broadcast_in_dim | solution.py:131
  91.7 2.7 %collective-permute-start.13 = (bf16[256,512]{1,0:T(8,128)(2,1)S(1)}, bf16[256,512]{1,0:T(8,128)(2,1)S(1)}, u32[]{:S(2)}, u32[]{:S(2)}) collective-permute-start(bf16[256,512]{1,0:T(8,128)(2,1)S(1)} %fusion.38), channel_id=1, source_target_pairs={{0,3},{1,0},{2,1},{3,2},{4,7},{5,4},{6,5},{7,6},{8,11},{9,8},{10,9... | collective-permute-start | bytes 786440 | tf_op jit(solution)/shard_map/ppermute | solution.py:15
  98.7 2.3 %collective-permute-start.27 = (bf16[256,512]{1,0:T(8,128)(2,1)}, bf16[256,512]{1,0:T(8,128)(2,1)}, u32[]{:S(2)}, u32[]{:S(2)}) collective-permute-start(bf16[256,512]{1,0:T(8,128)(2,1)} %fusion.31), channel_id=1, source_target_pairs={{0,3},{1,0},{2,1},{3,2},{4,7},{5,4},{6,5},{7,6},{8,11},{9,8},{10,9... | collective-permute-start | bytes 786440 | tf_op jit(solution)/shard_map/ppermute | solution.py:15
  101.0 4.2 %collective-permute-done.13 = bf16[256,512]{1,0:T(8,128)(2,1)S(1)} collective-permute-done((bf16[256,512]{1,0:T(8,128)(2,1)S(1)}, bf16[256,512]{1,0:T(8,128)(2,1)S(1)}, u32[]{:S(2)}, u32[]{:S(2)}) %collective-permute-start.13) | collective-permute-done | bytes 262176 | tf_op jit(solution)/shard_map/ppermute | solution.py:15
  105.2 4.3 %collective-permute-start.23 = (bf16[256,512]{1,0:T(8,128)(2,1)}, bf16[256,512]{1,0:T(8,128)(2,1)}, u32[]{:S(2)}, u32[]{:S(2)}) collective-permute-start(bf16[256,512]{1,0:T(8,128)(2,1)} %fusion.33), channel_id=1, source_target_pairs={{0,1},{1,2},{2,3},{3,0},{4,5},{5,6},{6,7},{7,4},{8,9},{9,10},{10,1... | collective-permute-start | bytes 786440 | tf_op jit(solution)/shard_map/ppermute | solution.py:15
  111.4 5.4 %collective-permute-done.27 = bf16[256,512]{1,0:T(8,128)(2,1)} collective-permute-done((bf16[256,512]{1,0:T(8,128)(2,1)}, bf16[256,512]{1,0:T(8,128)(2,1)}, u32[]{:S(2)}, u32[]{:S(2)}) %collective-permute-start.27) | collective-permute-done | bytes 262176 | tf_op jit(solution)/shard_map/ppermute | solution.py:15
  116.8 4.5 %collective-permute-done.23 = bf16[256,512]{1,0:T(8,128)(2,1)} collective-permute-done((bf16[256,512]{1,0:T(8,128)(2,1)}, bf16[256,512]{1,0:T(8,128)(2,1)}, u32[]{:S(2)}, u32[]{:S(2)}) %collective-permute-start.23) | collective-permute-done | bytes 262176 | tf_op jit(solution)/shard_map/ppermute | solution.py:15
  121.3 1.6 %fusion.37 = bf16[256,512]{1,0:T(8,128)(2,1)S(1)} fusion(f32[256,512]{1,0:T(8,128)} %collective-permute-done.21, f32[512,512]{1,0:T(8,128)} %copy-done.3, bf16[256,512]{1,0:T(8,128)(2,1)} %collective-permute-done.27, bf16[256,512]{1,0:T(8,128)(2,1)} %collective-permute-done.25, bf16[256,512]{1,0:T(8,128)(2,1)} %collective-permute-done.23), kind=kLoop, calls=%fused_computation.70 | loop fusion | flops 1048576 | bytes 2097152 | tf_op jit(solution)/shard_map/convert.2
  123.8 3.1 %pad_maximum_fusion = bf16[2,64,4,512]{3,0,2,1:T(2,128)(2,1)} fusion(bf16[1,64,4,512]{3,0,2,1:T(2,128)(2,1)} %stack.25, bf16[1,64,4,512]{3,0,2,1:T(2,128)(2,1)} %stack.24), kind=kLoop, calls=%fused_computation.82 | loop fusion | flops 1048576 | bytes 1048576 | tf_op jit(solution)/shard_map/stack | solution.py:155
  126.8 6.7 %all-to-all-start.1 = ((bf16[2,64,4,512]{3,0,2,1:T(2,128)(2,1)}), bf16[2,64,4,512]{3,0,2,1:T(2,128)(2,1)}, u32[]{:S(2)}, u32[]{:S(2)}) async-start(bf16[2,64,4,512]{3,0,2,1:T(2,128)(2,1)} %pad_maximum_fusion), calls=%async_computation.1 | async-start | bytes 1048576 | tf_op jit(solution)/shard_map/all_to_all | solution.py:157
  133.6 1.5 broadcast_in_dim.43.clone.1
  140.1 10.7 %all-to-all-done.1 = bf16[2,64,4,512]{3,0,2,1:T(2,128)(2,1)} async-done(((bf16[2,64,4,512]{3,0,2,1:T(2,128)(2,1)}), bf16[2,64,4,512]{3,0,2,1:T(2,128)(2,1)}, u32[]{:S(2)}, u32[]{:S(2)}) %all-to-all-start.1) | async-done | bytes 524320 | tf_op jit(solution)/shard_map/all_to_all | solution.py:157
  150.8 1.4 fusion.28
  (145 shorter events, 45.3 us)
Async XLA Ops:
  36.1 8.9 %collective-permute-start.15 = (bf16[256,512]{1,0:T(8,128)(2,1)S(1)}, bf16[256,512]{1,0:T(8,128)(2,1)S(1)}, u32[]{:S(2)}, u32[]{:S(2)}) collective-permute-start(bf16[256,512]{1,0:T(8,128)(2,1)S(1)} %squeeze.20), channel_id=1, source_target_pairs={{0,1},{1,2},{2,3},{3,0},{4,5},{5,6},{6,7},{7,4},{8,9},{9,10},{10,1... | collective-permute-start | bytes 786440 | tf_op jit(solution)/shard_map/ppermute | solution.py:15
  37.5 21.1 %collective-permute-start.5 = (bf16[256,512]{1,0:T(8,128)(2,1)S(1)}, bf16[256,512]{1,0:T(8,128)(2,1)S(1)}, u32[]{:S(2)}, u32[]{:S(2)}) collective-permute-start(bf16[256,512]{1,0:T(8,128)(2,1)S(1)} %squeeze.19), channel_id=1, source_target_pairs={{0,3},{1,0},{2,1},{3,2},{4,7},{5,4},{6,5},{7,6},{8,11},{9,8},{10,9... | collective-permute-start | bytes 786440 | tf_op jit(solution)/shard_map/ppermute | solution.py:15
  39.0 21.4 %collective-permute-start.3 = (bf16[256,512]{1,0:T(8,128)(2,1)S(1)}, bf16[256,512]{1,0:T(8,128)(2,1)S(1)}, u32[]{:S(2)}, u32[]{:S(2)}) collective-permute-start(bf16[256,512]{1,0:T(8,128)(2,1)S(1)} %squeeze.19), channel_id=1, source_target_pairs={{0,2},{1,3},{2,0},{3,1},{4,6},{5,7},{6,4},{7,5},{8,10},{9,11},{10,... | collective-permute-start | bytes 786440 | tf_op jit(solution)/shard_map/ppermute | solution.py:15
  40.5 20.0 %collective-permute-start.1 = (bf16[256,512]{1,0:T(8,128)(2,1)S(1)}, bf16[256,512]{1,0:T(8,128)(2,1)S(1)}, u32[]{:S(2)}, u32[]{:S(2)}) collective-permute-start(bf16[256,512]{1,0:T(8,128)(2,1)S(1)} %squeeze.19), channel_id=1, source_target_pairs={{0,1},{1,2},{2,3},{3,0},{4,5},{5,6},{6,7},{7,4},{8,9},{9,10},{10,1... | collective-permute-start | bytes 786440 | tf_op jit(solution)/shard_map/ppermute | solution.py:15
  40.8 15.2 %collective-permute-start.19 = (bf16[256,512]{1,0:T(8,128)(2,1)S(1)}, bf16[256,512]{1,0:T(8,128)(2,1)S(1)}, u32[]{:S(2)}, u32[]{:S(2)}) collective-permute-start(bf16[256,512]{1,0:T(8,128)(2,1)S(1)} %squeeze.20), channel_id=1, source_target_pairs={{0,3},{1,0},{2,1},{3,2},{4,7},{5,4},{6,5},{7,6},{8,11},{9,8},{10,9... | collective-permute-start | bytes 786440 | tf_op jit(solution)/shard_map/ppermute | solution.py:15
  45.0 16.2 %collective-permute-start = (bf16[256,512]{1,0:T(8,128)(2,1)S(1)}, bf16[256,512]{1,0:T(8,128)(2,1)S(1)}, u32[]{:S(2)}, u32[]{:S(2)}) collective-permute-start(bf16[256,512]{1,0:T(8,128)(2,1)S(1)} %squeeze.19), channel_id=1, source_target_pairs={{0,4},{4,0},{8,12},{12,8},{16,20},{20,16},{24,28},{28,24},{32,36},... | collective-permute-start | bytes 786440 | tf_op jit(solution)/shard_map/ppermute | solution.py:10
  56.1 7.8 %collective-permute-start.17 = (bf16[256,512]{1,0:T(8,128)(2,1)S(1)}, bf16[256,512]{1,0:T(8,128)(2,1)S(1)}, u32[]{:S(2)}, u32[]{:S(2)}) collective-permute-start(bf16[256,512]{1,0:T(8,128)(2,1)S(1)} %squeeze.20), channel_id=1, source_target_pairs={{0,2},{1,3},{2,0},{3,1},{4,6},{5,7},{6,4},{7,5},{8,10},{9,11},{10,... | collective-permute-start | bytes 786440 | tf_op jit(solution)/shard_map/ppermute | solution.py:15
  58.6 8.2 %collective-permute-start.14 = (bf16[256,512]{1,0:T(8,128)(2,1)S(1)}, bf16[256,512]{1,0:T(8,128)(2,1)S(1)}, u32[]{:S(2)}, u32[]{:S(2)}) collective-permute-start(bf16[256,512]{1,0:T(8,128)(2,1)S(1)} %squeeze.20), channel_id=1, source_target_pairs={{0,4},{4,0},{8,12},{12,8},{16,20},{20,16},{24,28},{28,24},{32,36},... | collective-permute-start | bytes 786440 | tf_op jit(solution)/shard_map/ppermute | solution.py:10
  60.4 9.4 %collective-permute-start.6 = (bf16[256,512]{1,0:T(8,128)(2,1)S(1)}, bf16[256,512]{1,0:T(8,128)(2,1)S(1)}, u32[]{:S(2)}, u32[]{:S(2)}) collective-permute-start(bf16[256,512]{1,0:T(8,128)(2,1)S(1)} %collective-permute-done.5), channel_id=1, source_target_pairs={{0,4},{4,0},{8,12},{12,8},{16,20},{20,16},{24,28},{28,24},{32,36},... | collective-permute-start | bytes 786440 | tf_op jit(solution)/shard_map/ppermute | solution.py:10
  60.6 9.8 %collective-permute-start.4 = (bf16[256,512]{1,0:T(8,128)(2,1)S(1)}, bf16[256,512]{1,0:T(8,128)(2,1)S(1)}, u32[]{:S(2)}, u32[]{:S(2)}) collective-permute-start(bf16[256,512]{1,0:T(8,128)(2,1)S(1)} %collective-permute-done.3), channel_id=1, source_target_pairs={{0,4},{4,0},{8,12},{12,8},{16,20},{20,16},{24,28},{28,24},{32,36},... | collective-permute-start | bytes 786440 | tf_op jit(solution)/shard_map/ppermute | solution.py:10
  63.9 7.4 %collective-permute-start.20 = (bf16[256,512]{1,0:T(8,128)(2,1)S(1)}, bf16[256,512]{1,0:T(8,128)(2,1)S(1)}, u32[]{:S(2)}, u32[]{:S(2)}) collective-permute-start(bf16[256,512]{1,0:T(8,128)(2,1)S(1)} %collective-permute-done.19), channel_id=1, source_target_pairs={{0,4},{4,0},{8,12},{12,8},{16,20},{20,16},{24,28},{28,24},{32,36},... | collective-permute-start | bytes 786440 | tf_op jit(solution)/shard_map/ppermute | solution.py:10
  77.0 14.0 %collective-permute-start.12 = (f32[256,512]{1,0:T(8,128)S(1)}, f32[256,512]{1,0:T(8,128)S(1)}, u32[]{:S(2)}, u32[]{:S(2)}) collective-permute-start(f32[256,512]{1,0:T(8,128)S(1)} %slice.90), channel_id=1, source_target_pairs={{0,4},{4,0},{8,12},{12,8},{16,20},{20,16},{24,28},{28,24},{32,36},... | collective-permute-start | bytes 1572872 | tf_op jit(solution)/shard_map/ppermute | solution.py:10
  77.5 13.9 %collective-permute-start.10 = (f32[256,512]{1,0:T(8,128)S(1)}, f32[256,512]{1,0:T(8,128)S(1)}, u32[]{:S(2)}, u32[]{:S(2)}) collective-permute-start(f32[256,512]{1,0:T(8,128)S(1)} %slice.88), channel_id=1, source_target_pairs={{0,4},{4,0},{8,12},{12,8},{16,20},{20,16},{24,28},{28,24},{32,36},... | collective-permute-start | bytes 1572872 | tf_op jit(solution)/shard_map/ppermute | solution.py:10
  77.7 14.0 %collective-permute-start.8 = (f32[256,512]{1,0:T(8,128)S(1)}, f32[256,512]{1,0:T(8,128)S(1)}, u32[]{:S(2)}, u32[]{:S(2)}) collective-permute-start(f32[256,512]{1,0:T(8,128)S(1)} %slice.86), channel_id=1, source_target_pairs={{0,4},{4,0},{8,12},{12,8},{16,20},{20,16},{24,28},{28,24},{32,36},... | collective-permute-start | bytes 1572872 | tf_op jit(solution)/shard_map/ppermute | solution.py:10
  78.2 20.5 %collective-permute-start.7 = (f32[256,512]{1,0:T(8,128)S(1)}, f32[256,512]{1,0:T(8,128)S(1)}, u32[]{:S(2)}, u32[]{:S(2)}) collective-permute-start(f32[256,512]{1,0:T(8,128)S(1)} %slice.84), channel_id=1, source_target_pairs={{0,4},{4,0},{8,12},{12,8},{16,20},{20,16},{24,28},{28,24},{32,36},... | collective-permute-start | bytes 1572872 | tf_op jit(solution)/shard_map/ppermute | solution.py:10
  79.0 15.6 %collective-permute-start.26 = (f32[256,512]{1,0:T(8,128)S(1)}, f32[256,512]{1,0:T(8,128)S(1)}, u32[]{:S(2)}, u32[]{:S(2)}) collective-permute-start(f32[256,512]{1,0:T(8,128)S(1)} %slice.99), channel_id=1, source_target_pairs={{0,4},{4,0},{8,12},{12,8},{16,20},{20,16},{24,28},{28,24},{32,36},... | collective-permute-start | bytes 1572872 | tf_op jit(solution)/shard_map/ppermute | solution.py:10
  91.7 13.4 %collective-permute-start.13 = (bf16[256,512]{1,0:T(8,128)(2,1)S(1)}, bf16[256,512]{1,0:T(8,128)(2,1)S(1)}, u32[]{:S(2)}, u32[]{:S(2)}) collective-permute-start(bf16[256,512]{1,0:T(8,128)(2,1)S(1)} %fusion.38), channel_id=1, source_target_pairs={{0,3},{1,0},{2,1},{3,2},{4,7},{5,4},{6,5},{7,6},{8,11},{9,8},{10,9... | collective-permute-start | bytes 786440 | tf_op jit(solution)/shard_map/ppermute | solution.py:15
  94.5 10.7 %collective-permute-start.11 = (bf16[256,512]{1,0:T(8,128)(2,1)S(1)}, bf16[256,512]{1,0:T(8,128)(2,1)S(1)}, u32[]{:S(2)}, u32[]{:S(2)}) collective-permute-start(bf16[256,512]{1,0:T(8,128)(2,1)S(1)} %fusion.39), channel_id=1, source_target_pairs={{0,2},{1,3},{2,0},{3,1},{4,6},{5,7},{6,4},{7,5},{8,10},{9,11},{10,... | collective-permute-start | bytes 786440 | tf_op jit(solution)/shard_map/ppermute | solution.py:15
  95.7 14.5 %collective-permute-start.9 = (bf16[256,512]{1,0:T(8,128)(2,1)S(1)}, bf16[256,512]{1,0:T(8,128)(2,1)S(1)}, u32[]{:S(2)}, u32[]{:S(2)}) collective-permute-start(bf16[256,512]{1,0:T(8,128)(2,1)S(1)} %fusion.40), channel_id=1, source_target_pairs={{0,1},{1,2},{2,3},{3,0},{4,5},{5,6},{6,7},{7,4},{8,9},{9,10},{10,1... | collective-permute-start | bytes 786440 | tf_op jit(solution)/shard_map/ppermute | solution.py:15
  96.9 14.5 %collective-permute-start.21 = (f32[256,512]{1,0:T(8,128)}, f32[256,512]{1,0:T(8,128)}, u32[]{:S(2)}, u32[]{:S(2)}) collective-permute-start(f32[256,512]{1,0:T(8,128)} %slice.93), channel_id=1, source_target_pairs={{0,4},{4,0},{8,12},{12,8},{16,20},{20,16},{24,28},{28,24},{32,36},... | collective-permute-start | bytes 1572872 | tf_op jit(solution)/shard_map/ppermute | solution.py:10
  98.7 18.0 %collective-permute-start.27 = (bf16[256,512]{1,0:T(8,128)(2,1)}, bf16[256,512]{1,0:T(8,128)(2,1)}, u32[]{:S(2)}, u32[]{:S(2)}) collective-permute-start(bf16[256,512]{1,0:T(8,128)(2,1)} %fusion.31), channel_id=1, source_target_pairs={{0,3},{1,0},{2,1},{3,2},{4,7},{5,4},{6,5},{7,6},{8,11},{9,8},{10,9... | collective-permute-start | bytes 786440 | tf_op jit(solution)/shard_map/ppermute | solution.py:15
  105.2 11.6 %collective-permute-start.25 = (bf16[256,512]{1,0:T(8,128)(2,1)}, bf16[256,512]{1,0:T(8,128)(2,1)}, u32[]{:S(2)}, u32[]{:S(2)}) collective-permute-start(bf16[256,512]{1,0:T(8,128)(2,1)} %fusion.32), channel_id=1, source_target_pairs={{0,2},{1,3},{2,0},{3,1},{4,6},{5,7},{6,4},{7,5},{8,10},{9,11},{10,... | collective-permute-start | bytes 786440 | tf_op jit(solution)/shard_map/ppermute | solution.py:15
  105.2 16.1 %collective-permute-start.23 = (bf16[256,512]{1,0:T(8,128)(2,1)}, bf16[256,512]{1,0:T(8,128)(2,1)}, u32[]{:S(2)}, u32[]{:S(2)}) collective-permute-start(bf16[256,512]{1,0:T(8,128)(2,1)} %fusion.33), channel_id=1, source_target_pairs={{0,1},{1,2},{2,3},{3,0},{4,5},{5,6},{6,7},{7,4},{8,9},{9,10},{10,1... | collective-permute-start | bytes 786440 | tf_op jit(solution)/shard_map/ppermute | solution.py:15
  126.8 23.9 %all-to-all-start.1 = ((bf16[2,64,4,512]{3,0,2,1:T(2,128)(2,1)}), bf16[2,64,4,512]{3,0,2,1:T(2,128)(2,1)}, u32[]{:S(2)}, u32[]{:S(2)}) async-start(bf16[2,64,4,512]{3,0,2,1:T(2,128)(2,1)} %pad_maximum_fusion), calls=%async_computation.1 | async-start | bytes 1048576 | tf_op jit(solution)/shard_map/all_to_all | solution.py:157
  (16 other events, 164.2 us)

commit v6 on v4

--- a/solution.py
+++ b/solution.py
@@ -46,21 +46,21 @@
     slot_pos = jnp.sum(before * lab_hot, axis=1).astype(jnp.int32)
     target_row = lang_label * capacity + slot_pos
     rows_out = n_expert * half_cap
-    sources = jnp.stack((tokens, grad_rows))
+    sources = jnp.concatenate((tokens, grad_rows), axis=1)
     dispatch_map = (
         jnp.arange(rows_out, dtype=jnp.int32)[:, None] == target_row[None, :]
     ).astype(jnp.bfloat16)
-    outbound = jnp.einsum(
-        "rt,ktw->krw", dispatch_map, sources, preferred_element_type=jnp.float32
-    ).astype(jnp.bfloat16)
-    outbound = outbound.reshape(2, n_expert, half_cap, feat_slice)
-    arrived = lax.all_to_all(outbound, "expert", split_axis=1, concat_axis=1, tiled=True)
-    pieces = [arrived.reshape(2, rows_out, feat_slice)]
+    outbound = jnp.dot(dispatch_map, sources, preferred_element_type=jnp.float32).astype(
+        jnp.bfloat16
+    )
+    outbound = outbound.reshape(n_expert, half_cap, 2 * feat_slice)
+    arrived = lax.all_to_all(outbound, "expert", split_axis=0, concat_axis=0, tiled=True)
+    pieces = [arrived.reshape(rows_out, 2 * feat_slice)]
     pieces += [shifted(pieces[0], "tensor", k) for k in range(1, n_tensor)]
     blocks = []
     for p in pieces:
-        q = partner(p, "expert", 0)
-        blocks.append([jnp.concatenate((p[i], q[i]), axis=0) for i in range(2)])
+        both = jnp.concatenate((p, partner(p, "expert", 0)), axis=0)
+        blocks.append((both[:, :feat_slice], both[:, feat_slice:]))
     src_off = [((t_idx - k) % n_tensor) * feat_slice for k in range(n_tensor)]
     w_gate = gate_weight[0]
     w_up = up_weight[0]
@@ -134,22 +134,26 @@
         ) + lax.dot_general(
             grad_up_pre, rows_of(w_up, off), contract_cols, preferred_element_type=jnp.float32
         )
-        part_m = jnp.stack((out_m, in_m))
-        core_m = part_m[:, :rows_out] + partner(part_m[:, rows_out:], "expert", 0)
+        part_m = jnp.concatenate((out_m, in_m), axis=1)
+        core_m = part_m[:rows_out] + partner(part_m[rows_out:], "expert", 0)
         if m == 0:
             acc = core_m
         else:
             acc = acc + shifted(core_m.astype(jnp.bfloat16), "tensor", m).astype(jnp.float32)
-    going_back = acc.astype(jnp.bfloat16).reshape(2, n_expert, half_cap, feat_slice)
-    returned = lax.all_to_all(going_back, "expert", split_axis=1, concat_axis=1, tiled=True)
-    flat_back = returned.reshape(2, rows_out, feat_slice)
+    going_back = acc.astype(jnp.bfloat16).reshape(n_expert, half_cap, 2 * feat_slice)
+    returned = lax.all_to_all(going_back, "expert", split_axis=0, concat_axis=0, tiled=True)
+    flat_back = returned.reshape(rows_out, 2 * feat_slice)
     home_map = (
         jnp.arange(rows_out, dtype=jnp.int32)[:, None] == target_row[None, :]
     ).astype(jnp.bfloat16)
-    gathered_home = jnp.einsum(
-        "rt,krw->ktw", home_map, flat_back, preferred_element_type=jnp.float32
-    ).astype(jnp.bfloat16)
-    return (gathered_home[0], gathered_home[1], gate_grad, up_grad, down_grad)
+    home = [
+        lax.dot_general(
+            home_map, flat_back[:, i * feat_slice : (i + 1) * feat_slice], contract_rows,
+            preferred_element_type=jnp.float32,
+        ).astype(jnp.bfloat16)
+        for i in range(2)
+    ]
+    return (home[0], home[1], gate_grad, up_grad, down_grad)
 
 
 def solution(mesh):

time: 146 us -> 142 us (0.973)
  starting transfers between devices: 18.8 us -> 30.5 us
  local copies, waits for them, and re-layouts: 20.4 us -> 9.69 us
  waiting for transfers between devices: 45.5 us -> 41.1 us
    slice x8 -> x0, local copies, waits for them, and re-layouts: 10.2 us -> none  [body(): blocks.append([jnp.concatenate((p[i], q[i]), axis=0) for i in range(2)])]
    ppermute x8, starting transfers between devices: 4.27 us -> 14.4 us  [partner(): lax.ppermute(value, axis, [(i, i ^ 1 << stride) for i in range(lax.axis_s...]
    ppermute x6, waiting for transfers between devices: 37.1 us -> 30.4 us  [shifted(): lax.ppermute(value, axis, [(i, (i + step) % size) for i in range(size)])]
    unnamed x51 -> x30, local copies, waits for them, and re-layouts: 4.43 us -> 2.01 us
    all_to_all x1, waiting for transfers between devices: 8.37 us -> 10.6 us  [body(): lax.all_to_all(going_back, 'expert', split_axis=0, concat_axis=0, tiled=T...]
    ppermute x6, starting transfers between devices: 7.08 us -> 9.19 us  [shifted(): lax.ppermute(value, axis, [(i, (i + step) % size) for i in range(size)])]
    dot_general x4, matrix products: 3.75 us -> 1.88 us  [body(): lax.dot_general(b[0], grad_up_pre, contract_rows, preferred_element_type=...]
    reshape x3 -> x4, local copies, waits for them, and re-layouts: 1.67 us -> 3.51 us  [the longest x1 2.04 us: body(): acc.astype(jnp.bfloat16).reshape(n_expert, half_cap, 2 * feat_slice)]
  transfers between devices with their start and end apart: 15 -> 15, of which waited for: 5 -> 4; matrix products, arithmetic and copies ran while one was open for 20% -> 13% of each run, Pallas kernels for 0% -> 0%
where the time goes in v6:
time: 142 us; the launch traced here: 141 us
  waiting for transfers between devices  41.1 us (29%)
  starting transfers between devices  30.5 us (21%)
  blocking collectives  30.4 us (21%)
  matrix products  24.4 us (17%)
  local copies, waits for them, and re-layouts  9.69 us (7%)
  other arithmetic  3.83 us (3%)
    ppermute x6, waiting for transfers between devices, shifted(): lax.ppermute(value, axis, [(i, (i + step) % size) for i in range(size)])  30.4 us
    all_to_all x1, blocking collectives, body(): lax.all_to_all(outbound, 'expert', split_axis=0, concat_axis=0, tiled=True)  30.4 us
    ppermute x8, starting transfers between devices, partner(): lax.ppermute(value, axis, [(i, i ^ 1 << stride) for i in range(lax.axis_s...  14.4 us
    all_to_all x1, waiting for transfers between devices, body(): lax.all_to_all(going_back, 'expert', split_axis=0, concat_axis=0, tiled=T...  10.6 us
    ppermute x6, starting transfers between devices, shifted(): lax.ppermute(value, axis, [(i, (i + step) % size) for i in range(size)])  9.19 us
    all_to_all x1, starting transfers between devices, body(): lax.all_to_all(going_back, 'expert', split_axis=0, concat_axis=0, tiled=T...  6.93 us
    dot_general x4, matrix products, body(): lax.dot_general(b[0], grad_gate_pre, contract_rows, preferred_element_typ...  5.12 us
  transfers between devices with their start and end apart: 15, of which 4 were waited for; matrix products, arithmetic and copies ran while one was open for 13% of the time, Pallas kernels for 0%

profile of v6, /device:TPU:1, one launch (start us, length us, event | category | flops | bytes accessed | tf_op | source)
XLA Modules:
  0.0 141.2 jit_solution(7695880193616096242)
XLA Ops:
  3.1 1.0 multiply_convert_fusion.3
  4.0 1.2 convolution_convert_fusion.12
  5.4 30.4 %all_to_all.10 = bf16[64,4,1024]{2,1,0:T(4,128)(2,1)} all-to-all(bf16[64,4,1024]{2,1,0:T(4,128)(2,1)S(1)} %reshape.79), channel_id=1, replica_groups=mesh['expert'=64,'tensor'=4] {'expert'}, dimensions={0} | all-to-all | bytes 1048576 | tf_op jit(solution)/shard_map/all_to_all | solution.py:57
  35.8 1.2 reshape.80
  37.0 1.3 collective-permute-start.1
  38.3 1.5 %collective-permute-start.5 = (bf16[256,1024]{1,0:T(8,128)(2,1)S(1)}, bf16[256,1024]{1,0:T(8,128)(2,1)}, u32[]{:S(2)}, u32[]{:S(2)}) collective-permute-start(bf16[256,1024]{1,0:T(8,128)(2,1)S(1)} %reshape.80), channel_id=1, source_target_pairs={{0,3},{1,0},{2,1},{3,2},{4,7},{5,4},{6,5},{7,6},{8,11},{9,8},{10,9... | collective-permute-start | bytes 1572872 | tf_op jit(solution)/shard_map/ppermute | solution.py:15
  40.6 1.5 %collective-permute-start.3 = (bf16[256,1024]{1,0:T(8,128)(2,1)S(1)}, bf16[256,1024]{1,0:T(8,128)(2,1)S(1)}, u32[]{:S(2)}, u32[]{:S(2)}) collective-permute-start(bf16[256,1024]{1,0:T(8,128)(2,1)S(1)} %reshape.80), channel_id=1, source_target_pairs={{0,2},{1,3},{2,0},{3,1},{4,6},{5,7},{6,4},{7,5},{8,10},{9,11},{10,... | collective-permute-start | bytes 1572872 | tf_op jit(solution)/shard_map/ppermute | solution.py:15
  42.2 9.3 %collective-permute-done.1 = bf16[256,1024]{1,0:T(8,128)(2,1)S(1)} collective-permute-done((bf16[256,1024]{1,0:T(8,128)(2,1)S(1)}, bf16[256,1024]{1,0:T(8,128)(2,1)S(1)}, u32[]{:S(2)}, u32[]{:S(2)}) %collective-permute-start.1) | collective-permute-done | bytes 524320 | tf_op jit(solution)/shard_map/ppermute | solution.py:15
  51.5 1.2 collective-permute-start.2
  52.8 10.4 %collective-permute-start.6 = (bf16[256,1024]{1,0:T(8,128)(2,1)}, bf16[256,1024]{1,0:T(8,128)(2,1)S(1)}, u32[]{:S(2)}, u32[]{:S(2)}) collective-permute-start(bf16[256,1024]{1,0:T(8,128)(2,1)} %collective-permute-done.5), channel_id=1, source_target_pairs={{0,4},{4,0},{8,12},{12,8},{16,20},{20,16},{24,28},{28,24},{32,36},... | collective-permute-start | bytes 1572872 | tf_op jit(solution)/shard_map/ppermute | solution.py:10
  63.1 1.1 constant_dynamic-update-slice_fusion.7
  64.3 1.2 constant_dynamic-update-slice_fusion
  84.4 4.7 %collective-permute-start.11 = (bf16[256,1024]{0,1:T(8,128)(2,1)S(1)}, bf16[256,1024]{0,1:T(8,128)(2,1)S(1)}, u32[]{:S(2)}, u32[]{:S(2)}) collective-permute-start(bf16[256,1024]{0,1:T(8,128)(2,1)S(1)} %fusion.33), channel_id=1, source_target_pairs={{0,2},{1,3},{2,0},{3,1},{4,6},{5,7},{6,4},{7,5},{8,10},{9,11},{10,... | collective-permute-start | bytes 1572872 | tf_op jit(solution)/shard_map/ppermute | solution.py:15
  90.5 9.1 %collective-permute-done.9 = bf16[256,1024]{0,1:T(8,128)(2,1)S(1)} collective-permute-done((bf16[256,1024]{0,1:T(8,128)(2,1)S(1)}, bf16[256,1024]{0,1:T(8,128)(2,1)S(1)}, u32[]{:S(2)}, u32[]{:S(2)}) %collective-permute-start.9) | collective-permute-done | bytes 524320 | tf_op jit(solution)/shard_map/ppermute | solution.py:15
  99.5 12.1 %collective-permute-done.11 = bf16[256,1024]{0,1:T(8,128)(2,1)S(1)} collective-permute-done((bf16[256,1024]{0,1:T(8,128)(2,1)S(1)}, bf16[256,1024]{0,1:T(8,128)(2,1)S(1)}, u32[]{:S(2)}, u32[]{:S(2)}) %collective-permute-start.11) | collective-permute-done | bytes 524320 | tf_op jit(solution)/shard_map/ppermute | solution.py:15
  112.0 1.0 copy.14
  113.0 2.0 %reshape.81 = bf16[64,4,1024]{2,1,0:T(4,128)(2,1)} reshape(bf16[256,1024]{1,0:T(8,128)(2,1)} %copy.14) | data formatting | bytes 1048576 | tf_op jit(solution)/shard_map/reshape | solution.py:143
  115.0 6.9 %all-to-all-start.1 = ((bf16[64,4,1024]{2,1,0:T(4,128)(2,1)}), bf16[64,4,1024]{2,1,0:T(4,128)(2,1)S(1)}, u32[]{:S(2)}, u32[]{:S(2)}) async-start(bf16[64,4,1024]{2,1,0:T(4,128)(2,1)} %reshape.81), calls=%async_computation.1 | async-start | bytes 1048576 | tf_op jit(solution)/shard_map/all_to_all | solution.py:144
  122.0 1.5 %broadcast_in_dim.43.clone = bf16[1,2048,512]{2,1,0:T(8,128)(2,1)} broadcast(bf16[]{:T(256)} %constant.102.clone.1), dimensions={} | broadcast | bytes 2097154 | tf_op jit(solution)/shard_map/broadcast_in_dim | solution.py:125
  123.5 1.3 fusion.4
  124.8 1.3 fusion.6
  126.1 1.3 fusion.8
  127.4 1.3 fusion.10
  128.7 10.6 %all-to-all-done.1 = bf16[64,4,1024]{2,1,0:T(4,128)(2,1)S(1)} async-done(((bf16[64,4,1024]{2,1,0:T(4,128)(2,1)}), bf16[64,4,1024]{2,1,0:T(4,128)(2,1)S(1)}, u32[]{:S(2)}, u32[]{:S(2)}) %all-to-all-start.1) | async-done | bytes 524320 | tf_op jit(solution)/shard_map/all_to_all | solution.py:144
  (100 shorter events, 25.7 us)
Async XLA Ops:
  0.6 66.1 %copy-start = (bf16[1,2048,512]{2,1,0:T(8,128)(2,1)S(1)}, bf16[1,2048,512]{2,1,0:T(8,128)(2,1)}, u32[]{:S(2)}) copy-start(bf16[1,2048,512]{2,1,0:T(8,128)(2,1)} %param.14) | copy-start | bytes 6291460
  37.0 14.5 %collective-permute-start.1 = (bf16[256,1024]{1,0:T(8,128)(2,1)S(1)}, bf16[256,1024]{1,0:T(8,128)(2,1)S(1)}, u32[]{:S(2)}, u32[]{:S(2)}) collective-permute-start(bf16[256,1024]{1,0:T(8,128)(2,1)S(1)} %reshape.80), channel_id=1, source_target_pairs={{0,1},{1,2},{2,3},{3,0},{4,5},{5,6},{6,7},{7,4},{8,9},{9,10},{10,1... | collective-permute-start | bytes 1572872 | tf_op jit(solution)/shard_map/ppermute | solution.py:15
  38.3 14.5 %collective-permute-start.5 = (bf16[256,1024]{1,0:T(8,128)(2,1)S(1)}, bf16[256,1024]{1,0:T(8,128)(2,1)}, u32[]{:S(2)}, u32[]{:S(2)}) collective-permute-start(bf16[256,1024]{1,0:T(8,128)(2,1)S(1)} %reshape.80), channel_id=1, source_target_pairs={{0,3},{1,0},{2,1},{3,2},{4,7},{5,4},{6,5},{7,6},{8,11},{9,8},{10,9... | collective-permute-start | bytes 1572872 | tf_op jit(solution)/shard_map/ppermute | solution.py:15
  39.7 24.5 %collective-permute-start = (bf16[256,1024]{1,0:T(8,128)(2,1)S(1)}, bf16[256,1024]{1,0:T(8,128)(2,1)}, u32[]{:S(2)}, u32[]{:S(2)}) collective-permute-start(bf16[256,1024]{1,0:T(8,128)(2,1)S(1)} %reshape.80), channel_id=1, source_target_pairs={{0,4},{4,0},{8,12},{12,8},{16,20},{20,16},{24,28},{28,24},{32,36},... | collective-permute-start | bytes 1572872 | tf_op jit(solution)/shard_map/ppermute | solution.py:10
  40.6 24.8 %copy-start.2 = (bf16[1,512,2048]{2,1,0:T(8,128)(2,1)S(1)}, bf16[1,512,2048]{2,1,0:T(8,128)(2,1)}, u32[]{:S(2)}) copy-start(bf16[1,512,2048]{2,1,0:T(8,128)(2,1)} %param.15) | copy-start | bytes 6291460
  40.6 25.4 %collective-permute-start.3 = (bf16[256,1024]{1,0:T(8,128)(2,1)S(1)}, bf16[256,1024]{1,0:T(8,128)(2,1)S(1)}, u32[]{:S(2)}, u32[]{:S(2)}) collective-permute-start(bf16[256,1024]{1,0:T(8,128)(2,1)S(1)} %reshape.80), channel_id=1, source_target_pairs={{0,2},{1,3},{2,0},{3,1},{4,6},{5,7},{6,4},{7,5},{8,10},{9,11},{10,... | collective-permute-start | bytes 1572872 | tf_op jit(solution)/shard_map/ppermute | solution.py:15
  51.5 16.7 %collective-permute-start.2 = (bf16[256,1024]{1,0:T(8,128)(2,1)S(1)}, bf16[256,1024]{1,0:T(8,128)(2,1)S(1)}, u32[]{:S(2)}, u32[]{:S(2)}) collective-permute-start(bf16[256,1024]{1,0:T(8,128)(2,1)S(1)} %collective-permute-done.1), channel_id=1, source_target_pairs={{0,4},{4,0},{8,12},{12,8},{16,20},{20,16},{24,28},{28,24},{32,36},... | collective-permute-start | bytes 1572872 | tf_op jit(solution)/shard_map/ppermute | solution.py:10
  52.8 14.5 %collective-permute-start.6 = (bf16[256,1024]{1,0:T(8,128)(2,1)}, bf16[256,1024]{1,0:T(8,128)(2,1)S(1)}, u32[]{:S(2)}, u32[]{:S(2)}) collective-permute-start(bf16[256,1024]{1,0:T(8,128)(2,1)} %collective-permute-done.5), channel_id=1, source_target_pairs={{0,4},{4,0},{8,12},{12,8},{16,20},{20,16},{24,28},{28,24},{32,36},... | collective-permute-start | bytes 1572872 | tf_op jit(solution)/shard_map/ppermute | solution.py:10
  65.5 16.7 %copy-start.5 = (bf16[512,1024]{1,0:T(8,128)(2,1)}, bf16[512,1024]{1,0:T(8,128)(2,1)S(1)}, u32[]{:S(2)}) copy-start(bf16[512,1024]{1,0:T(8,128)(2,1)S(1)} %constant_dynamic-update-slice_fusion) | copy-start | bytes 3145732
  66.0 4.1 %collective-permute-start.4 = (bf16[256,1024]{1,0:T(8,128)(2,1)S(1)}, bf16[256,1024]{1,0:T(8,128)(2,1)S(1)}, u32[]{:S(2)}, u32[]{:S(2)}) collective-permute-start(bf16[256,1024]{1,0:T(8,128)(2,1)S(1)} %collective-permute-done.3), channel_id=1, source_target_pairs={{0,4},{4,0},{8,12},{12,8},{16,20},{20,16},{24,28},{28,24},{32,36},... | collective-permute-start | bytes 1572872 | tf_op jit(solution)/shard_map/ppermute | solution.py:10
  67.3 22.7 %copy-start.3 = (bf16[512,1024]{1,0:T(8,128)(2,1)}, bf16[512,1024]{1,0:T(8,128)(2,1)S(1)}, u32[]{:S(2)}) copy-start(bf16[512,1024]{1,0:T(8,128)(2,1)S(1)} %constant_dynamic-update-slice_fusion.6) | copy-start | bytes 3145732
  68.3 14.4 %copy-start.7 = (bf16[512,1024]{1,0:T(8,128)(2,1)}, bf16[512,1024]{1,0:T(8,128)(2,1)S(1)}, u32[]{:S(2)}) copy-start(bf16[512,1024]{1,0:T(8,128)(2,1)S(1)} %constant_dynamic-update-slice_fusion.2) | copy-start | bytes 3145732
  70.2 19.3 %copy-start.9 = (bf16[512,1024]{1,0:T(8,128)(2,1)}, bf16[512,1024]{1,0:T(8,128)(2,1)S(1)}, u32[]{:S(2)}) copy-start(bf16[512,1024]{1,0:T(8,128)(2,1)S(1)} %constant_dynamic-update-slice_fusion.4) | copy-start | bytes 3145732
  77.7 6.1 %collective-permute-start.8 = (f32[256,1024]{0,1:T(8,128)S(1)}, f32[256,1024]{0,1:T(8,128)S(1)}, u32[]{:S(2)}, u32[]{:S(2)}) collective-permute-start(f32[256,1024]{0,1:T(8,128)S(1)} %pad_maximum_fusion.2), channel_id=1, source_target_pairs={{0,4},{4,0},{8,12},{12,8},{16,20},{20,16},{24,28},{28,24},{32,36},... | collective-permute-start | bytes 3145736 | tf_op jit(solution)/shard_map/ppermute | solution.py:10
  78.9 5.3 %collective-permute-start.10 = (f32[256,1024]{0,1:T(8,128)S(1)}, f32[256,1024]{0,1:T(8,128)S(1)}, u32[]{:S(2)}, u32[]{:S(2)}) collective-permute-start(f32[256,1024]{0,1:T(8,128)S(1)} %pad_maximum_fusion.1), channel_id=1, source_target_pairs={{0,4},{4,0},{8,12},{12,8},{16,20},{20,16},{24,28},{28,24},{32,36},... | collective-permute-start | bytes 3145736 | tf_op jit(solution)/shard_map/ppermute | solution.py:10
  79.6 9.5 %collective-permute-start.12 = (f32[256,1024]{0,1:T(8,128)S(1)}, f32[256,1024]{0,1:T(8,128)S(1)}, u32[]{:S(2)}, u32[]{:S(2)}) collective-permute-start(f32[256,1024]{0,1:T(8,128)S(1)} %pad_maximum_fusion), channel_id=1, source_target_pairs={{0,4},{4,0},{8,12},{12,8},{16,20},{20,16},{24,28},{28,24},{32,36},... | collective-permute-start | bytes 3145736 | tf_op jit(solution)/shard_map/ppermute | solution.py:10
  80.8 9.7 %collective-permute-start.7 = (f32[256,1024]{0,1:T(8,128)S(1)}, f32[256,1024]{0,1:T(8,128)S(1)}, u32[]{:S(2)}, u32[]{:S(2)}) collective-permute-start(f32[256,1024]{0,1:T(8,128)S(1)} %pad_maximum_fusion.3), channel_id=1, source_target_pairs={{0,4},{4,0},{8,12},{12,8},{16,20},{20,16},{24,28},{28,24},{32,36},... | collective-permute-start | bytes 3145736 | tf_op jit(solution)/shard_map/ppermute | solution.py:10
  84.1 15.5 %collective-permute-start.9 = (bf16[256,1024]{0,1:T(8,128)(2,1)S(1)}, bf16[256,1024]{0,1:T(8,128)(2,1)S(1)}, u32[]{:S(2)}, u32[]{:S(2)}) collective-permute-start(bf16[256,1024]{0,1:T(8,128)(2,1)S(1)} %fusion.36), channel_id=1, source_target_pairs={{0,1},{1,2},{2,3},{3,0},{4,5},{5,6},{6,7},{7,4},{8,9},{9,10},{10,1... | collective-permute-start | bytes 1572872 | tf_op jit(solution)/shard_map/ppermute | solution.py:15
  84.4 27.2 %collective-permute-start.11 = (bf16[256,1024]{0,1:T(8,128)(2,1)S(1)}, bf16[256,1024]{0,1:T(8,128)(2,1)S(1)}, u32[]{:S(2)}, u32[]{:S(2)}) collective-permute-start(bf16[256,1024]{0,1:T(8,128)(2,1)S(1)} %fusion.33), channel_id=1, source_target_pairs={{0,2},{1,3},{2,0},{3,1},{4,6},{5,7},{6,4},{7,5},{8,10},{9,11},{10,... | collective-permute-start | bytes 1572872 | tf_op jit(solution)/shard_map/ppermute | solution.py:15
  89.4 22.3 %collective-permute-start.13 = (bf16[256,1024]{0,1:T(8,128)(2,1)S(1)}, bf16[256,1024]{0,1:T(8,128)(2,1)S(1)}, u32[]{:S(2)}, u32[]{:S(2)}) collective-permute-start(bf16[256,1024]{0,1:T(8,128)(2,1)S(1)} %fusion.30), channel_id=1, source_target_pairs={{0,3},{1,0},{2,1},{3,2},{4,7},{5,4},{6,5},{7,6},{8,11},{9,8},{10,9... | collective-permute-start | bytes 1572872 | tf_op jit(solution)/shard_map/ppermute | solution.py:15
  90.4 21.2 %copy-start.12 = (bf16[1,2048,512]{2,1,0:T(8,128)(2,1)}, bf16[1,2048,512]{2,1,0:T(8,128)(2,1)S(1)}, u32[]{:S(2)}) copy-start(bf16[1,2048,512]{2,1,0:T(8,128)(2,1)S(1)} %fusion.18) | copy-start | bytes 6291460
  115.0 24.3 %all-to-all-start.1 = ((bf16[64,4,1024]{2,1,0:T(4,128)(2,1)}), bf16[64,4,1024]{2,1,0:T(4,128)(2,1)S(1)}, u32[]{:S(2)}, u32[]{:S(2)}) async-start(bf16[64,4,1024]{2,1,0:T(4,128)(2,1)} %reshape.81), calls=%async_computation.1 | async-start | bytes 1048576 | tf_op jit(solution)/shard_map/all_to_all | solution.py:144
  122.0 2.9 %copy-start.8 = (bf16[512,1024]{1,0:T(8,128)(2,1)S(1)}, bf16[512,1024]{1,0:T(8,128)(2,1)}, u32[]{:S(2)}) copy-start(bf16[512,1024]{1,0:T(8,128)(2,1)} %copy-done.7) | copy-start | bytes 3145732
  123.5 2.6 %copy-start.10 = (bf16[512,1024]{1,0:T(8,128)(2,1)S(1)}, bf16[512,1024]{1,0:T(8,128)(2,1)}, u32[]{:S(2)}) copy-start(bf16[512,1024]{1,0:T(8,128)(2,1)} %copy-done.9) | copy-start | bytes 3145732
  (4 other events, 7.6 us)

commit v7 on v6

--- a/solution.py
+++ b/solution.py
@@ -42,7 +42,7 @@
     )
     row_ids = jnp.arange(tok_rows, dtype=jnp.int32)
     earlier = (row_ids[None, :] < row_ids[:, None]).astype(jnp.float32)
-    before = jnp.dot(earlier, lab_hot, precision=lax.Precision.HIGHEST)
+    before = jnp.dot(earlier, lab_hot, preferred_element_type=jnp.float32)
     slot_pos = jnp.sum(before * lab_hot, axis=1).astype(jnp.int32)
     target_row = lang_label * capacity + slot_pos
     rows_out = n_expert * half_cap
@@ -55,13 +55,16 @@
     )
     outbound = outbound.reshape(n_expert, half_cap, 2 * feat_slice)
     arrived = lax.all_to_all(outbound, "expert", split_axis=0, concat_axis=0, tiled=True)
-    pieces = [arrived.reshape(rows_out, 2 * feat_slice)]
-    pieces += [shifted(pieces[0], "tensor", k) for k in range(1, n_tensor)]
+    own_piece = arrived.reshape(rows_out, 2 * feat_slice)
+    order = sorted(range(n_tensor), key=lambda k: -min(k, n_tensor - k))
+    received = {k: shifted(own_piece, "tensor", k) for k in order if k}
+    order = [0] + [k for k in reversed(order) if k]
+    pieces = [own_piece if k == 0 else received[k] for k in order]
     blocks = []
     for p in pieces:
         both = jnp.concatenate((p, partner(p, "expert", 0)), axis=0)
         blocks.append((both[:, :feat_slice], both[:, feat_slice:]))
-    src_off = [((t_idx - k) % n_tensor) * feat_slice for k in range(n_tensor)]
+    src_off = [((t_idx - k) % n_tensor) * feat_slice for k in order]
     w_gate = gate_weight[0]
     w_up = up_weight[0]
     w_down = down_weight[0]
@@ -126,7 +129,7 @@
     up_grad = up_grad[None]
     down_grad = down_grad[None]
     acc = None
-    for m in range(n_tensor):
+    for m in sorted(range(n_tensor), key=lambda k: -min(k, n_tensor - k)):
         off = ((t_idx + m) % n_tensor) * feat_slice
         out_m = jnp.dot(hidden, cols_of(w_down, off), preferred_element_type=jnp.float32)
         in_m = lax.dot_general(
@@ -136,10 +139,9 @@
         )
         part_m = jnp.concatenate((out_m, in_m), axis=1)
         core_m = part_m[:rows_out] + partner(part_m[rows_out:], "expert", 0)
-        if m == 0:
-            acc = core_m
-        else:
-            acc = acc + shifted(core_m.astype(jnp.bfloat16), "tensor", m).astype(jnp.float32)
+        if m:
+            core_m = shifted(core_m.astype(jnp.bfloat16), "tensor", m).astype(jnp.float32)
+        acc = core_m if acc is None else acc + core_m
     going_back = acc.astype(jnp.bfloat16).reshape(n_expert, half_cap, 2 * feat_slice)
     returned = lax.all_to_all(going_back, "expert", split_axis=0, concat_axis=0, tiled=True)
     flat_back = returned.reshape(rows_out, 2 * feat_slice)

time: 142 us -> 141 us (level)
  starting transfers between devices: 30.5 us -> 18.9 us
  waiting for transfers between devices: 41.1 us -> 52.5 us
    ppermute x6, waiting for transfers between devices: 30.4 us -> 41.8 us  [shifted(): lax.ppermute(value, axis, [(i, (i + step) % size) for i in range(size)])]
    ppermute x8, starting transfers between devices: 14.4 us -> 4.7 us  [partner(): lax.ppermute(value, axis, [(i, i ^ 1 << stride) for i in range(lax.axis_s...]
    ppermute x6, starting transfers between devices: 9.19 us -> 7.72 us  [shifted(): lax.ppermute(value, axis, [(i, (i + step) % size) for i in range(size)])]
  transfers between devices with their start and end apart: 15 -> 15, of which waited for: 4 -> 6; matrix products, arithmetic and copies ran while one was open for 13% -> 13% of each run, Pallas kernels for 0% -> 0%
where the time goes in v7:
time: 141 us
  waiting for transfers between devices  52.5 us (37%)
  blocking collectives  30.4 us (22%)
  matrix products  24.4 us (17%)
  starting transfers between devices  18.9 us (13%)
  local copies, waits for them, and re-layouts  9.69 us (7%)
  other arithmetic  3.83 us (3%)
    ppermute x6, waiting for transfers between devices, shifted(): lax.ppermute(value, axis, [(i, (i + step) % size) for i in range(size)])  41.8 us
    all_to_all x1, blocking collectives, body(): lax.all_to_all(outbound, 'expert', split_axis=0, concat_axis=0, tiled=True)  30.4 us
    all_to_all x1, waiting for transfers between devices, body(): lax.all_to_all(going_back, 'expert', split_axis=0, concat_axis=0, tiled=T...  10.6 us
    ppermute x6, starting transfers between devices, shifted(): lax.ppermute(value, axis, [(i, (i + step) % size) for i in range(size)])  7.72 us
    all_to_all x1, starting transfers between devices, body(): lax.all_to_all(going_back, 'expert', split_axis=0, concat_axis=0, tiled=T...  6.5 us
    dot_general x4, matrix products, body(): lax.dot_general(b[0], grad_gate_pre, contract_rows, preferred_element_typ...  5.12 us
    ppermute x8, starting transfers between devices, partner(): lax.ppermute(value, axis, [(i, i ^ 1 << stride) for i in range(lax.axis_s...  4.7 us
  transfers between devices with their start and end apart: 15, of which 6 were waited for; matrix products, arithmetic and copies ran while one was open for 13% of the time, Pallas kernels for 0%

profile of v7, /device:TPU:1, one launch (start us, length us, event | category | flops | bytes accessed | tf_op | source)
XLA Modules:
  0.0 140.9 jit_solution(17611266270631460700)
XLA Ops:
  0.6 1.0 fusion.27
  3.1 1.0 multiply_convert_fusion.3
  4.0 1.2 convolution_convert_fusion.12
  5.4 30.4 %all_to_all.10 = bf16[64,4,1024]{2,1,0:T(4,128)(2,1)} all-to-all(bf16[64,4,1024]{2,1,0:T(4,128)(2,1)S(1)} %reshape.79), channel_id=1, replica_groups=mesh['expert'=64,'tensor'=4] {'expert'}, dimensions={0} | all-to-all | bytes 1048576 | tf_op jit(solution)/shard_map/all_to_all | solution.py:57
  35.8 1.2 reshape.80
  37.0 2.6 %collective-permute-start.1 = (bf16[256,1024]{1,0:T(8,128)(2,1)S(1)}, bf16[256,1024]{1,0:T(8,128)(2,1)S(1)}, u32[]{:S(2)}, u32[]{:S(2)}) collective-permute-start(bf16[256,1024]{1,0:T(8,128)(2,1)S(1)} %reshape.80), channel_id=1, source_target_pairs={{0,3},{1,0},{2,1},{3,2},{4,7},{5,4},{6,5},{7,6},{8,11},{9,8},{10,9... | collective-permute-start | bytes 1572872 | tf_op jit(solution)/shard_map/ppermute | solution.py:15
  41.6 20.0 %collective-permute-done.1 = bf16[256,1024]{1,0:T(8,128)(2,1)S(1)} collective-permute-done((bf16[256,1024]{1,0:T(8,128)(2,1)S(1)}, bf16[256,1024]{1,0:T(8,128)(2,1)S(1)}, u32[]{:S(2)}, u32[]{:S(2)}) %collective-permute-start.1) | collective-permute-done | bytes 524320 | tf_op jit(solution)/shard_map/ppermute | solution.py:15
  61.7 1.4 collective-permute-start.2
  63.2 1.1 constant_dynamic-update-slice_fusion.7
  64.3 1.2 constant_dynamic-update-slice_fusion
  85.5 3.3 %collective-permute-start.10 = (bf16[256,1024]{0,1:T(8,128)(2,1)S(1)}, bf16[256,1024]{0,1:T(8,128)(2,1)S(1)}, u32[]{:S(2)}, u32[]{:S(2)}) collective-permute-start(bf16[256,1024]{0,1:T(8,128)(2,1)S(1)} %fusion.37), channel_id=1, source_target_pairs={{0,1},{1,2},{2,3},{3,0},{4,5},{5,6},{6,7},{7,4},{8,9},{9,10},{10,1... | collective-permute-start | bytes 1572872 | tf_op jit(solution)/shard_map/ppermute | solution.py:15
  90.2 9.6 %collective-permute-done.8 = bf16[256,1024]{0,1:T(8,128)(2,1)S(1)} collective-permute-done((bf16[256,1024]{0,1:T(8,128)(2,1)S(1)}, bf16[256,1024]{0,1:T(8,128)(2,1)S(1)}, u32[]{:S(2)}, u32[]{:S(2)}) %collective-permute-start.8) | collective-permute-done | bytes 524320 | tf_op jit(solution)/shard_map/ppermute | solution.py:15
  99.8 11.6 %collective-permute-done.10 = bf16[256,1024]{0,1:T(8,128)(2,1)S(1)} collective-permute-done((bf16[256,1024]{0,1:T(8,128)(2,1)S(1)}, bf16[256,1024]{0,1:T(8,128)(2,1)S(1)}, u32[]{:S(2)}, u32[]{:S(2)}) %collective-permute-start.10) | collective-permute-done | bytes 524320 | tf_op jit(solution)/shard_map/ppermute | solution.py:15
  112.2 1.0 copy.14
  113.2 2.0 %reshape.81 = bf16[64,4,1024]{2,1,0:T(4,128)(2,1)} reshape(bf16[256,1024]{1,0:T(8,128)(2,1)} %copy.14) | data formatting | bytes 1048576 | tf_op jit(solution)/shard_map/reshape | solution.py:145
  115.2 6.5 %all-to-all-start.1 = ((bf16[64,4,1024]{2,1,0:T(4,128)(2,1)}), bf16[64,4,1024]{2,1,0:T(4,128)(2,1)S(1)}, u32[]{:S(2)}, u32[]{:S(2)}) async-start(bf16[64,4,1024]{2,1,0:T(4,128)(2,1)} %reshape.81), calls=%async_computation.1 | async-start | bytes 1048576 | tf_op jit(solution)/shard_map/all_to_all | solution.py:146
  121.7 1.5 %broadcast_in_dim.43.clone = bf16[1,2048,512]{2,1,0:T(8,128)(2,1)} broadcast(bf16[]{:T(256)} %constant.102.clone.1), dimensions={} | broadcast | bytes 2097154 | tf_op jit(solution)/shard_map/broadcast_in_dim | solution.py:128
  123.3 1.3 fusion.4
  124.6 1.3 fusion.6
  125.9 1.3 fusion.8
  127.2 1.3 fusion.10
  128.4 10.6 %all-to-all-done.1 = bf16[64,4,1024]{2,1,0:T(4,128)(2,1)S(1)} async-done(((bf16[64,4,1024]{2,1,0:T(4,128)(2,1)}), bf16[64,4,1024]{2,1,0:T(4,128)(2,1)S(1)}, u32[]{:S(2)}, u32[]{:S(2)}) %all-to-all-start.1) | async-done | bytes 524320 | tf_op jit(solution)/shard_map/all_to_all | solution.py:146
  139.2 0.9 convolution_convert_fusion.13
  140.1 0.9 convolution_convert_fusion.14
  (100 shorter events, 25.8 us)
Async XLA Ops:
  0.6 66.8 %copy-start = (bf16[1,2048,512]{2,1,0:T(8,128)(2,1)S(1)}, bf16[1,2048,512]{2,1,0:T(8,128)(2,1)}, u32[]{:S(2)}) copy-start(bf16[1,2048,512]{2,1,0:T(8,128)(2,1)} %param.14) | copy-start | bytes 6291460
  37.0 24.6 %collective-permute-start.1 = (bf16[256,1024]{1,0:T(8,128)(2,1)S(1)}, bf16[256,1024]{1,0:T(8,128)(2,1)S(1)}, u32[]{:S(2)}, u32[]{:S(2)}) collective-permute-start(bf16[256,1024]{1,0:T(8,128)(2,1)S(1)} %reshape.80), channel_id=1, source_target_pairs={{0,3},{1,0},{2,1},{3,2},{4,7},{5,4},{6,5},{7,6},{8,11},{9,8},{10,9... | collective-permute-start | bytes 1572872 | tf_op jit(solution)/shard_map/ppermute | solution.py:15
  39.6 23.5 %collective-permute-start.5 = (bf16[256,1024]{1,0:T(8,128)(2,1)S(1)}, bf16[256,1024]{1,0:T(8,128)(2,1)}, u32[]{:S(2)}, u32[]{:S(2)}) collective-permute-start(bf16[256,1024]{1,0:T(8,128)(2,1)S(1)} %reshape.80), channel_id=1, source_target_pairs={{0,2},{1,3},{2,0},{3,1},{4,6},{5,7},{6,4},{7,5},{8,10},{9,11},{10,... | collective-permute-start | bytes 1572872 | tf_op jit(solution)/shard_map/ppermute | solution.py:15
  40.1 24.2 %collective-permute-start = (bf16[256,1024]{1,0:T(8,128)(2,1)S(1)}, bf16[256,1024]{1,0:T(8,128)(2,1)}, u32[]{:S(2)}, u32[]{:S(2)}) collective-permute-start(bf16[256,1024]{1,0:T(8,128)(2,1)S(1)} %reshape.80), channel_id=1, source_target_pairs={{0,4},{4,0},{8,12},{12,8},{16,20},{20,16},{24,28},{28,24},{32,36},... | collective-permute-start | bytes 1572872 | tf_op jit(solution)/shard_map/ppermute | solution.py:10
  41.0 24.6 %copy-start.2 = (bf16[1,512,2048]{2,1,0:T(8,128)(2,1)S(1)}, bf16[1,512,2048]{2,1,0:T(8,128)(2,1)}, u32[]{:S(2)}) copy-start(bf16[1,512,2048]{2,1,0:T(8,128)(2,1)} %param.15) | copy-start | bytes 6291460
  41.0 25.2 %collective-permute-start.3 = (bf16[256,1024]{1,0:T(8,128)(2,1)S(1)}, bf16[256,1024]{1,0:T(8,128)(2,1)S(1)}, u32[]{:S(2)}, u32[]{:S(2)}) collective-permute-start(bf16[256,1024]{1,0:T(8,128)(2,1)S(1)} %reshape.80), channel_id=1, source_target_pairs={{0,1},{1,2},{2,3},{3,0},{4,5},{5,6},{6,7},{7,4},{8,9},{9,10},{10,1... | collective-permute-start | bytes 1572872 | tf_op jit(solution)/shard_map/ppermute | solution.py:15
  61.7 7.2 %collective-permute-start.2 = (bf16[256,1024]{1,0:T(8,128)(2,1)S(1)}, bf16[256,1024]{1,0:T(8,128)(2,1)S(1)}, u32[]{:S(2)}, u32[]{:S(2)}) collective-permute-start(bf16[256,1024]{1,0:T(8,128)(2,1)S(1)} %collective-permute-done.1), channel_id=1, source_target_pairs={{0,4},{4,0},{8,12},{12,8},{16,20},{20,16},{24,28},{28,24},{32,36},... | collective-permute-start | bytes 1572872 | tf_op jit(solution)/shard_map/ppermute | solution.py:10
  63.1 4.8 %collective-permute-start.6 = (bf16[256,1024]{1,0:T(8,128)(2,1)}, bf16[256,1024]{1,0:T(8,128)(2,1)S(1)}, u32[]{:S(2)}, u32[]{:S(2)}) collective-permute-start(bf16[256,1024]{1,0:T(8,128)(2,1)} %collective-permute-done.5), channel_id=1, source_target_pairs={{0,4},{4,0},{8,12},{12,8},{16,20},{20,16},{24,28},{28,24},{32,36},... | collective-permute-start | bytes 1572872 | tf_op jit(solution)/shard_map/ppermute | solution.py:10
  64.3 2.7 %copy-start.1 = (bf16[1,2048,512]{2,1,0:T(8,128)(2,1)S(1)}, bf16[1,2048,512]{2,1,0:T(8,128)(2,1)}, u32[]{:S(2)}) copy-start(bf16[1,2048,512]{2,1,0:T(8,128)(2,1)} %param.13) | copy-start | bytes 6291460
  65.5 17.3 %copy-start.5 = (bf16[512,1024]{1,0:T(8,128)(2,1)}, bf16[512,1024]{1,0:T(8,128)(2,1)S(1)}, u32[]{:S(2)}) copy-start(bf16[512,1024]{1,0:T(8,128)(2,1)S(1)} %constant_dynamic-update-slice_fusion) | copy-start | bytes 3145732
  66.2 4.5 %collective-permute-start.4 = (bf16[256,1024]{1,0:T(8,128)(2,1)S(1)}, bf16[256,1024]{1,0:T(8,128)(2,1)S(1)}, u32[]{:S(2)}, u32[]{:S(2)}) collective-permute-start(bf16[256,1024]{1,0:T(8,128)(2,1)S(1)} %collective-permute-done.3), channel_id=1, source_target_pairs={{0,4},{4,0},{8,12},{12,8},{16,20},{20,16},{24,28},{28,24},{32,36},... | collective-permute-start | bytes 1572872 | tf_op jit(solution)/shard_map/ppermute | solution.py:10
  67.9 21.8 %copy-start.3 = (bf16[512,1024]{1,0:T(8,128)(2,1)}, bf16[512,1024]{1,0:T(8,128)(2,1)S(1)}, u32[]{:S(2)}) copy-start(bf16[512,1024]{1,0:T(8,128)(2,1)S(1)} %constant_dynamic-update-slice_fusion.6) | copy-start | bytes 3145732
  68.9 14.4 %copy-start.7 = (bf16[512,1024]{1,0:T(8,128)(2,1)}, bf16[512,1024]{1,0:T(8,128)(2,1)S(1)}, u32[]{:S(2)}) copy-start(bf16[512,1024]{1,0:T(8,128)(2,1)S(1)} %constant_dynamic-update-slice_fusion.2) | copy-start | bytes 3145732
  70.8 18.4 %copy-start.9 = (bf16[512,1024]{1,0:T(8,128)(2,1)}, bf16[512,1024]{1,0:T(8,128)(2,1)S(1)}, u32[]{:S(2)}) copy-start(bf16[512,1024]{1,0:T(8,128)(2,1)S(1)} %constant_dynamic-update-slice_fusion.4) | copy-start | bytes 3145732
  78.3 6.1 %collective-permute-start.7 = (f32[256,1024]{0,1:T(8,128)S(1)}, f32[256,1024]{0,1:T(8,128)S(1)}, u32[]{:S(2)}, u32[]{:S(2)}) collective-permute-start(f32[256,1024]{0,1:T(8,128)S(1)} %pad_maximum_fusion.3), channel_id=1, source_target_pairs={{0,4},{4,0},{8,12},{12,8},{16,20},{20,16},{24,28},{28,24},{32,36},... | collective-permute-start | bytes 3145736 | tf_op jit(solution)/shard_map/ppermute | solution.py:10
  79.1 6.2 %collective-permute-start.9 = (f32[256,1024]{0,1:T(8,128)S(1)}, f32[256,1024]{0,1:T(8,128)S(1)}, u32[]{:S(2)}, u32[]{:S(2)}) collective-permute-start(f32[256,1024]{0,1:T(8,128)S(1)} %pad_maximum_fusion.2), channel_id=1, source_target_pairs={{0,4},{4,0},{8,12},{12,8},{16,20},{20,16},{24,28},{28,24},{32,36},... | collective-permute-start | bytes 3145736 | tf_op jit(solution)/shard_map/ppermute | solution.py:10
  80.2 8.7 %collective-permute-start.11 = (f32[256,1024]{0,1:T(8,128)S(1)}, f32[256,1024]{0,1:T(8,128)S(1)}, u32[]{:S(2)}, u32[]{:S(2)}) collective-permute-start(f32[256,1024]{0,1:T(8,128)S(1)} %pad_maximum_fusion.1), channel_id=1, source_target_pairs={{0,4},{4,0},{8,12},{12,8},{16,20},{20,16},{24,28},{28,24},{32,36},... | collective-permute-start | bytes 3145736 | tf_op jit(solution)/shard_map/ppermute | solution.py:10
  81.0 9.2 %collective-permute-start.13 = (f32[256,1024]{0,1:T(8,128)S(1)}, f32[256,1024]{0,1:T(8,128)S(1)}, u32[]{:S(2)}, u32[]{:S(2)}) collective-permute-start(f32[256,1024]{0,1:T(8,128)S(1)} %pad_maximum_fusion), channel_id=1, source_target_pairs={{0,4},{4,0},{8,12},{12,8},{16,20},{20,16},{24,28},{28,24},{32,36},... | collective-permute-start | bytes 3145736 | tf_op jit(solution)/shard_map/ppermute | solution.py:10
  84.7 15.1 %collective-permute-start.8 = (bf16[256,1024]{0,1:T(8,128)(2,1)S(1)}, bf16[256,1024]{0,1:T(8,128)(2,1)S(1)}, u32[]{:S(2)}, u32[]{:S(2)}) collective-permute-start(bf16[256,1024]{0,1:T(8,128)(2,1)S(1)} %fusion.40), channel_id=1, source_target_pairs={{0,2},{1,3},{2,0},{3,1},{4,6},{5,7},{6,4},{7,5},{8,10},{9,11},{10,... | collective-permute-start | bytes 1572872 | tf_op jit(solution)/shard_map/ppermute | solution.py:15
  85.5 25.8 %collective-permute-start.10 = (bf16[256,1024]{0,1:T(8,128)(2,1)S(1)}, bf16[256,1024]{0,1:T(8,128)(2,1)S(1)}, u32[]{:S(2)}, u32[]{:S(2)}) collective-permute-start(bf16[256,1024]{0,1:T(8,128)(2,1)S(1)} %fusion.37), channel_id=1, source_target_pairs={{0,1},{1,2},{2,3},{3,0},{4,5},{5,6},{6,7},{7,4},{8,9},{9,10},{10,1... | collective-permute-start | bytes 1572872 | tf_op jit(solution)/shard_map/ppermute | solution.py:15
  89.1 22.7 %collective-permute-start.12 = (bf16[256,1024]{0,1:T(8,128)(2,1)S(1)}, bf16[256,1024]{0,1:T(8,128)(2,1)S(1)}, u32[]{:S(2)}, u32[]{:S(2)}) collective-permute-start(bf16[256,1024]{0,1:T(8,128)(2,1)S(1)} %fusion.34), channel_id=1, source_target_pairs={{0,3},{1,0},{2,1},{3,2},{4,7},{5,4},{6,5},{7,6},{8,11},{9,8},{10,9... | collective-permute-start | bytes 1572872 | tf_op jit(solution)/shard_map/ppermute | solution.py:15
  90.2 21.2 %copy-start.12 = (bf16[1,2048,512]{2,1,0:T(8,128)(2,1)}, bf16[1,2048,512]{2,1,0:T(8,128)(2,1)S(1)}, u32[]{:S(2)}) copy-start(bf16[1,2048,512]{2,1,0:T(8,128)(2,1)S(1)} %fusion.18) | copy-start | bytes 6291460
  115.2 23.8 %all-to-all-start.1 = ((bf16[64,4,1024]{2,1,0:T(4,128)(2,1)}), bf16[64,4,1024]{2,1,0:T(4,128)(2,1)S(1)}, u32[]{:S(2)}, u32[]{:S(2)}) async-start(bf16[64,4,1024]{2,1,0:T(4,128)(2,1)} %reshape.81), calls=%async_computation.1 | async-start | bytes 1048576 | tf_op jit(solution)/shard_map/all_to_all | solution.py:146
  121.7 2.9 %copy-start.8 = (bf16[512,1024]{1,0:T(8,128)(2,1)S(1)}, bf16[512,1024]{1,0:T(8,128)(2,1)}, u32[]{:S(2)}) copy-start(bf16[512,1024]{1,0:T(8,128)(2,1)} %copy-done.7) | copy-start | bytes 3145732
  (4 other events, 8.0 us)

commit v8 on v7

--- a/solution.py
+++ b/solution.py
@@ -37,13 +37,9 @@
     ).astype(jnp.float32)
     tok_scale = jnp.sum(dom_hot * domain_weights[None, :], axis=1)
     grad_rows = (tok_scale[:, None] * cotangent.astype(jnp.float32)).astype(jnp.bfloat16)
-    lab_hot = (lang_label[:, None] == jnp.arange(experts_all, dtype=jnp.int32)[None, :]).astype(
-        jnp.float32
-    )
     row_ids = jnp.arange(tok_rows, dtype=jnp.int32)
-    earlier = (row_ids[None, :] < row_ids[:, None]).astype(jnp.float32)
-    before = jnp.dot(earlier, lab_hot, preferred_element_type=jnp.float32)
-    slot_pos = jnp.sum(before * lab_hot, axis=1).astype(jnp.int32)
+    same_before = (lang_label[None, :] == lang_label[:, None]) & (row_ids[None, :] < row_ids[:, None])
+    slot_pos = jnp.sum(same_before.astype(jnp.int32), axis=1)
     target_row = lang_label * capacity + slot_pos
     rows_out = n_expert * half_cap
     sources = jnp.concatenate((tokens, grad_rows), axis=1)
@@ -138,7 +134,8 @@
             grad_up_pre, rows_of(w_up, off), contract_cols, preferred_element_type=jnp.float32
         )
         part_m = jnp.concatenate((out_m, in_m), axis=1)
-        core_m = part_m[:rows_out] + partner(part_m[rows_out:], "expert", 0)
+        handed = partner(part_m[rows_out:].astype(jnp.bfloat16), "expert", 0)
+        core_m = part_m[:rows_out] + handed.astype(jnp.float32)
         if m:
             core_m = shifted(core_m.astype(jnp.bfloat16), "tensor", m).astype(jnp.float32)
         acc = core_m if acc is None else acc + core_m

time: 141 us -> 142 us (level)
  starting transfers between devices: 18.9 us -> 21.2 us
    dot_general x4, matrix products: 5.12 us -> 1.89 us  [body(): lax.dot_general(b[0], grad_gate_pre, contract_rows, preferred_element_typ...]
    dot_general x4, matrix products: 1.85 us -> 5.05 us  [body(): lax.dot_general(hidden, b[1], contract_rows, preferred_element_type=jnp.f...]
  transfers between devices with their start and end apart: 15 -> 15, of which waited for: 6 -> 5; matrix products, arithmetic and copies ran while one was open for 13% -> 14% of each run, Pallas kernels for 0% -> 0%
where the time goes in v8:
time: 142 us
  waiting for transfers between devices  51.2 us (36%)
  blocking collectives  30.4 us (21%)
  matrix products  23.5 us (17%)
  starting transfers between devices  21.2 us (15%)
  local copies, waits for them, and re-layouts  9.6 us (7%)
  other arithmetic  4.57 us (3%)
    ppermute x6, waiting for transfers between devices, shifted(): lax.ppermute(value, axis, [(i, (i + step) % size) for i in range(size)])  40.5 us
    all_to_all x1, blocking collectives, body(): lax.all_to_all(outbound, 'expert', split_axis=0, concat_axis=0, tiled=True)  30.4 us
    all_to_all x1, waiting for transfers between devices, body(): lax.all_to_all(going_back, 'expert', split_axis=0, concat_axis=0, tiled=T...  10.7 us
    ppermute x6, starting transfers between devices, shifted(): lax.ppermute(value, axis, [(i, (i + step) % size) for i in range(size)])  8.08 us
    all_to_all x1, starting transfers between devices, body(): lax.all_to_all(going_back, 'expert', split_axis=0, concat_axis=0, tiled=T...  7.26 us
    ppermute x8, starting transfers between devices, partner(): lax.ppermute(value, axis, [(i, i ^ 1 << stride) for i in range(lax.axis_s...  5.87 us
    dot_general x4, matrix products, body(): lax.dot_general(hidden, b[1], contract_rows, preferred_element_type=jnp.f...  5.05 us
  transfers between devices with their start and end apart: 15, of which 5 were waited for; matrix products, arithmetic and copies ran while one was open for 14% of the time, Pallas kernels for 0%

profile of v8, /device:TPU:1, one launch (start us, length us, event | category | flops | bytes accessed | tf_op | source)
XLA Modules:
  0.0 141.7 jit_solution(16140040025604793126)
XLA Ops:
  0.6 1.0 convert_reduce_fusion
  4.1 1.2 convolution_convert_fusion.12
  5.5 30.4 %all_to_all.10 = bf16[64,4,1024]{2,1,0:T(4,128)(2,1)} all-to-all(bf16[64,4,1024]{2,1,0:T(4,128)(2,1)S(1)} %reshape.79), channel_id=1, replica_groups=mesh['expert'=64,'tensor'=4] {'expert'}, dimensions={0} | all-to-all | bytes 1048576 | tf_op jit(solution)/shard_map/all_to_all | solution.py:53
  35.8 1.2 reshape.80
  37.0 2.8 %collective-permute-start.5 = (bf16[256,1024]{1,0:T(8,128)(2,1)S(1)}, bf16[256,1024]{1,0:T(8,128)(2,1)}, u32[]{:S(2)}, u32[]{:S(2)}) collective-permute-start(bf16[256,1024]{1,0:T(8,128)(2,1)S(1)} %reshape.80), channel_id=1, source_target_pairs={{0,2},{1,3},{2,0},{3,1},{4,6},{5,7},{6,4},{7,5},{8,10},{9,11},{10,... | collective-permute-start | bytes 1572872 | tf_op jit(solution)/shard_map/ppermute | solution.py:15
  42.2 9.7 %collective-permute-done.5 = bf16[256,1024]{1,0:T(8,128)(2,1)} collective-permute-done((bf16[256,1024]{1,0:T(8,128)(2,1)S(1)}, bf16[256,1024]{1,0:T(8,128)(2,1)}, u32[]{:S(2)}, u32[]{:S(2)}) %collective-permute-start.5) | collective-permute-done | bytes 524320 | tf_op jit(solution)/shard_map/ppermute | solution.py:15
  51.9 1.1 constant_dynamic-update-slice_fusion.7
  53.0 2.0 %collective-permute-start.6 = (bf16[256,1024]{1,0:T(8,128)(2,1)}, bf16[256,1024]{1,0:T(8,128)(2,1)S(1)}, u32[]{:S(2)}, u32[]{:S(2)}) collective-permute-start(bf16[256,1024]{1,0:T(8,128)(2,1)} %collective-permute-done.5), channel_id=1, source_target_pairs={{0,4},{4,0},{8,12},{12,8},{16,20},{20,16},{24,28},{28,24},{32,36},... | collective-permute-start | bytes 1572872 | tf_op jit(solution)/shard_map/ppermute | solution.py:10
  55.0 8.2 %collective-permute-done.1 = bf16[256,1024]{1,0:T(8,128)(2,1)S(1)} collective-permute-done((bf16[256,1024]{1,0:T(8,128)(2,1)S(1)}, bf16[256,1024]{1,0:T(8,128)(2,1)S(1)}, u32[]{:S(2)}, u32[]{:S(2)}) %collective-permute-start.1) | collective-permute-done | bytes 524320 | tf_op jit(solution)/shard_map/ppermute | solution.py:15
  63.2 1.1 collective-permute-start.2
  64.4 1.2 constant_dynamic-update-slice_fusion
  84.0 2.4 %collective-permute-start.12 = (bf16[256,1024]{0,1:T(8,128)(2,1)S(1)}, bf16[256,1024]{0,1:T(8,128)(2,1)S(1)}, u32[]{:S(2)}, u32[]{:S(2)}) collective-permute-start(bf16[256,1024]{0,1:T(8,128)(2,1)S(1)} %fusion.33), channel_id=1, source_target_pairs={{0,3},{1,0},{2,1},{3,2},{4,7},{5,4},{6,5},{7,6},{8,11},{9,8},{10,9... | collective-permute-start | bytes 1572872 | tf_op jit(solution)/shard_map/ppermute | solution.py:15
  86.9 1.3 collective-permute-start.8
  89.2 8.7 %collective-permute-done.12 = bf16[256,1024]{0,1:T(8,128)(2,1)S(1)} collective-permute-done((bf16[256,1024]{0,1:T(8,128)(2,1)S(1)}, bf16[256,1024]{0,1:T(8,128)(2,1)S(1)}, u32[]{:S(2)}, u32[]{:S(2)}) %collective-permute-start.12) | collective-permute-done | bytes 524320 | tf_op jit(solution)/shard_map/ppermute | solution.py:15
  97.9 13.9 %collective-permute-done.10 = bf16[256,1024]{0,1:T(8,128)(2,1)S(1)} collective-permute-done((bf16[256,1024]{0,1:T(8,128)(2,1)S(1)}, bf16[256,1024]{0,1:T(8,128)(2,1)S(1)}, u32[]{:S(2)}, u32[]{:S(2)}) %collective-permute-start.10) | collective-permute-done | bytes 524320 | tf_op jit(solution)/shard_map/ppermute | solution.py:15
  112.1 1.0 copy.14
  113.2 2.0 %reshape.81 = bf16[64,4,1024]{2,1,0:T(4,128)(2,1)} reshape(bf16[256,1024]{1,0:T(8,128)(2,1)} %copy.14) | data formatting | bytes 1048576 | tf_op jit(solution)/shard_map/reshape | solution.py:142
  115.2 7.3 %all-to-all-start.1 = ((bf16[64,4,1024]{2,1,0:T(4,128)(2,1)}), bf16[64,4,1024]{2,1,0:T(4,128)(2,1)S(1)}, u32[]{:S(2)}, u32[]{:S(2)}) async-start(bf16[64,4,1024]{2,1,0:T(4,128)(2,1)} %reshape.81), calls=%async_computation.1 | async-start | bytes 1048576 | tf_op jit(solution)/shard_map/all_to_all | solution.py:143
  122.5 1.6 %broadcast_in_dim.51 = bf16[1,512,2048]{2,1,0:T(8,128)(2,1)} broadcast(bf16[]{:T(256)} %constant.101.clone.1), dimensions={} | broadcast | bytes 2097154 | tf_op jit(solution)/shard_map/broadcast_in_dim | solution.py:126
  124.1 1.3 fusion.20
  125.3 1.3 fusion.22
  126.6 1.3 fusion.24
  127.9 1.3 fusion.26
  129.1 10.7 %all-to-all-done.1 = bf16[64,4,1024]{2,1,0:T(4,128)(2,1)S(1)} async-done(((bf16[64,4,1024]{2,1,0:T(4,128)(2,1)}), bf16[64,4,1024]{2,1,0:T(4,128)(2,1)S(1)}, u32[]{:S(2)}, u32[]{:S(2)}) %all-to-all-start.1) | async-done | bytes 524320 | tf_op jit(solution)/shard_map/all_to_all | solution.py:143
  (100 shorter events, 26.7 us)
Async XLA Ops:
  0.6 66.2 %copy-start = (bf16[1,512,2048]{2,1,0:T(8,128)(2,1)S(1)}, bf16[1,512,2048]{2,1,0:T(8,128)(2,1)}, u32[]{:S(2)}) copy-start(bf16[1,512,2048]{2,1,0:T(8,128)(2,1)} %param.15) | copy-start | bytes 6291460
  37.0 14.9 %collective-permute-start.5 = (bf16[256,1024]{1,0:T(8,128)(2,1)S(1)}, bf16[256,1024]{1,0:T(8,128)(2,1)}, u32[]{:S(2)}, u32[]{:S(2)}) collective-permute-start(bf16[256,1024]{1,0:T(8,128)(2,1)S(1)} %reshape.80), channel_id=1, source_target_pairs={{0,2},{1,3},{2,0},{3,1},{4,6},{5,7},{6,4},{7,5},{8,10},{9,11},{10,... | collective-permute-start | bytes 1572872 | tf_op jit(solution)/shard_map/ppermute | solution.py:15
  39.8 23.3 %collective-permute-start.1 = (bf16[256,1024]{1,0:T(8,128)(2,1)S(1)}, bf16[256,1024]{1,0:T(8,128)(2,1)S(1)}, u32[]{:S(2)}, u32[]{:S(2)}) collective-permute-start(bf16[256,1024]{1,0:T(8,128)(2,1)S(1)} %reshape.80), channel_id=1, source_target_pairs={{0,3},{1,0},{2,1},{3,2},{4,7},{5,4},{6,5},{7,6},{8,11},{9,8},{10,9... | collective-permute-start | bytes 1572872 | tf_op jit(solution)/shard_map/ppermute | solution.py:15
  40.7 23.7 %collective-permute-start = (bf16[256,1024]{1,0:T(8,128)(2,1)S(1)}, bf16[256,1024]{1,0:T(8,128)(2,1)}, u32[]{:S(2)}, u32[]{:S(2)}) collective-permute-start(bf16[256,1024]{1,0:T(8,128)(2,1)S(1)} %reshape.80), channel_id=1, source_target_pairs={{0,4},{4,0},{8,12},{12,8},{16,20},{20,16},{24,28},{28,24},{32,36},... | collective-permute-start | bytes 1572872 | tf_op jit(solution)/shard_map/ppermute | solution.py:10
  41.6 24.0 %copy-start.1 = (bf16[1,2048,512]{2,1,0:T(8,128)(2,1)S(1)}, bf16[1,2048,512]{2,1,0:T(8,128)(2,1)}, u32[]{:S(2)}) copy-start(bf16[1,2048,512]{2,1,0:T(8,128)(2,1)} %param.13) | copy-start | bytes 6291460
  41.6 24.5 %collective-permute-start.3 = (bf16[256,1024]{1,0:T(8,128)(2,1)S(1)}, bf16[256,1024]{1,0:T(8,128)(2,1)S(1)}, u32[]{:S(2)}, u32[]{:S(2)}) collective-permute-start(bf16[256,1024]{1,0:T(8,128)(2,1)S(1)} %reshape.80), channel_id=1, source_target_pairs={{0,1},{1,2},{2,3},{3,0},{4,5},{5,6},{6,7},{7,4},{8,9},{9,10},{10,1... | collective-permute-start | bytes 1572872 | tf_op jit(solution)/shard_map/ppermute | solution.py:15
  53.0 14.3 %collective-permute-start.6 = (bf16[256,1024]{1,0:T(8,128)(2,1)}, bf16[256,1024]{1,0:T(8,128)(2,1)S(1)}, u32[]{:S(2)}, u32[]{:S(2)}) collective-permute-start(bf16[256,1024]{1,0:T(8,128)(2,1)} %collective-permute-done.5), channel_id=1, source_target_pairs={{0,4},{4,0},{8,12},{12,8},{16,20},{20,16},{24,28},{28,24},{32,36},... | collective-permute-start | bytes 1572872 | tf_op jit(solution)/shard_map/ppermute | solution.py:10
  63.2 5.2 %collective-permute-start.2 = (bf16[256,1024]{1,0:T(8,128)(2,1)S(1)}, bf16[256,1024]{1,0:T(8,128)(2,1)S(1)}, u32[]{:S(2)}, u32[]{:S(2)}) collective-permute-start(bf16[256,1024]{1,0:T(8,128)(2,1)S(1)} %collective-permute-done.1), channel_id=1, source_target_pairs={{0,4},{4,0},{8,12},{12,8},{16,20},{20,16},{24,28},{28,24},{32,36},... | collective-permute-start | bytes 1572872 | tf_op jit(solution)/shard_map/ppermute | solution.py:10
  65.6 16.5 %copy-start.5 = (bf16[512,1024]{1,0:T(8,128)(2,1)}, bf16[512,1024]{1,0:T(8,128)(2,1)S(1)}, u32[]{:S(2)}) copy-start(bf16[512,1024]{1,0:T(8,128)(2,1)S(1)} %constant_dynamic-update-slice_fusion) | copy-start | bytes 3145732
  66.1 4.2 %collective-permute-start.4 = (bf16[256,1024]{1,0:T(8,128)(2,1)S(1)}, bf16[256,1024]{1,0:T(8,128)(2,1)S(1)}, u32[]{:S(2)}, u32[]{:S(2)}) collective-permute-start(bf16[256,1024]{1,0:T(8,128)(2,1)S(1)} %collective-permute-done.3), channel_id=1, source_target_pairs={{0,4},{4,0},{8,12},{12,8},{16,20},{20,16},{24,28},{28,24},{32,36},... | collective-permute-start | bytes 1572872 | tf_op jit(solution)/shard_map/ppermute | solution.py:10
  67.4 21.3 %copy-start.3 = (bf16[512,1024]{1,0:T(8,128)(2,1)}, bf16[512,1024]{1,0:T(8,128)(2,1)S(1)}, u32[]{:S(2)}) copy-start(bf16[512,1024]{1,0:T(8,128)(2,1)S(1)} %constant_dynamic-update-slice_fusion.6) | copy-start | bytes 3145732
  68.4 14.2 %copy-start.7 = (bf16[512,1024]{1,0:T(8,128)(2,1)}, bf16[512,1024]{1,0:T(8,128)(2,1)S(1)}, u32[]{:S(2)}) copy-start(bf16[512,1024]{1,0:T(8,128)(2,1)S(1)} %constant_dynamic-update-slice_fusion.2) | copy-start | bytes 3145732
  70.3 17.9 %copy-start.9 = (bf16[512,1024]{1,0:T(8,128)(2,1)}, bf16[512,1024]{1,0:T(8,128)(2,1)S(1)}, u32[]{:S(2)}) copy-start(bf16[512,1024]{1,0:T(8,128)(2,1)S(1)} %constant_dynamic-update-slice_fusion.4) | copy-start | bytes 3145732
  76.7 12.5 %collective-permute-start.13 = (bf16[256,1024]{0,1:T(8,128)(2,1)S(1)}, bf16[256,1024]{0,1:T(8,128)(2,1)S(1)}, u32[]{:S(2)}, u32[]{:S(2)}) collective-permute-start(bf16[256,1024]{0,1:T(8,128)(2,1)S(1)} %fusion.40), channel_id=1, source_target_pairs={{0,4},{4,0},{8,12},{12,8},{16,20},{20,16},{24,28},{28,24},{32,36},... | collective-permute-start | bytes 1572872 | tf_op jit(solution)/shard_map/ppermute | solution.py:10
  77.8 6.0 %collective-permute-start.11 = (bf16[256,1024]{0,1:T(8,128)(2,1)S(1)}, bf16[256,1024]{0,1:T(8,128)(2,1)S(1)}, u32[]{:S(2)}, u32[]{:S(2)}) collective-permute-start(bf16[256,1024]{0,1:T(8,128)(2,1)S(1)} %fusion.41), channel_id=1, source_target_pairs={{0,4},{4,0},{8,12},{12,8},{16,20},{20,16},{24,28},{28,24},{32,36},... | collective-permute-start | bytes 1572872 | tf_op jit(solution)/shard_map/ppermute | solution.py:10
  78.4 8.0 %collective-permute-start.9 = (bf16[256,1024]{0,1:T(8,128)(2,1)S(1)}, bf16[256,1024]{0,1:T(8,128)(2,1)S(1)}, u32[]{:S(2)}, u32[]{:S(2)}) collective-permute-start(bf16[256,1024]{0,1:T(8,128)(2,1)S(1)} %fusion.42), channel_id=1, source_target_pairs={{0,4},{4,0},{8,12},{12,8},{16,20},{20,16},{24,28},{28,24},{32,36},... | collective-permute-start | bytes 1572872 | tf_op jit(solution)/shard_map/ppermute | solution.py:10
  79.6 7.1 %collective-permute-start.7 = (bf16[256,1024]{0,1:T(8,128)(2,1)S(1)}, bf16[256,1024]{0,1:T(8,128)(2,1)S(1)}, u32[]{:S(2)}, u32[]{:S(2)}) collective-permute-start(bf16[256,1024]{0,1:T(8,128)(2,1)S(1)} %fusion.43), channel_id=1, source_target_pairs={{0,4},{4,0},{8,12},{12,8},{16,20},{20,16},{24,28},{28,24},{32,36},... | collective-permute-start | bytes 1572872 | tf_op jit(solution)/shard_map/ppermute | solution.py:10
  84.0 13.9 %collective-permute-start.12 = (bf16[256,1024]{0,1:T(8,128)(2,1)S(1)}, bf16[256,1024]{0,1:T(8,128)(2,1)S(1)}, u32[]{:S(2)}, u32[]{:S(2)}) collective-permute-start(bf16[256,1024]{0,1:T(8,128)(2,1)S(1)} %fusion.33), channel_id=1, source_target_pairs={{0,3},{1,0},{2,1},{3,2},{4,7},{5,4},{6,5},{7,6},{8,11},{9,8},{10,9... | collective-permute-start | bytes 1572872 | tf_op jit(solution)/shard_map/ppermute | solution.py:15
  86.6 25.2 %collective-permute-start.10 = (bf16[256,1024]{0,1:T(8,128)(2,1)S(1)}, bf16[256,1024]{0,1:T(8,128)(2,1)S(1)}, u32[]{:S(2)}, u32[]{:S(2)}) collective-permute-start(bf16[256,1024]{0,1:T(8,128)(2,1)S(1)} %fusion.36), channel_id=1, source_target_pairs={{0,1},{1,2},{2,3},{3,0},{4,5},{5,6},{6,7},{7,4},{8,9},{9,10},{10,1... | collective-permute-start | bytes 1572872 | tf_op jit(solution)/shard_map/ppermute | solution.py:15
  86.9 24.9 %collective-permute-start.8 = (bf16[256,1024]{0,1:T(8,128)(2,1)S(1)}, bf16[256,1024]{0,1:T(8,128)(2,1)S(1)}, u32[]{:S(2)}, u32[]{:S(2)}) collective-permute-start(bf16[256,1024]{0,1:T(8,128)(2,1)S(1)} %fusion.39), channel_id=1, source_target_pairs={{0,2},{1,3},{2,0},{3,1},{4,6},{5,7},{6,4},{7,5},{8,10},{9,11},{10,... | collective-permute-start | bytes 1572872 | tf_op jit(solution)/shard_map/ppermute | solution.py:15
  89.2 22.7 %copy-start.12 = (bf16[1,2048,512]{2,1,0:T(8,128)(2,1)}, bf16[1,2048,512]{2,1,0:T(8,128)(2,1)S(1)}, u32[]{:S(2)}) copy-start(bf16[1,2048,512]{2,1,0:T(8,128)(2,1)S(1)} %fusion.18) | copy-start | bytes 6291460
  115.2 24.6 %all-to-all-start.1 = ((bf16[64,4,1024]{2,1,0:T(4,128)(2,1)}), bf16[64,4,1024]{2,1,0:T(4,128)(2,1)S(1)}, u32[]{:S(2)}, u32[]{:S(2)}) async-start(bf16[64,4,1024]{2,1,0:T(4,128)(2,1)} %reshape.81), calls=%async_computation.1 | async-start | bytes 1048576 | tf_op jit(solution)/shard_map/all_to_all | solution.py:143
  122.5 2.9 %copy-start.8 = (bf16[512,1024]{1,0:T(8,128)(2,1)S(1)}, bf16[512,1024]{1,0:T(8,128)(2,1)}, u32[]{:S(2)}) copy-start(bf16[512,1024]{1,0:T(8,128)(2,1)} %copy-done.7) | copy-start | bytes 3145732
  124.0 2.5 %copy-start.10 = (bf16[512,1024]{1,0:T(8,128)(2,1)S(1)}, bf16[512,1024]{1,0:T(8,128)(2,1)}, u32[]{:S(2)}) copy-start(bf16[512,1024]{1,0:T(8,128)(2,1)} %copy-done.9) | copy-start | bytes 3145732
  (4 other events, 7.5 us)

commit v9 on v7

--- a/solution.py
+++ b/solution.py
@@ -46,6 +46,10 @@
     slot_pos = jnp.sum(before * lab_hot, axis=1).astype(jnp.int32)
     target_row = lang_label * capacity + slot_pos
     rows_out = n_expert * half_cap
+    w_gate = jnp.concatenate((gate_weight[0], partner(gate_weight[0], "expert", 0)), axis=1)
+    w_up = jnp.concatenate((up_weight[0], partner(up_weight[0], "expert", 0)), axis=1)
+    w_down = jnp.concatenate((down_weight[0], partner(down_weight[0], "expert", 0)), axis=0)
+    hid_own = gate_weight.shape[2]
     sources = jnp.concatenate((tokens, grad_rows), axis=1)
     dispatch_map = (
         jnp.arange(rows_out, dtype=jnp.int32)[:, None] == target_row[None, :]
@@ -60,14 +64,8 @@
     received = {k: shifted(own_piece, "tensor", k) for k in order if k}
     order = [0] + [k for k in reversed(order) if k]
     pieces = [own_piece if k == 0 else received[k] for k in order]
-    blocks = []
-    for p in pieces:
-        both = jnp.concatenate((p, partner(p, "expert", 0)), axis=0)
-        blocks.append((both[:, :feat_slice], both[:, feat_slice:]))
+    blocks = [(p[:, :feat_slice], p[:, feat_slice:]) for p in pieces]
     src_off = [((t_idx - k) % n_tensor) * feat_slice for k in order]
-    w_gate = gate_weight[0]
-    w_up = up_weight[0]
-    w_down = down_weight[0]
     contract_rows = (((0,), (0,)), ((), ()))
     contract_cols = (((1,), (1,)), ((), ()))
 
@@ -109,25 +107,6 @@
         jnp.bfloat16
     )
     grad_up_pre = (grad_hidden * activated).astype(jnp.bfloat16)
-    gate_grad = jnp.zeros(w_gate.shape, jnp.bfloat16)
-    up_grad = jnp.zeros(w_up.shape, jnp.bfloat16)
-    down_grad = jnp.zeros(w_down.shape, jnp.bfloat16)
-    for b, o in zip(blocks, src_off):
-        gate_piece = lax.dot_general(
-            b[0], grad_gate_pre, contract_rows, preferred_element_type=jnp.float32
-        ).astype(jnp.bfloat16)
-        up_piece = lax.dot_general(
-            b[0], grad_up_pre, contract_rows, preferred_element_type=jnp.float32
-        ).astype(jnp.bfloat16)
-        down_piece = lax.dot_general(
-            hidden, b[1], contract_rows, preferred_element_type=jnp.float32
-        ).astype(jnp.bfloat16)
-        gate_grad = lax.dynamic_update_slice_in_dim(gate_grad, gate_piece, o, axis=0)
-        up_grad = lax.dynamic_update_slice_in_dim(up_grad, up_piece, o, axis=0)
-        down_grad = lax.dynamic_update_slice_in_dim(down_grad, down_piece, o, axis=1)
-    gate_grad = gate_grad[None]
-    up_grad = up_grad[None]
-    down_grad = down_grad[None]
     acc = None
     for m in sorted(range(n_tensor), key=lambda k: -min(k, n_tensor - k)):
         off = ((t_idx + m) % n_tensor) * feat_slice
@@ -137,11 +116,35 @@
         ) + lax.dot_general(
             grad_up_pre, rows_of(w_up, off), contract_cols, preferred_element_type=jnp.float32
         )
-        part_m = jnp.concatenate((out_m, in_m), axis=1)
-        core_m = part_m[:rows_out] + partner(part_m[rows_out:], "expert", 0)
+        core_m = jnp.concatenate((out_m, in_m), axis=1)
         if m:
             core_m = shifted(core_m.astype(jnp.bfloat16), "tensor", m).astype(jnp.float32)
         acc = core_m if acc is None else acc + core_m
+    gate_both = jnp.zeros(w_gate.shape, jnp.float32)
+    up_both = jnp.zeros(w_up.shape, jnp.float32)
+    down_both = jnp.zeros(w_down.shape, jnp.float32)
+    for b, o in zip(blocks, src_off):
+        gate_piece = lax.dot_general(
+            b[0], grad_gate_pre, contract_rows, preferred_element_type=jnp.float32
+        )
+        up_piece = lax.dot_general(
+            b[0], grad_up_pre, contract_rows, preferred_element_type=jnp.float32
+        )
+        down_piece = lax.dot_general(
+            hidden, b[1], contract_rows, preferred_element_type=jnp.float32
+        )
+        gate_both = lax.dynamic_update_slice_in_dim(gate_both, gate_piece, o, axis=0)
+        up_both = lax.dynamic_update_slice_in_dim(up_both, up_piece, o, axis=0)
+        down_both = lax.dynamic_update_slice_in_dim(down_both, down_piece, o, axis=1)
+    gate_grad = (
+        gate_both[:, :hid_own] + partner(gate_both[:, hid_own:], "expert", 0)
+    ).astype(jnp.bfloat16)[None]
+    up_grad = (up_both[:, :hid_own] + partner(up_both[:, hid_own:], "expert", 0)).astype(
+        jnp.bfloat16
+    )[None]
+    down_grad = (
+        down_both[:hid_own] + partner(down_both[hid_own:], "expert", 0)
+    ).astype(jnp.bfloat16)[None]
     going_back = acc.astype(jnp.bfloat16).reshape(n_expert, half_cap, 2 * feat_slice)
     returned = lax.all_to_all(going_back, "expert", split_axis=0, concat_axis=0, tiled=True)
     flat_back = returned.reshape(rows_out, 2 * feat_slice)

time: 141 us -> 191 us (1.35)
  blocking collectives: 30.4 us -> 51.2 us
  matrix products: 24.4 us -> 41.9 us
  other arithmetic: 3.83 us -> 20.6 us
  waiting for transfers between devices: 52.5 us -> 42 us
  local copies, waits for them, and re-layouts: 9.69 us -> 19.3 us
  starting transfers between devices: 18.9 us -> 13.5 us
    all_to_all x0 -> x1, blocking collectives: none -> 23.7 us  [body(): lax.all_to_all(going_back, 'expert', split_axis=0, concat_axis=0, tiled=T...]
    broadcast_in_dim x0 -> x3, other arithmetic: none -> 15.4 us  [the longest x1 5.67 us: body(): (gate_both[:, :hid_own] + partner(gate_both[:, hid_own:], 'expert', 0)).a...]
    all_to_all x1 -> x0, waiting for transfers between devices: 10.6 us -> none  [body(): lax.all_to_all(going_back, 'expert', split_axis=0, concat_axis=0, tiled=T...]
    slice x0 -> x3, local copies, waits for them, and re-layouts: none -> 8.43 us  [the longest x1 3.05 us: body(): up_both[:, hid_own:]]
    all_to_all x1 -> x0, starting transfers between devices: 6.5 us -> none  [body(): lax.all_to_all(going_back, 'expert', split_axis=0, concat_axis=0, tiled=T...]
    dot_general x4, matrix products: 1.87 us -> 6.06 us  [body(): lax.dot_general(grad_gate_pre, rows_of(w_gate, off), contract_cols, prefe...]
    dot_general x4, matrix products: 1.8 us -> 5.93 us  [body(): jnp.dot(b[0], rows_of(w_gate, o), preferred_element_type=jnp.float32)]
    unnamed x30 -> x16, local copies, waits for them, and re-layouts: 2.01 us -> 6.05 us
  transfers between devices with their start and end apart: 15 -> 12, of which waited for: 6 -> 3; matrix products, arithmetic and copies ran while one was open for 13% -> 31% of each run, Pallas kernels for 0% -> 0%
where the time goes in v9:
time: 191 us; the launch traced here: 189 us
  blocking collectives  51.2 us (27%)
  waiting for transfers between devices  42 us (22%)
  matrix products  41.9 us (22%)
  other arithmetic  20.6 us (11%)
  local copies, waits for them, and re-layouts  19.3 us (10%)
  starting transfers between devices  13.5 us (7%)
    ppermute x6, waiting for transfers between devices, shifted(): lax.ppermute(value, axis, [(i, (i + step) % size) for i in range(size)])  41.9 us
    all_to_all x1, blocking collectives, body(): lax.all_to_all(outbound, 'expert', split_axis=0, concat_axis=0, tiled=True)  27.5 us
    all_to_all x1, blocking collectives, body(): lax.all_to_all(going_back, 'expert', split_axis=0, concat_axis=0, tiled=T...  23.7 us
    ppermute x6, starting transfers between devices, partner(): lax.ppermute(value, axis, [(i, i ^ 1 << stride) for i in range(lax.axis_s...  7.16 us
    ppermute x6, starting transfers between devices, shifted(): lax.ppermute(value, axis, [(i, (i + step) % size) for i in range(size)])  6.31 us
    dot_general x4, matrix products, body(): lax.dot_general(grad_gate_pre, rows_of(w_gate, off), contract_cols, prefe...  6.06 us
    unnamed x16, local copies, waits for them, and re-layouts  6.05 us
    dot_general x4, matrix products, body(): jnp.dot(b[0], rows_of(w_gate, o), preferred_element_type=jnp.float32)  5.93 us
  transfers between devices with their start and end apart: 12, of which 3 were waited for; matrix products, arithmetic and copies ran while one was open for 31% of the time, Pallas kernels for 0%

profile of v9, /device:TPU:1, one launch (start us, length us, event | category | flops | bytes accessed | tf_op | source)
XLA Modules:
  0.0 189.5 jit_solution(5264020790442507263)
XLA Ops:
  0.6 3.3 %collective-permute-start = (bf16[2048,512]{1,0:T(8,128)(2,1)}, bf16[2048,512]{1,0:T(8,128)(2,1)}, u32[]{:S(2)}, u32[]{:S(2)}) collective-permute-start(bf16[2048,512]{1,0:T(8,128)(2,1)} %bitcast.39), channel_id=1, source_target_pairs={{0,4},{4,0},{8,12},{12,8},{16,20},{20,16},{24,28},{28,24},{32,36},... | collective-permute-start | bytes 6291464 | tf_op jit(solution)/shard_map/ppermute | solution.py:10
  8.9 27.5 %all_to_all.10 = bf16[64,4,1024]{2,1,0:T(4,128)(2,1)} all-to-all(bf16[64,4,1024]{2,1,0:T(4,128)(2,1)S(1)} %reshape.34), channel_id=1, replica_groups=mesh['expert'=64,'tensor'=4] {'expert'}, dimensions={0} | all-to-all | bytes 1048576 | tf_op jit(solution)/shard_map/all_to_all | solution.py:61
  37.6 2.6 %collective-permute-start.1 = (bf16[256,1024]{1,0:T(8,128)(2,1)S(1)}, bf16[256,1024]{1,0:T(8,128)(2,1)S(1)}, u32[]{:S(2)}, u32[]{:S(2)}) collective-permute-start(bf16[256,1024]{1,0:T(8,128)(2,1)S(1)} %reshape.35), channel_id=1, source_target_pairs={{0,3},{1,0},{2,1},{3,2},{4,7},{5,4},{6,5},{7,6},{8,11},{9,8},{10,9... | collective-permute-start | bytes 1572872 | tf_op jit(solution)/shard_map/ppermute | solution.py:15
  41.3 21.0 %collective-permute-done.1 = bf16[256,1024]{1,0:T(8,128)(2,1)S(1)} collective-permute-done((bf16[256,1024]{1,0:T(8,128)(2,1)S(1)}, bf16[256,1024]{1,0:T(8,128)(2,1)S(1)}, u32[]{:S(2)}, u32[]{:S(2)}) %collective-permute-start.1) | collective-permute-done | bytes 524320 | tf_op jit(solution)/shard_map/ppermute | solution.py:15
  63.7 1.5 fusion.22
  66.4 10.5 %collective-permute-done.2 = bf16[256,1024]{1,0:T(8,128)(2,1)S(1)} collective-permute-done((bf16[256,1024]{1,0:T(8,128)(2,1)S(1)}, bf16[256,1024]{1,0:T(8,128)(2,1)S(1)}, u32[]{:S(2)}, u32[]{:S(2)}) %collective-permute-start.2) | collective-permute-done | bytes 524320 | tf_op jit(solution)/shard_map/ppermute | solution.py:15
  78.4 1.5 fusion.25
  81.4 1.5 fusion.28
  94.1 1.5 fusion.65
  95.6 1.5 fusion.12
  99.1 1.5 fusion.63
  100.6 1.5 fusion.13
  102.2 1.7 collective-permute-start.7
  106.8 3.0 %slice.75 = f32[2048,512]{1,0:T(8,128)} slice(f32[2048,1024]{1,0:T(8,128)S(1)} %convolution_dynamic-update-slice_fusion.8), slice={[0:2048], [512:1024]} | slice | bytes 8388608 | tf_op jit(solution)/shard_map/slice | solution.py:140
  111.3 2.6 %collective-permute-start.9 = (f32[2048,512]{1,0:T(8,128)}, f32[2048,512]{1,0:T(8,128)}, u32[]{:S(2)}, u32[]{:S(2)}) collective-permute-start(f32[2048,512]{1,0:T(8,128)} %slice.75), channel_id=1, source_target_pairs={{0,4},{4,0},{8,12},{12,8},{16,20},{20,16},{24,28},{28,24},{32,36},... | collective-permute-start | bytes 12582920 | tf_op jit(solution)/shard_map/ppermute | solution.py:10
  116.9 3.0 %slice.77 = f32[2048,512]{1,0:T(8,128)} slice(f32[2048,1024]{1,0:T(8,128)S(1)} %convolution_dynamic-update-slice_fusion.4), slice={[0:2048], [512:1024]} | slice | bytes 8388608 | tf_op jit(solution)/shard_map/slice | solution.py:142
  124.3 2.4 %slice.79 = f32[512,2048]{1,0:T(8,128)} slice(f32[1024,2048]{1,0:T(8,128)S(1)} %convolution_dynamic-update-slice_fusion), slice={[512:1024], [0:2048]} | slice | bytes 8388608 | tf_op jit(solution)/shard_map/slice | solution.py:146
  126.7 2.1 %copy-done.3 = f32[1024,2048]{1,0:T(8,128)} copy-done((f32[1024,2048]{1,0:T(8,128)}, f32[1024,2048]{1,0:T(8,128)S(1)}, u32[]{:S(2)}) %copy-start.3) | copy-done | bytes 8388632
  130.8 1.5 fusion.14
  137.5 10.5 %collective-permute-done.8 = bf16[256,1024]{1,0:T(8,128)(2,1)S(1)} collective-permute-done((bf16[256,1024]{1,0:T(8,128)(2,1)S(1)}, bf16[256,1024]{1,0:T(8,128)(2,1)S(1)}, u32[]{:S(2)}, u32[]{:S(2)}) %collective-permute-start.8) | collective-permute-done | bytes 524320 | tf_op jit(solution)/shard_map/ppermute | solution.py:15
  148.5 23.7 %all_to_all.11 = bf16[64,4,1024]{2,1,0:T(4,128)(2,1)S(1)} all-to-all(bf16[64,4,1024]{2,1,0:T(4,128)(2,1)S(1)} %reshape.36), channel_id=1, replica_groups=mesh['expert'=64,'tensor'=4] {'expert'}, dimensions={0} | all-to-all | bytes 1048576 | tf_op jit(solution)/shard_map/all_to_all | solution.py:149
  174.0 5.7 %fusion.3 = bf16[1,2048,512]{2,1,0:T(8,128)(2,1)} fusion(f32[2048,512]{1,0:T(8,128)} %collective-permute-done.9, f32[2048,1024]{1,0:T(8,128)} %copy-done.4), kind=kLoop, calls=%fused_computation.48 | loop fusion | flops 2097152 | bytes 10485760 | tf_op jit(solution)/shard_map/broadcast_in_dim | solution.py:139
  179.7 5.7 %fusion.4 = bf16[1,2048,512]{2,1,0:T(8,128)(2,1)} fusion(f32[2048,512]{1,0:T(8,128)} %collective-permute-done.10, f32[2048,1024]{1,0:T(8,128)} %copy-done.5), kind=kLoop, calls=%fused_computation.49 | loop fusion | flops 2097152 | bytes 10485760 | tf_op jit(solution)/shard_map/broadcast_in_dim | solution.py:142
  185.4 4.1 %fusion.5 = bf16[1,512,2048]{2,1,0:T(8,128)(2,1)} fusion(f32[512,2048]{1,0:T(8,128)} %collective-permute-done.11, f32[1024,2048]{1,0:T(8,128)S(1)} %bitcast.65), kind=kLoop, calls=%fused_computation.50 | loop fusion | flops 2097152 | bytes 10485760 | tf_op jit(solution)/shard_map/broadcast_in_dim | solution.py:145
  (81 shorter events, 47.0 us)
Async XLA Ops:
  0.6 61.6 %collective-permute-start = (bf16[2048,512]{1,0:T(8,128)(2,1)}, bf16[2048,512]{1,0:T(8,128)(2,1)}, u32[]{:S(2)}, u32[]{:S(2)}) collective-permute-start(bf16[2048,512]{1,0:T(8,128)(2,1)} %bitcast.39), channel_id=1, source_target_pairs={{0,4},{4,0},{8,12},{12,8},{16,20},{20,16},{24,28},{28,24},{32,36},... | collective-permute-start | bytes 6291464 | tf_op jit(solution)/shard_map/ppermute | solution.py:10
  4.0 59.8 %collective-permute-start.5 = (bf16[512,2048]{1,0:T(8,128)(2,1)}, bf16[512,2048]{1,0:T(8,128)(2,1)}, u32[]{:S(2)}, u32[]{:S(2)}) collective-permute-start(bf16[512,2048]{1,0:T(8,128)(2,1)} %bitcast.56), channel_id=1, source_target_pairs={{0,4},{4,0},{8,12},{12,8},{16,20},{20,16},{24,28},{28,24},{32,36},... | collective-permute-start | bytes 6291464 | tf_op jit(solution)/shard_map/ppermute | solution.py:10
  5.8 56.4 %copy-start = (bf16[1,2048,512]{2,1,0:T(8,128)(2,1)S(1)}, bf16[1,2048,512]{2,1,0:T(8,128)(2,1)}, u32[]{:S(2)}) copy-start(bf16[1,2048,512]{2,1,0:T(8,128)(2,1)} %param.13) | copy-start | bytes 6291460
  37.6 24.6 %collective-permute-start.1 = (bf16[256,1024]{1,0:T(8,128)(2,1)S(1)}, bf16[256,1024]{1,0:T(8,128)(2,1)S(1)}, u32[]{:S(2)}, u32[]{:S(2)}) collective-permute-start(bf16[256,1024]{1,0:T(8,128)(2,1)S(1)} %reshape.35), channel_id=1, source_target_pairs={{0,3},{1,0},{2,1},{3,2},{4,7},{5,4},{6,5},{7,6},{8,11},{9,8},{10,9... | collective-permute-start | bytes 1572872 | tf_op jit(solution)/shard_map/ppermute | solution.py:15
  40.1 43.3 %collective-permute-start.4 = (bf16[2048,512]{1,0:T(8,128)(2,1)}, bf16[2048,512]{1,0:T(8,128)(2,1)}, u32[]{:S(2)}, u32[]{:S(2)}) collective-permute-start(bf16[2048,512]{1,0:T(8,128)(2,1)} %bitcast.48), channel_id=1, source_target_pairs={{0,4},{4,0},{8,12},{12,8},{16,20},{20,16},{24,28},{28,24},{32,36},... | collective-permute-start | bytes 6291464 | tf_op jit(solution)/shard_map/ppermute | solution.py:10
  40.7 23.0 %copy-start.2 = (bf16[1,512,2048]{2,1,0:T(8,128)(2,1)S(1)}, bf16[1,512,2048]{2,1,0:T(8,128)(2,1)}, u32[]{:S(2)}) copy-start(bf16[1,512,2048]{2,1,0:T(8,128)(2,1)} %param.15) | copy-start | bytes 6291460
  40.7 39.2 %collective-permute-start.3 = (bf16[256,1024]{1,0:T(8,128)(2,1)S(1)}, bf16[256,1024]{1,0:T(8,128)(2,1)S(1)}, u32[]{:S(2)}, u32[]{:S(2)}) collective-permute-start(bf16[256,1024]{1,0:T(8,128)(2,1)S(1)} %reshape.35), channel_id=1, source_target_pairs={{0,2},{1,3},{2,0},{3,1},{4,6},{5,7},{6,4},{7,5},{8,10},{9,11},{10,... | collective-permute-start | bytes 1572872 | tf_op jit(solution)/shard_map/ppermute | solution.py:15
  62.2 14.7 %collective-permute-start.2 = (bf16[256,1024]{1,0:T(8,128)(2,1)S(1)}, bf16[256,1024]{1,0:T(8,128)(2,1)S(1)}, u32[]{:S(2)}, u32[]{:S(2)}) collective-permute-start(bf16[256,1024]{1,0:T(8,128)(2,1)S(1)} %reshape.35), channel_id=1, source_target_pairs={{0,1},{1,2},{2,3},{3,0},{4,5},{5,6},{6,7},{7,4},{8,9},{9,10},{10,1... | collective-permute-start | bytes 1572872 | tf_op jit(solution)/shard_map/ppermute | solution.py:15
  82.9 1.6 copy-start.1
  97.2 37.2 %collective-permute-start.6 = (bf16[256,1024]{1,0:T(8,128)(2,1)S(1)}, bf16[256,1024]{1,0:T(8,128)(2,1)S(1)}, u32[]{:S(2)}, u32[]{:S(2)}) collective-permute-start(bf16[256,1024]{1,0:T(8,128)(2,1)S(1)} %pad_maximum_fusion), channel_id=1, source_target_pairs={{0,2},{1,3},{2,0},{3,1},{4,6},{5,7},{6,4},{7,5},{8,10},{9,11},{10,... | collective-permute-start | bytes 1572872 | tf_op jit(solution)/shard_map/ppermute | solution.py:15
  102.2 35.2 %collective-permute-start.7 = (bf16[256,1024]{1,0:T(8,128)(2,1)S(1)}, bf16[256,1024]{1,0:T(8,128)(2,1)S(1)}, u32[]{:S(2)}, u32[]{:S(2)}) collective-permute-start(bf16[256,1024]{1,0:T(8,128)(2,1)S(1)} %pad_maximum_fusion.1), channel_id=1, source_target_pairs={{0,1},{1,2},{2,3},{3,0},{4,5},{5,6},{6,7},{7,4},{8,9},{9,10},{10,1... | collective-permute-start | bytes 1572872 | tf_op jit(solution)/shard_map/ppermute | solution.py:15
  106.8 4.5 %copy-start.4 = (f32[2048,1024]{1,0:T(8,128)}, f32[2048,1024]{1,0:T(8,128)S(1)}, u32[]{:S(2)}) copy-start(f32[2048,1024]{1,0:T(8,128)S(1)} %convolution_dynamic-update-slice_fusion.8) | copy-start | bytes 25165828
  111.3 62.7 %collective-permute-start.9 = (f32[2048,512]{1,0:T(8,128)}, f32[2048,512]{1,0:T(8,128)}, u32[]{:S(2)}, u32[]{:S(2)}) collective-permute-start(f32[2048,512]{1,0:T(8,128)} %slice.75), channel_id=1, source_target_pairs={{0,4},{4,0},{8,12},{12,8},{16,20},{20,16},{24,28},{28,24},{32,36},... | collective-permute-start | bytes 12582920 | tf_op jit(solution)/shard_map/ppermute | solution.py:10
  116.9 4.5 %copy-start.5 = (f32[2048,1024]{1,0:T(8,128)}, f32[2048,1024]{1,0:T(8,128)S(1)}, u32[]{:S(2)}) copy-start(f32[2048,1024]{1,0:T(8,128)S(1)} %convolution_dynamic-update-slice_fusion.4) | copy-start | bytes 25165828
  121.3 58.4 %collective-permute-start.10 = (f32[2048,512]{1,0:T(8,128)}, f32[2048,512]{1,0:T(8,128)}, u32[]{:S(2)}, u32[]{:S(2)}) collective-permute-start(f32[2048,512]{1,0:T(8,128)} %slice.77), channel_id=1, source_target_pairs={{0,4},{4,0},{8,12},{12,8},{16,20},{20,16},{24,28},{28,24},{32,36},... | collective-permute-start | bytes 12582920 | tf_op jit(solution)/shard_map/ppermute | solution.py:10
  124.3 4.5 %copy-start.3 = (f32[1024,2048]{1,0:T(8,128)}, f32[1024,2048]{1,0:T(8,128)S(1)}, u32[]{:S(2)}) copy-start(f32[1024,2048]{1,0:T(8,128)S(1)} %convolution_dynamic-update-slice_fusion) | copy-start | bytes 25165828
  128.7 56.6 %collective-permute-start.11 = (f32[512,2048]{1,0:T(8,128)}, f32[512,2048]{1,0:T(8,128)}, u32[]{:S(2)}, u32[]{:S(2)}) collective-permute-start(f32[512,2048]{1,0:T(8,128)} %slice.79), channel_id=1, source_target_pairs={{0,4},{4,0},{8,12},{12,8},{16,20},{20,16},{24,28},{28,24},{32,36},... | collective-permute-start | bytes 12582920 | tf_op jit(solution)/shard_map/ppermute | solution.py:10
  134.3 13.6 %collective-permute-start.8 = (bf16[256,1024]{1,0:T(8,128)(2,1)S(1)}, bf16[256,1024]{1,0:T(8,128)(2,1)S(1)}, u32[]{:S(2)}, u32[]{:S(2)}) collective-permute-start(bf16[256,1024]{1,0:T(8,128)(2,1)S(1)} %pad_maximum_fusion.2), channel_id=1, source_target_pairs={{0,3},{1,0},{2,1},{3,2},{4,7},{5,4},{6,5},{7,6},{8,11},{9,8},{10,9... | collective-permute-start | bytes 1572872 | tf_op jit(solution)/shard_map/ppermute | solution.py:15
  174.0 11.3 %slice-start = ((s8[8388608]{0:T(1024)(128)(4,1)}), s8[4194304]{0:T(1024)(128)(4,1)S(1)}, s32[]{:S(2)}) async-start(s8[8388608]{0:T(1024)(128)(4,1)} %bitcast.64), calls=%async_computation.2 | async-start | bytes 8388608
  179.7 5.7 %slice-start.1 = ((s8[8388608]{0:T(1024)(128)(4,1)}), s8[4194304]{0:T(1024)(128)(4,1)S(1)}, s32[]{:S(2)}) async-start(s8[8388608]{0:T(1024)(128)(4,1)} %bitcast.64), calls=%async_computation.3 | async-start | bytes 8388608

commit v10 on v7

--- a/solution.py
+++ b/solution.py
@@ -60,9 +60,11 @@
     received = {k: shifted(own_piece, "tensor", k) for k in order if k}
     order = [0] + [k for k in reversed(order) if k]
     pieces = [own_piece if k == 0 else received[k] for k in order]
+    late = partner(jnp.stack(pieces[1:]), "expert", 0)
+    swapped = [partner(pieces[0], "expert", 0)] + [late[i] for i in range(n_tensor - 1)]
     blocks = []
-    for p in pieces:
-        both = jnp.concatenate((p, partner(p, "expert", 0)), axis=0)
+    for p, q in zip(pieces, swapped):
+        both = jnp.concatenate((p, q), axis=0)
         blocks.append((both[:, :feat_slice], both[:, feat_slice:]))
     src_off = [((t_idx - k) % n_tensor) * feat_slice for k in order]
     w_gate = gate_weight[0]

time: 141 us -> 154 us (1.092)
  local copies, waits for them, and re-layouts: 9.69 us -> 14.7 us
  waiting for transfers between devices: 52.5 us -> 57.2 us
  other arithmetic: 3.83 us -> 6.13 us
    unnamed x30 -> x37, local copies, waits for them, and re-layouts: 2.01 us -> 5.12 us
    ppermute x8 -> x6, waiting for transfers between devices: 0.02 us -> 3.06 us  [partner(): lax.ppermute(value, axis, [(i, i ^ 1 << stride) for i in range(lax.axis_s...]
    dot_general x4, matrix products: 1.85 us -> 3.77 us  [body(): lax.dot_general(hidden, b[1], contract_rows, preferred_element_type=jnp.f...]
    squeeze x0 -> x1, local copies, waits for them, and re-layouts: none -> 1.62 us  [body(): late[i]]
    ppermute x8 -> x6, starting transfers between devices: 4.7 us -> 4.74 us  [partner(): lax.ppermute(value, axis, [(i, i ^ 1 << stride) for i in range(lax.axis_s...]
  transfers between devices with their start and end apart: 15 -> 13, of which waited for: 6 -> 6; matrix products, arithmetic and copies ran while one was open for 13% -> 9% of each run, Pallas kernels for 0% -> 0%
where the time goes in v10:
time: 154 us; the launch traced here: 153 us
  waiting for transfers between devices  57.2 us (37%)
  blocking collectives  30.3 us (20%)
  matrix products  25.4 us (16%)
  starting transfers between devices  18.1 us (12%)
  local copies, waits for them, and re-layouts  14.7 us (10%)
  other arithmetic  6.13 us (4%)
    ppermute x6, waiting for transfers between devices, shifted(): lax.ppermute(value, axis, [(i, (i + step) % size) for i in range(size)])  43.1 us
    all_to_all x1, blocking collectives, body(): lax.all_to_all(outbound, 'expert', split_axis=0, concat_axis=0, tiled=True)  30.3 us
    all_to_all x1, waiting for transfers between devices, body(): lax.all_to_all(going_back, 'expert', split_axis=0, concat_axis=0, tiled=T...  11.1 us
    ppermute x6, starting transfers between devices, shifted(): lax.ppermute(value, axis, [(i, (i + step) % size) for i in range(size)])  7.04 us
    all_to_all x1, starting transfers between devices, body(): lax.all_to_all(going_back, 'expert', split_axis=0, concat_axis=0, tiled=T...  6.3 us
    unnamed x37, local copies, waits for them, and re-layouts  5.12 us
    ppermute x6, starting transfers between devices, partner(): lax.ppermute(value, axis, [(i, i ^ 1 << stride) for i in range(lax.axis_s...  4.74 us
    dot_general x4, matrix products, body(): lax.dot_general(b[0], grad_gate_pre, contract_rows, preferred_element_typ...  4.23 us
  transfers between devices with their start and end apart: 13, of which 6 were waited for; matrix products, arithmetic and copies ran while one was open for 9% of the time, Pallas kernels for 0%

profile of v10, /device:TPU:1, one launch (start us, length us, event | category | flops | bytes accessed | tf_op | source)
XLA Modules:
  0.0 153.0 jit_solution(11876416850590113337)
XLA Ops:
  4.0 1.2 convolution_convert_fusion.12
  5.4 30.3 %all_to_all.10 = bf16[64,4,1024]{2,1,0:T(4,128)(2,1)S(1)} all-to-all(bf16[64,4,1024]{2,1,0:T(4,128)(2,1)S(1)} %reshape.79), channel_id=1, replica_groups=mesh['expert'=64,'tensor'=4] {'expert'}, dimensions={0} | all-to-all | bytes 1048576 | tf_op jit(solution)/shard_map/all_to_all | solution.py:57
  36.6 2.5 %collective-permute-start.1 = (bf16[256,1024]{1,0:T(8,128)(2,1)}, bf16[256,1024]{1,0:T(8,128)(2,1)S(1)}, u32[]{:S(2)}, u32[]{:S(2)}) collective-permute-start(bf16[256,1024]{1,0:T(8,128)(2,1)} %reshape.80), channel_id=1, source_target_pairs={{0,3},{1,0},{2,1},{3,2},{4,7},{5,4},{6,5},{7,6},{8,11},{9,8},{10,9... | collective-permute-start | bytes 1572872 | tf_op jit(solution)/shard_map/ppermute | solution.py:15
  39.1 1.7 %collective-permute-start.3 = (bf16[256,1024]{1,0:T(8,128)(2,1)}, bf16[256,1024]{1,0:T(8,128)(2,1)S(1)}, u32[]{:S(2)}, u32[]{:S(2)}) collective-permute-start(bf16[256,1024]{1,0:T(8,128)(2,1)} %reshape.80), channel_id=1, source_target_pairs={{0,2},{1,3},{2,0},{3,1},{4,6},{5,7},{6,4},{7,5},{8,10},{9,11},{10,... | collective-permute-start | bytes 1572872 | tf_op jit(solution)/shard_map/ppermute | solution.py:15
  40.8 20.7 %collective-permute-done.1 = bf16[256,1024]{1,0:T(8,128)(2,1)S(1)} collective-permute-done((bf16[256,1024]{1,0:T(8,128)(2,1)}, bf16[256,1024]{1,0:T(8,128)(2,1)S(1)}, u32[]{:S(2)}, u32[]{:S(2)}) %collective-permute-start.1) | collective-permute-done | bytes 524320 | tf_op jit(solution)/shard_map/ppermute | solution.py:15
  61.5 2.2 %collective-permute-done.3 = bf16[256,1024]{1,0:T(8,128)(2,1)S(1)} collective-permute-done((bf16[256,1024]{1,0:T(8,128)(2,1)}, bf16[256,1024]{1,0:T(8,128)(2,1)S(1)}, u32[]{:S(2)}, u32[]{:S(2)}) %collective-permute-start.3) | collective-permute-done | bytes 524320 | tf_op jit(solution)/shard_map/ppermute | solution.py:15
  63.8 1.3 pad_maximum_fusion
  65.1 3.2 %collective-permute-start.4 = (bf16[3,256,1024]{2,1,0:T(8,128)(2,1)}, bf16[3,256,1024]{2,1,0:T(8,128)(2,1)}, u32[]{:S(2)}, u32[]{:S(2)}) collective-permute-start(bf16[3,256,1024]{2,1,0:T(8,128)(2,1)} %pad_maximum_fusion), channel_id=1, source_target_pairs={{0,4},{4,0},{8,12},{12,8},{16,20},{20,16},{24,28},{28,24},{32,36},... | collective-permute-start | bytes 4718600 | tf_op jit(solution)/shard_map/ppermute | solution.py:10
  69.3 3.0 %collective-permute-done = bf16[256,1024]{1,0:T(8,128)(2,1)} collective-permute-done((bf16[256,1024]{1,0:T(8,128)(2,1)}, bf16[256,1024]{1,0:T(8,128)(2,1)}, u32[]{:S(2)}, u32[]{:S(2)}) %collective-permute-start) | collective-permute-done | bytes 524320 | tf_op jit(solution)/shard_map/ppermute | solution.py:10
  73.5 1.6 %slice_bitcast_fusion.2 = (bf16[256,1024]{1,0:T(8,128)(2,1)S(1)}, bf16[256,1024]{1,0:T(8,128)(2,1)S(1)}, bf16[256,1024]{1,0:T(8,128)(2,1)S(1)}) fusion(bf16[3,256,1024]{2,1,0:T(8,128)(2,1)} %collective-permute-done.4), kind=kLoop, calls=%fused_computation.99 | loop fusion | bytes 3145728 | tf_op jit(solution)/shard_map/squeeze | solution.py:64
  95.8 2.1 %collective-permute-start.10 = (bf16[256,1024]{0,1:T(8,128)(2,1)S(1)}, bf16[256,1024]{0,1:T(8,128)(2,1)S(1)}, u32[]{:S(2)}, u32[]{:S(2)}) collective-permute-start(bf16[256,1024]{0,1:T(8,128)(2,1)S(1)} %fusion.37), channel_id=1, source_target_pairs={{0,3},{1,0},{2,1},{3,2},{4,7},{5,4},{6,5},{7,6},{8,11},{9,8},{10,9... | collective-permute-start | bytes 1572872 | tf_op jit(solution)/shard_map/ppermute | solution.py:15
  99.8 1.3 copy-done.15
  101.1 8.3 %collective-permute-done.6 = bf16[256,1024]{0,1:T(8,128)(2,1)S(1)} collective-permute-done((bf16[256,1024]{0,1:T(8,128)(2,1)S(1)}, bf16[256,1024]{0,1:T(8,128)(2,1)S(1)}, u32[]{:S(2)}, u32[]{:S(2)}) %collective-permute-start.6) | collective-permute-done | bytes 524320 | tf_op jit(solution)/shard_map/ppermute | solution.py:15
  109.3 11.9 %collective-permute-done.8 = bf16[256,1024]{0,1:T(8,128)(2,1)S(1)} collective-permute-done((bf16[256,1024]{0,1:T(8,128)(2,1)S(1)}, bf16[256,1024]{0,1:T(8,128)(2,1)S(1)}, u32[]{:S(2)}, u32[]{:S(2)}) %collective-permute-start.8) | collective-permute-done | bytes 524320 | tf_op jit(solution)/shard_map/ppermute | solution.py:15
  121.3 1.1 fusion.34
  122.4 2.1 %copy.14 = bf16[256,1024]{1,0:T(8,128)(2,1)} copy(bf16[256,1024]{0,1:T(8,128)(2,1)} %fusion.34) | data formatting | bytes 1048576 | tf_op jit(solution)/shard_map/convert_element_type | solution.py:147
  124.4 2.0 %reshape.81 = bf16[64,4,1024]{2,1,0:T(4,128)(2,1)} reshape(bf16[256,1024]{1,0:T(8,128)(2,1)} %copy.14) | data formatting | bytes 1048576 | tf_op jit(solution)/shard_map/reshape | solution.py:147
  126.5 6.3 %all-to-all-start.1 = ((bf16[64,4,1024]{2,1,0:T(4,128)(2,1)}), bf16[64,4,1024]{2,1,0:T(4,128)(2,1)}, u32[]{:S(2)}, u32[]{:S(2)}) async-start(bf16[64,4,1024]{2,1,0:T(4,128)(2,1)} %reshape.81), calls=%async_computation.1 | async-start | bytes 1048576 | tf_op jit(solution)/shard_map/all_to_all | solution.py:148
  132.8 2.4 %fusion.29 = bf16[1,512,2048]{2,1,0:T(8,128)(2,1)} fusion(bf16[1,512,2048]{2,1,0:T(8,128)(2,1)} %copy-done.16, s32[]{:T(128)S(6)} %select_n.90, bf16[512,512]{1,0:T(8,128)(2,1)S(1)} %get-tuple-element.5, bf16[256,1024]{1,0:T(8,128)(2,1)} %copy-done.14, bf16[256,1024]{1,0:T(8,128)(2,1)} %copy-done.11), kind=kOutput, calls=%fused_computation.58 | convolution fusion | flops 269746176 | bytes 2097156 | tf_op jit(solution)/shard_map/dot_general | solution.py:124
  135.2 1.3 fusion.9
  136.4 1.3 fusion.11
  137.7 1.3 fusion.13
  139.0 11.1 %all-to-all-done.1 = bf16[64,4,1024]{2,1,0:T(4,128)(2,1)} async-done(((bf16[64,4,1024]{2,1,0:T(4,128)(2,1)}), bf16[64,4,1024]{2,1,0:T(4,128)(2,1)}, u32[]{:S(2)}, u32[]{:S(2)}) %all-to-all-start.1) | async-done | bytes 524320 | tf_op jit(solution)/shard_map/all_to_all | solution.py:148
  150.0 1.2 reshape.82
  (104 shorter events, 30.6 us)
Async XLA Ops:
  0.6 75.3 %copy-start = (bf16[1,2048,512]{2,1,0:T(8,128)(2,1)S(1)}, bf16[1,2048,512]{2,1,0:T(8,128)(2,1)}, u32[]{:S(2)}) copy-start(bf16[1,2048,512]{2,1,0:T(8,128)(2,1)} %param.14) | copy-start | bytes 6291460
  36.6 24.9 %collective-permute-start.1 = (bf16[256,1024]{1,0:T(8,128)(2,1)}, bf16[256,1024]{1,0:T(8,128)(2,1)S(1)}, u32[]{:S(2)}, u32[]{:S(2)}) collective-permute-start(bf16[256,1024]{1,0:T(8,128)(2,1)} %reshape.80), channel_id=1, source_target_pairs={{0,3},{1,0},{2,1},{3,2},{4,7},{5,4},{6,5},{7,6},{8,11},{9,8},{10,9... | collective-permute-start | bytes 1572872 | tf_op jit(solution)/shard_map/ppermute | solution.py:15
  39.1 22.4 %collective-permute-start.2 = (bf16[256,1024]{1,0:T(8,128)(2,1)}, bf16[256,1024]{1,0:T(8,128)(2,1)S(1)}, u32[]{:S(2)}, u32[]{:S(2)}) collective-permute-start(bf16[256,1024]{1,0:T(8,128)(2,1)} %reshape.80), channel_id=1, source_target_pairs={{0,1},{1,2},{2,3},{3,0},{4,5},{5,6},{6,7},{7,4},{8,9},{9,10},{10,1... | collective-permute-start | bytes 1572872 | tf_op jit(solution)/shard_map/ppermute | solution.py:15
  39.1 24.6 %collective-permute-start.3 = (bf16[256,1024]{1,0:T(8,128)(2,1)}, bf16[256,1024]{1,0:T(8,128)(2,1)S(1)}, u32[]{:S(2)}, u32[]{:S(2)}) collective-permute-start(bf16[256,1024]{1,0:T(8,128)(2,1)} %reshape.80), channel_id=1, source_target_pairs={{0,2},{1,3},{2,0},{3,1},{4,6},{5,7},{6,4},{7,5},{8,10},{9,11},{10,... | collective-permute-start | bytes 1572872 | tf_op jit(solution)/shard_map/ppermute | solution.py:15
  61.5 18.8 %copy-start.9 = (bf16[256,1024]{1,0:T(8,128)(2,1)}, bf16[256,1024]{1,0:T(8,128)(2,1)S(1)}, u32[]{:S(2)}) copy-start(bf16[256,1024]{1,0:T(8,128)(2,1)S(1)} %collective-permute-done.1) | copy-start | bytes 1572868
  61.5 2.2 %copy-start.12 = (bf16[256,1024]{1,0:T(8,128)(2,1)}, bf16[256,1024]{1,0:T(8,128)(2,1)S(1)}, u32[]{:S(2)}) copy-start(bf16[256,1024]{1,0:T(8,128)(2,1)S(1)} %collective-permute-done.2) | copy-start | bytes 1572868
  63.7 14.9 %copy-start.11 = (bf16[256,1024]{1,0:T(8,128)(2,1)}, bf16[256,1024]{1,0:T(8,128)(2,1)S(1)}, u32[]{:S(2)}) copy-start(bf16[256,1024]{1,0:T(8,128)(2,1)S(1)} %collective-permute-done.3) | copy-start | bytes 1572868
  65.1 8.4 %collective-permute-start.4 = (bf16[3,256,1024]{2,1,0:T(8,128)(2,1)}, bf16[3,256,1024]{2,1,0:T(8,128)(2,1)}, u32[]{:S(2)}, u32[]{:S(2)}) collective-permute-start(bf16[3,256,1024]{2,1,0:T(8,128)(2,1)} %pad_maximum_fusion), channel_id=1, source_target_pairs={{0,4},{4,0},{8,12},{12,8},{16,20},{20,16},{24,28},{28,24},{32,36},... | collective-permute-start | bytes 4718600 | tf_op jit(solution)/shard_map/ppermute | solution.py:10
  68.2 4.1 %collective-permute-start = (bf16[256,1024]{1,0:T(8,128)(2,1)}, bf16[256,1024]{1,0:T(8,128)(2,1)}, u32[]{:S(2)}, u32[]{:S(2)}) collective-permute-start(bf16[256,1024]{1,0:T(8,128)(2,1)} %reshape.80), channel_id=1, source_target_pairs={{0,4},{4,0},{8,12},{12,8},{16,20},{20,16},{24,28},{28,24},{32,36},... | collective-permute-start | bytes 1572872 | tf_op jit(solution)/shard_map/ppermute | solution.py:10
  75.1 3.6 %copy-start.14 = (bf16[256,1024]{1,0:T(8,128)(2,1)}, bf16[256,1024]{1,0:T(8,128)(2,1)S(1)}, u32[]{:S(2)}) copy-start(bf16[256,1024]{1,0:T(8,128)(2,1)S(1)} %get-tuple-element.9) | copy-start | bytes 1572868
  75.5 15.8 %copy-start.3 = (bf16[512,512]{1,0:T(8,128)(2,1)}, bf16[512,512]{1,0:T(8,128)(2,1)S(1)}, u32[]{:S(2)}) copy-start(bf16[512,512]{1,0:T(8,128)(2,1)S(1)} %fusion.47) | copy-start | bytes 1572868
  76.8 16.5 %copy-start.7 = (bf16[512,512]{1,0:T(8,128)(2,1)}, bf16[512,512]{1,0:T(8,128)(2,1)S(1)}, u32[]{:S(2)}) copy-start(bf16[512,512]{1,0:T(8,128)(2,1)S(1)} %get-tuple-element.12) | copy-start | bytes 1572868
  76.8 21.1 %copy-start.5 = (bf16[512,512]{1,0:T(8,128)(2,1)}, bf16[512,512]{1,0:T(8,128)(2,1)S(1)}, u32[]{:S(2)}) copy-start(bf16[512,512]{1,0:T(8,128)(2,1)S(1)} %get-tuple-element.11) | copy-start | bytes 1572868
  88.5 5.3 %collective-permute-start.5 = (f32[256,1024]{0,1:T(8,128)S(1)}, f32[256,1024]{0,1:T(8,128)S(1)}, u32[]{:S(2)}, u32[]{:S(2)}) collective-permute-start(f32[256,1024]{0,1:T(8,128)S(1)} %pad_maximum_fusion.4), channel_id=1, source_target_pairs={{0,4},{4,0},{8,12},{12,8},{16,20},{20,16},{24,28},{28,24},{32,36},... | collective-permute-start | bytes 3145736 | tf_op jit(solution)/shard_map/ppermute | solution.py:10
  89.6 5.1 %collective-permute-start.7 = (f32[256,1024]{0,1:T(8,128)S(1)}, f32[256,1024]{0,1:T(8,128)S(1)}, u32[]{:S(2)}, u32[]{:S(2)}) collective-permute-start(f32[256,1024]{0,1:T(8,128)S(1)} %pad_maximum_fusion.3), channel_id=1, source_target_pairs={{0,4},{4,0},{8,12},{12,8},{16,20},{20,16},{24,28},{28,24},{32,36},... | collective-permute-start | bytes 3145736 | tf_op jit(solution)/shard_map/ppermute | solution.py:10
  90.4 5.2 %collective-permute-start.9 = (f32[256,1024]{0,1:T(8,128)S(1)}, f32[256,1024]{0,1:T(8,128)S(1)}, u32[]{:S(2)}, u32[]{:S(2)}) collective-permute-start(f32[256,1024]{0,1:T(8,128)S(1)} %pad_maximum_fusion.2), channel_id=1, source_target_pairs={{0,4},{4,0},{8,12},{12,8},{16,20},{20,16},{24,28},{28,24},{32,36},... | collective-permute-start | bytes 3145736 | tf_op jit(solution)/shard_map/ppermute | solution.py:10
  91.9 9.1 %collective-permute-start.11 = (f32[256,1024]{0,1:T(8,128)S(1)}, f32[256,1024]{0,1:T(8,128)S(1)}, u32[]{:S(2)}, u32[]{:S(2)}) collective-permute-start(f32[256,1024]{0,1:T(8,128)S(1)} %pad_maximum_fusion.1), channel_id=1, source_target_pairs={{0,4},{4,0},{8,12},{12,8},{16,20},{20,16},{24,28},{28,24},{32,36},... | collective-permute-start | bytes 3145736 | tf_op jit(solution)/shard_map/ppermute | solution.py:10
  94.7 14.7 %collective-permute-start.6 = (bf16[256,1024]{0,1:T(8,128)(2,1)S(1)}, bf16[256,1024]{0,1:T(8,128)(2,1)S(1)}, u32[]{:S(2)}, u32[]{:S(2)}) collective-permute-start(bf16[256,1024]{0,1:T(8,128)(2,1)S(1)} %fusion.43), channel_id=1, source_target_pairs={{0,2},{1,3},{2,0},{3,1},{4,6},{5,7},{6,4},{7,5},{8,10},{9,11},{10,... | collective-permute-start | bytes 1572872 | tf_op jit(solution)/shard_map/ppermute | solution.py:15
  94.9 26.4 %collective-permute-start.8 = (bf16[256,1024]{0,1:T(8,128)(2,1)S(1)}, bf16[256,1024]{0,1:T(8,128)(2,1)S(1)}, u32[]{:S(2)}, u32[]{:S(2)}) collective-permute-start(bf16[256,1024]{0,1:T(8,128)(2,1)S(1)} %fusion.40), channel_id=1, source_target_pairs={{0,1},{1,2},{2,3},{3,0},{4,5},{5,6},{6,7},{7,4},{8,9},{9,10},{10,1... | collective-permute-start | bytes 1572872 | tf_op jit(solution)/shard_map/ppermute | solution.py:15
  95.8 25.4 %collective-permute-start.10 = (bf16[256,1024]{0,1:T(8,128)(2,1)S(1)}, bf16[256,1024]{0,1:T(8,128)(2,1)S(1)}, u32[]{:S(2)}, u32[]{:S(2)}) collective-permute-start(bf16[256,1024]{0,1:T(8,128)(2,1)S(1)} %fusion.37), channel_id=1, source_target_pairs={{0,3},{1,0},{2,1},{3,2},{4,7},{5,4},{6,5},{7,6},{8,11},{9,8},{10,9... | collective-permute-start | bytes 1572872 | tf_op jit(solution)/shard_map/ppermute | solution.py:15
  126.5 23.5 %all-to-all-start.1 = ((bf16[64,4,1024]{2,1,0:T(4,128)(2,1)}), bf16[64,4,1024]{2,1,0:T(4,128)(2,1)}, u32[]{:S(2)}, u32[]{:S(2)}) async-start(bf16[64,4,1024]{2,1,0:T(4,128)(2,1)} %reshape.81), calls=%async_computation.1 | async-start | bytes 1048576 | tf_op jit(solution)/shard_map/all_to_all | solution.py:148
  132.8 2.4 %copy-start.4 = (bf16[512,512]{1,0:T(8,128)(2,1)S(1)}, bf16[512,512]{1,0:T(8,128)(2,1)}, u32[]{:S(2)}) copy-start(bf16[512,512]{1,0:T(8,128)(2,1)} %copy-done.3) | copy-start | bytes 1572868
  132.8 3.6 %copy-start.8 = (bf16[512,512]{1,0:T(8,128)(2,1)S(1)}, bf16[512,512]{1,0:T(8,128)(2,1)}, u32[]{:S(2)}) copy-start(bf16[512,512]{1,0:T(8,128)(2,1)} %copy-done.7) | copy-start | bytes 1572868
  135.2 2.5 %copy-start.6 = (bf16[512,512]{1,0:T(8,128)(2,1)S(1)}, bf16[512,512]{1,0:T(8,128)(2,1)}, u32[]{:S(2)}) copy-start(bf16[512,512]{1,0:T(8,128)(2,1)} %copy-done.5) | copy-start | bytes 1572868
  (7 other events, 9.9 us)

commit v11 on v7

--- a/solution.py
+++ b/solution.py
@@ -142,15 +142,17 @@
         if m:
             core_m = shifted(core_m.astype(jnp.bfloat16), "tensor", m).astype(jnp.float32)
         acc = core_m if acc is None else acc + core_m
-    going_back = acc.astype(jnp.bfloat16).reshape(n_expert, half_cap, 2 * feat_slice)
-    returned = lax.all_to_all(going_back, "expert", split_axis=0, concat_axis=0, tiled=True)
-    flat_back = returned.reshape(rows_out, 2 * feat_slice)
+    acc = acc.astype(jnp.bfloat16)
+    going_back = jnp.stack((acc[:, :feat_slice], acc[:, feat_slice:]))
+    going_back = going_back.reshape(2, n_expert, half_cap, feat_slice)
+    returned = lax.all_to_all(going_back, "expert", split_axis=1, concat_axis=1, tiled=True)
+    flat_back = returned.reshape(2, rows_out, feat_slice)
     home_map = (
         jnp.arange(rows_out, dtype=jnp.int32)[:, None] == target_row[None, :]
     ).astype(jnp.bfloat16)
     home = [
         lax.dot_general(
-            home_map, flat_back[:, i * feat_slice : (i + 1) * feat_slice], contract_rows,
+            home_map, flat_back[i], contract_rows,
             preferred_element_type=jnp.float32,
         ).astype(jnp.bfloat16)
         for i in range(2)

time: 141 us -> 140 us (level)
    reshape x2 -> x0, local copies, waits for them, and re-layouts: 2.15 us -> none  [the longest x1 2.04 us: body(): acc.astype(jnp.bfloat16).reshape(n_expert, half_cap, 2 * feat_slice)]
where the time goes in v11:
time: 140 us
  waiting for transfers between devices  52.5 us (38%)
  blocking collectives  30.4 us (22%)
  matrix products  24.4 us (17%)
  starting transfers between devices  18.9 us (13%)
  local copies, waits for them, and re-layouts  8.29 us (6%)
  other arithmetic  4.2 us (3%)
    ppermute x6, waiting for transfers between devices, shifted(): lax.ppermute(value, axis, [(i, (i + step) % size) for i in range(size)])  41.9 us
    all_to_all x1, blocking collectives, body(): lax.all_to_all(outbound, 'expert', split_axis=0, concat_axis=0, tiled=True)  30.4 us
    all_to_all x1, waiting for transfers between devices, body(): lax.all_to_all(going_back, 'expert', split_axis=1, concat_axis=1, tiled=T...  10.6 us
    ppermute x6, starting transfers between devices, shifted(): lax.ppermute(value, axis, [(i, (i + step) % size) for i in range(size)])  7.72 us
    all_to_all x1, starting transfers between devices, body(): lax.all_to_all(going_back, 'expert', split_axis=1, concat_axis=1, tiled=T...  6.5 us
    dot_general x4, matrix products, body(): lax.dot_general(b[0], grad_gate_pre, contract_rows, preferred_element_typ...  5.11 us
    ppermute x8, starting transfers between devices, partner(): lax.ppermute(value, axis, [(i, i ^ 1 << stride) for i in range(lax.axis_s...  4.7 us
  transfers between devices with their start and end apart: 15, of which 6 were waited for; matrix products, arithmetic and copies ran while one was open for 13% of the time, Pallas kernels for 0%

profile of v11, /device:TPU:1, one launch (start us, length us, event | category | flops | bytes accessed | tf_op | source)
XLA Modules:
  0.0 140.0 jit_solution(10997383529131991804)
XLA Ops:
  0.6 1.0 fusion.27
  3.1 1.0 multiply_convert_fusion.3
  4.0 1.2 convolution_convert_fusion.12
  5.4 30.4 %all_to_all.10 = bf16[64,4,1024]{2,1,0:T(4,128)(2,1)} all-to-all(bf16[64,4,1024]{2,1,0:T(4,128)(2,1)S(1)} %reshape.83), channel_id=1, replica_groups=mesh['expert'=64,'tensor'=4] {'expert'}, dimensions={0} | all-to-all | bytes 1048576 | tf_op jit(solution)/shard_map/all_to_all | solution.py:57
  35.8 1.2 reshape.84
  37.0 2.6 %collective-permute-start.1 = (bf16[256,1024]{1,0:T(8,128)(2,1)S(1)}, bf16[256,1024]{1,0:T(8,128)(2,1)S(1)}, u32[]{:S(2)}, u32[]{:S(2)}) collective-permute-start(bf16[256,1024]{1,0:T(8,128)(2,1)S(1)} %reshape.84), channel_id=1, source_target_pairs={{0,3},{1,0},{2,1},{3,2},{4,7},{5,4},{6,5},{7,6},{8,11},{9,8},{10,9... | collective-permute-start | bytes 1572872 | tf_op jit(solution)/shard_map/ppermute | solution.py:15
  40.1 0.9 collective-permute-start
  41.6 20.0 %collective-permute-done.1 = bf16[256,1024]{1,0:T(8,128)(2,1)S(1)} collective-permute-done((bf16[256,1024]{1,0:T(8,128)(2,1)S(1)}, bf16[256,1024]{1,0:T(8,128)(2,1)S(1)}, u32[]{:S(2)}, u32[]{:S(2)}) %collective-permute-start.1) | collective-permute-done | bytes 524320 | tf_op jit(solution)/shard_map/ppermute | solution.py:15
  61.7 1.4 %collective-permute-start.2 = (bf16[256,1024]{1,0:T(8,128)(2,1)S(1)}, bf16[256,1024]{1,0:T(8,128)(2,1)S(1)}, u32[]{:S(2)}, u32[]{:S(2)}) collective-permute-start(bf16[256,1024]{1,0:T(8,128)(2,1)S(1)} %collective-permute-done.1), channel_id=1, source_target_pairs={{0,4},{4,0},{8,12},{12,8},{16,20},{20,16},{24,28},{28,24},{32,36},... | collective-permute-start | bytes 1572872 | tf_op jit(solution)/shard_map/ppermute | solution.py:10
  63.2 1.1 constant_dynamic-update-slice_fusion.7
  64.3 1.2 constant_dynamic-update-slice_fusion
  85.5 3.3 %collective-permute-start.10 = (bf16[256,1024]{0,1:T(8,128)(2,1)S(1)}, bf16[256,1024]{0,1:T(8,128)(2,1)S(1)}, u32[]{:S(2)}, u32[]{:S(2)}) collective-permute-start(bf16[256,1024]{0,1:T(8,128)(2,1)S(1)} %fusion.37), channel_id=1, source_target_pairs={{0,1},{1,2},{2,3},{3,0},{4,5},{5,6},{6,7},{7,4},{8,9},{9,10},{10,1... | collective-permute-start | bytes 1572872 | tf_op jit(solution)/shard_map/ppermute | solution.py:15
  90.2 9.6 %collective-permute-done.8 = bf16[256,1024]{0,1:T(8,128)(2,1)S(1)} collective-permute-done((bf16[256,1024]{0,1:T(8,128)(2,1)S(1)}, bf16[256,1024]{0,1:T(8,128)(2,1)S(1)}, u32[]{:S(2)}, u32[]{:S(2)}) %collective-permute-start.8) | collective-permute-done | bytes 524320 | tf_op jit(solution)/shard_map/ppermute | solution.py:15
  99.8 11.6 %collective-permute-done.10 = bf16[256,1024]{0,1:T(8,128)(2,1)S(1)} collective-permute-done((bf16[256,1024]{0,1:T(8,128)(2,1)S(1)}, bf16[256,1024]{0,1:T(8,128)(2,1)S(1)}, u32[]{:S(2)}, u32[]{:S(2)}) %collective-permute-start.10) | collective-permute-done | bytes 524320 | tf_op jit(solution)/shard_map/ppermute | solution.py:15
  113.0 1.0 copy.20
  114.0 6.5 %all-to-all-start.1 = ((bf16[2,64,4,512]{3,2,0,1:T(4,128)(2,1)}), bf16[2,64,4,512]{3,2,0,1:T(4,128)(2,1)S(1)}, u32[]{:S(2)}, u32[]{:S(2)}) async-start(bf16[2,64,4,512]{3,2,0,1:T(4,128)(2,1)} %copy.20), calls=%async_computation.1 | async-start | bytes 1048576 | tf_op jit(solution)/shard_map/all_to_all | solution.py:148
  120.5 1.5 %broadcast_in_dim.43.clone = bf16[1,2048,512]{2,1,0:T(8,128)(2,1)} broadcast(bf16[]{:T(256)} %constant.102.clone.1), dimensions={} | broadcast | bytes 2097154 | tf_op jit(solution)/shard_map/broadcast_in_dim | solution.py:128
  122.1 1.3 fusion.4
  123.4 1.3 fusion.6
  124.7 1.3 fusion.8
  126.0 1.3 fusion.10
  127.2 10.6 %all-to-all-done.1 = bf16[2,64,4,512]{3,2,0,1:T(4,128)(2,1)S(1)} async-done(((bf16[2,64,4,512]{3,2,0,1:T(4,128)(2,1)}), bf16[2,64,4,512]{3,2,0,1:T(4,128)(2,1)S(1)}, u32[]{:S(2)}, u32[]{:S(2)}) %all-to-all-start.1) | async-done | bytes 524320 | tf_op jit(solution)/shard_map/all_to_all | solution.py:148
  138.1 0.9 convolution_convert_fusion.13
  139.1 0.9 convolution_convert_fusion.14
  (107 shorter events, 25.9 us)
Async XLA Ops:
  0.6 66.8 %copy-start = (bf16[1,2048,512]{2,1,0:T(8,128)(2,1)S(1)}, bf16[1,2048,512]{2,1,0:T(8,128)(2,1)}, u32[]{:S(2)}) copy-start(bf16[1,2048,512]{2,1,0:T(8,128)(2,1)} %param.14) | copy-start | bytes 6291460
  37.0 24.6 %collective-permute-start.1 = (bf16[256,1024]{1,0:T(8,128)(2,1)S(1)}, bf16[256,1024]{1,0:T(8,128)(2,1)S(1)}, u32[]{:S(2)}, u32[]{:S(2)}) collective-permute-start(bf16[256,1024]{1,0:T(8,128)(2,1)S(1)} %reshape.84), channel_id=1, source_target_pairs={{0,3},{1,0},{2,1},{3,2},{4,7},{5,4},{6,5},{7,6},{8,11},{9,8},{10,9... | collective-permute-start | bytes 1572872 | tf_op jit(solution)/shard_map/ppermute | solution.py:15
  39.6 23.5 %collective-permute-start.5 = (bf16[256,1024]{1,0:T(8,128)(2,1)S(1)}, bf16[256,1024]{1,0:T(8,128)(2,1)}, u32[]{:S(2)}, u32[]{:S(2)}) collective-permute-start(bf16[256,1024]{1,0:T(8,128)(2,1)S(1)} %reshape.84), channel_id=1, source_target_pairs={{0,2},{1,3},{2,0},{3,1},{4,6},{5,7},{6,4},{7,5},{8,10},{9,11},{10,... | collective-permute-start | bytes 1572872 | tf_op jit(solution)/shard_map/ppermute | solution.py:15
  40.1 24.2 %collective-permute-start = (bf16[256,1024]{1,0:T(8,128)(2,1)S(1)}, bf16[256,1024]{1,0:T(8,128)(2,1)}, u32[]{:S(2)}, u32[]{:S(2)}) collective-permute-start(bf16[256,1024]{1,0:T(8,128)(2,1)S(1)} %reshape.84), channel_id=1, source_target_pairs={{0,4},{4,0},{8,12},{12,8},{16,20},{20,16},{24,28},{28,24},{32,36},... | collective-permute-start | bytes 1572872 | tf_op jit(solution)/shard_map/ppermute | solution.py:10
  41.0 24.6 %copy-start.2 = (bf16[1,512,2048]{2,1,0:T(8,128)(2,1)S(1)}, bf16[1,512,2048]{2,1,0:T(8,128)(2,1)}, u32[]{:S(2)}) copy-start(bf16[1,512,2048]{2,1,0:T(8,128)(2,1)} %param.15) | copy-start | bytes 6291460
  41.0 25.2 %collective-permute-start.3 = (bf16[256,1024]{1,0:T(8,128)(2,1)S(1)}, bf16[256,1024]{1,0:T(8,128)(2,1)S(1)}, u32[]{:S(2)}, u32[]{:S(2)}) collective-permute-start(bf16[256,1024]{1,0:T(8,128)(2,1)S(1)} %reshape.84), channel_id=1, source_target_pairs={{0,1},{1,2},{2,3},{3,0},{4,5},{5,6},{6,7},{7,4},{8,9},{9,10},{10,1... | collective-permute-start | bytes 1572872 | tf_op jit(solution)/shard_map/ppermute | solution.py:15
  61.7 7.2 %collective-permute-start.2 = (bf16[256,1024]{1,0:T(8,128)(2,1)S(1)}, bf16[256,1024]{1,0:T(8,128)(2,1)S(1)}, u32[]{:S(2)}, u32[]{:S(2)}) collective-permute-start(bf16[256,1024]{1,0:T(8,128)(2,1)S(1)} %collective-permute-done.1), channel_id=1, source_target_pairs={{0,4},{4,0},{8,12},{12,8},{16,20},{20,16},{24,28},{28,24},{32,36},... | collective-permute-start | bytes 1572872 | tf_op jit(solution)/shard_map/ppermute | solution.py:10
  63.1 4.8 %collective-permute-start.6 = (bf16[256,1024]{1,0:T(8,128)(2,1)}, bf16[256,1024]{1,0:T(8,128)(2,1)S(1)}, u32[]{:S(2)}, u32[]{:S(2)}) collective-permute-start(bf16[256,1024]{1,0:T(8,128)(2,1)} %collective-permute-done.5), channel_id=1, source_target_pairs={{0,4},{4,0},{8,12},{12,8},{16,20},{20,16},{24,28},{28,24},{32,36},... | collective-permute-start | bytes 1572872 | tf_op jit(solution)/shard_map/ppermute | solution.py:10
  64.3 2.7 %copy-start.1 = (bf16[1,2048,512]{2,1,0:T(8,128)(2,1)S(1)}, bf16[1,2048,512]{2,1,0:T(8,128)(2,1)}, u32[]{:S(2)}) copy-start(bf16[1,2048,512]{2,1,0:T(8,128)(2,1)} %param.13) | copy-start | bytes 6291460
  65.5 17.3 %copy-start.5 = (bf16[512,1024]{1,0:T(8,128)(2,1)}, bf16[512,1024]{1,0:T(8,128)(2,1)S(1)}, u32[]{:S(2)}) copy-start(bf16[512,1024]{1,0:T(8,128)(2,1)S(1)} %constant_dynamic-update-slice_fusion) | copy-start | bytes 3145732
  66.2 4.5 %collective-permute-start.4 = (bf16[256,1024]{1,0:T(8,128)(2,1)S(1)}, bf16[256,1024]{1,0:T(8,128)(2,1)S(1)}, u32[]{:S(2)}, u32[]{:S(2)}) collective-permute-start(bf16[256,1024]{1,0:T(8,128)(2,1)S(1)} %collective-permute-done.3), channel_id=1, source_target_pairs={{0,4},{4,0},{8,12},{12,8},{16,20},{20,16},{24,28},{28,24},{32,36},... | collective-permute-start | bytes 1572872 | tf_op jit(solution)/shard_map/ppermute | solution.py:10
  67.9 21.8 %copy-start.3 = (bf16[512,1024]{1,0:T(8,128)(2,1)}, bf16[512,1024]{1,0:T(8,128)(2,1)S(1)}, u32[]{:S(2)}) copy-start(bf16[512,1024]{1,0:T(8,128)(2,1)S(1)} %constant_dynamic-update-slice_fusion.6) | copy-start | bytes 3145732
  68.9 14.4 %copy-start.7 = (bf16[512,1024]{1,0:T(8,128)(2,1)}, bf16[512,1024]{1,0:T(8,128)(2,1)S(1)}, u32[]{:S(2)}) copy-start(bf16[512,1024]{1,0:T(8,128)(2,1)S(1)} %constant_dynamic-update-slice_fusion.2) | copy-start | bytes 3145732
  70.8 18.4 %copy-start.9 = (bf16[512,1024]{1,0:T(8,128)(2,1)}, bf16[512,1024]{1,0:T(8,128)(2,1)S(1)}, u32[]{:S(2)}) copy-start(bf16[512,1024]{1,0:T(8,128)(2,1)S(1)} %constant_dynamic-update-slice_fusion.4) | copy-start | bytes 3145732
  78.3 6.1 %collective-permute-start.7 = (f32[256,1024]{0,1:T(8,128)S(1)}, f32[256,1024]{0,1:T(8,128)S(1)}, u32[]{:S(2)}, u32[]{:S(2)}) collective-permute-start(f32[256,1024]{0,1:T(8,128)S(1)} %pad_maximum_fusion.3), channel_id=1, source_target_pairs={{0,4},{4,0},{8,12},{12,8},{16,20},{20,16},{24,28},{28,24},{32,36},... | collective-permute-start | bytes 3145736 | tf_op jit(solution)/shard_map/ppermute | solution.py:10
  79.1 6.2 %collective-permute-start.9 = (f32[256,1024]{0,1:T(8,128)S(1)}, f32[256,1024]{0,1:T(8,128)S(1)}, u32[]{:S(2)}, u32[]{:S(2)}) collective-permute-start(f32[256,1024]{0,1:T(8,128)S(1)} %pad_maximum_fusion.2), channel_id=1, source_target_pairs={{0,4},{4,0},{8,12},{12,8},{16,20},{20,16},{24,28},{28,24},{32,36},... | collective-permute-start | bytes 3145736 | tf_op jit(solution)/shard_map/ppermute | solution.py:10
  80.2 8.7 %collective-permute-start.11 = (f32[256,1024]{0,1:T(8,128)S(1)}, f32[256,1024]{0,1:T(8,128)S(1)}, u32[]{:S(2)}, u32[]{:S(2)}) collective-permute-start(f32[256,1024]{0,1:T(8,128)S(1)} %pad_maximum_fusion.1), channel_id=1, source_target_pairs={{0,4},{4,0},{8,12},{12,8},{16,20},{20,16},{24,28},{28,24},{32,36},... | collective-permute-start | bytes 3145736 | tf_op jit(solution)/shard_map/ppermute | solution.py:10
  81.0 9.2 %collective-permute-start.13 = (f32[256,1024]{0,1:T(8,128)S(1)}, f32[256,1024]{0,1:T(8,128)S(1)}, u32[]{:S(2)}, u32[]{:S(2)}) collective-permute-start(f32[256,1024]{0,1:T(8,128)S(1)} %pad_maximum_fusion), channel_id=1, source_target_pairs={{0,4},{4,0},{8,12},{12,8},{16,20},{20,16},{24,28},{28,24},{32,36},... | collective-permute-start | bytes 3145736 | tf_op jit(solution)/shard_map/ppermute | solution.py:10
  84.7 15.1 %collective-permute-start.8 = (bf16[256,1024]{0,1:T(8,128)(2,1)S(1)}, bf16[256,1024]{0,1:T(8,128)(2,1)S(1)}, u32[]{:S(2)}, u32[]{:S(2)}) collective-permute-start(bf16[256,1024]{0,1:T(8,128)(2,1)S(1)} %fusion.40), channel_id=1, source_target_pairs={{0,2},{1,3},{2,0},{3,1},{4,6},{5,7},{6,4},{7,5},{8,10},{9,11},{10,... | collective-permute-start | bytes 1572872 | tf_op jit(solution)/shard_map/ppermute | solution.py:15
  85.5 25.8 %collective-permute-start.10 = (bf16[256,1024]{0,1:T(8,128)(2,1)S(1)}, bf16[256,1024]{0,1:T(8,128)(2,1)S(1)}, u32[]{:S(2)}, u32[]{:S(2)}) collective-permute-start(bf16[256,1024]{0,1:T(8,128)(2,1)S(1)} %fusion.37), channel_id=1, source_target_pairs={{0,1},{1,2},{2,3},{3,0},{4,5},{5,6},{6,7},{7,4},{8,9},{9,10},{10,1... | collective-permute-start | bytes 1572872 | tf_op jit(solution)/shard_map/ppermute | solution.py:15
  89.1 22.7 %collective-permute-start.12 = (bf16[256,1024]{0,1:T(8,128)(2,1)S(1)}, bf16[256,1024]{0,1:T(8,128)(2,1)S(1)}, u32[]{:S(2)}, u32[]{:S(2)}) collective-permute-start(bf16[256,1024]{0,1:T(8,128)(2,1)S(1)} %fusion.34), channel_id=1, source_target_pairs={{0,3},{1,0},{2,1},{3,2},{4,7},{5,4},{6,5},{7,6},{8,11},{9,8},{10,9... | collective-permute-start | bytes 1572872 | tf_op jit(solution)/shard_map/ppermute | solution.py:15
  90.2 22.0 %copy-start.12 = (bf16[1,2048,512]{2,1,0:T(8,128)(2,1)}, bf16[1,2048,512]{2,1,0:T(8,128)(2,1)S(1)}, u32[]{:S(2)}) copy-start(bf16[1,2048,512]{2,1,0:T(8,128)(2,1)S(1)} %fusion.18) | copy-start | bytes 6291460
  114.0 23.8 %all-to-all-start.1 = ((bf16[2,64,4,512]{3,2,0,1:T(4,128)(2,1)}), bf16[2,64,4,512]{3,2,0,1:T(4,128)(2,1)S(1)}, u32[]{:S(2)}, u32[]{:S(2)}) async-start(bf16[2,64,4,512]{3,2,0,1:T(4,128)(2,1)} %copy.20), calls=%async_computation.1 | async-start | bytes 1048576 | tf_op jit(solution)/shard_map/all_to_all | solution.py:148
  120.5 2.9 %copy-start.8 = (bf16[512,1024]{1,0:T(8,128)(2,1)S(1)}, bf16[512,1024]{1,0:T(8,128)(2,1)}, u32[]{:S(2)}) copy-start(bf16[512,1024]{1,0:T(8,128)(2,1)} %copy-done.7) | copy-start | bytes 3145732
  (4 other events, 8.0 us)

commit v12 on v11

--- a/solution.py
+++ b/solution.py
@@ -37,13 +37,9 @@
     ).astype(jnp.float32)
     tok_scale = jnp.sum(dom_hot * domain_weights[None, :], axis=1)
     grad_rows = (tok_scale[:, None] * cotangent.astype(jnp.float32)).astype(jnp.bfloat16)
-    lab_hot = (lang_label[:, None] == jnp.arange(experts_all, dtype=jnp.int32)[None, :]).astype(
-        jnp.float32
-    )
     row_ids = jnp.arange(tok_rows, dtype=jnp.int32)
-    earlier = (row_ids[None, :] < row_ids[:, None]).astype(jnp.float32)
-    before = jnp.dot(earlier, lab_hot, preferred_element_type=jnp.float32)
-    slot_pos = jnp.sum(before * lab_hot, axis=1).astype(jnp.int32)
+    same_before = (lang_label[None, :] == lang_label[:, None]) & (row_ids[None, :] < row_ids[:, None])
+    slot_pos = jnp.sum(same_before.astype(jnp.int32), axis=1)
     target_row = lang_label * capacity + slot_pos
     rows_out = n_expert * half_cap
     sources = jnp.concatenate((tokens, grad_rows), axis=1)

time: 140 us -> 140 us (level)
  no operation moved by 1% of the time
where the time goes in v12:
time: 140 us
  waiting for transfers between devices  52.5 us (38%)
  blocking collectives  30.4 us (22%)
  matrix products  23.5 us (17%)
  starting transfers between devices  18.9 us (13%)
  local copies, waits for them, and re-layouts  8.29 us (6%)
  other arithmetic  5.18 us (4%)
    ppermute x6, waiting for transfers between devices, shifted(): lax.ppermute(value, axis, [(i, (i + step) % size) for i in range(size)])  41.9 us
    all_to_all x1, blocking collectives, body(): lax.all_to_all(outbound, 'expert', split_axis=0, concat_axis=0, tiled=True)  30.4 us
    all_to_all x1, waiting for transfers between devices, body(): lax.all_to_all(going_back, 'expert', split_axis=1, concat_axis=1, tiled=T...  10.6 us
    ppermute x6, starting transfers between devices, shifted(): lax.ppermute(value, axis, [(i, (i + step) % size) for i in range(size)])  7.72 us
    all_to_all x1, starting transfers between devices, body(): lax.all_to_all(going_back, 'expert', split_axis=1, concat_axis=1, tiled=T...  6.48 us
    dot_general x4, matrix products, body(): lax.dot_general(b[0], grad_gate_pre, contract_rows, preferred_element_typ...  5.12 us
    ppermute x8, starting transfers between devices, partner(): lax.ppermute(value, axis, [(i, i ^ 1 << stride) for i in range(lax.axis_s...  4.7 us
  transfers between devices with their start and end apart: 15, of which 6 were waited for; matrix products, arithmetic and copies ran while one was open for 13% of the time, Pallas kernels for 0%

profile of v12, /device:TPU:1, one launch (start us, length us, event | category | flops | bytes accessed | tf_op | source)
XLA Modules:
  0.0 139.9 jit_solution(10736525917106821613)
XLA Ops:
  0.6 1.0 convert_reduce_fusion
  3.1 1.0 multiply_convert_fusion.3
  4.1 1.2 convolution_convert_fusion.12
  5.5 30.4 %all_to_all.10 = bf16[64,4,1024]{2,1,0:T(4,128)(2,1)} all-to-all(bf16[64,4,1024]{2,1,0:T(4,128)(2,1)S(1)} %reshape.83), channel_id=1, replica_groups=mesh['expert'=64,'tensor'=4] {'expert'}, dimensions={0} | all-to-all | bytes 1048576 | tf_op jit(solution)/shard_map/all_to_all | solution.py:53
  35.8 1.2 reshape.84
  37.0 2.6 %collective-permute-start.1 = (bf16[256,1024]{1,0:T(8,128)(2,1)S(1)}, bf16[256,1024]{1,0:T(8,128)(2,1)S(1)}, u32[]{:S(2)}, u32[]{:S(2)}) collective-permute-start(bf16[256,1024]{1,0:T(8,128)(2,1)S(1)} %reshape.84), channel_id=1, source_target_pairs={{0,3},{1,0},{2,1},{3,2},{4,7},{5,4},{6,5},{7,6},{8,11},{9,8},{10,9... | collective-permute-start | bytes 1572872 | tf_op jit(solution)/shard_map/ppermute | solution.py:15
  40.1 0.9 collective-permute-start
  41.6 20.0 %collective-permute-done.1 = bf16[256,1024]{1,0:T(8,128)(2,1)S(1)} collective-permute-done((bf16[256,1024]{1,0:T(8,128)(2,1)S(1)}, bf16[256,1024]{1,0:T(8,128)(2,1)S(1)}, u32[]{:S(2)}, u32[]{:S(2)}) %collective-permute-start.1) | collective-permute-done | bytes 524320 | tf_op jit(solution)/shard_map/ppermute | solution.py:15
  61.7 1.4 %collective-permute-start.2 = (bf16[256,1024]{1,0:T(8,128)(2,1)S(1)}, bf16[256,1024]{1,0:T(8,128)(2,1)S(1)}, u32[]{:S(2)}, u32[]{:S(2)}) collective-permute-start(bf16[256,1024]{1,0:T(8,128)(2,1)S(1)} %collective-permute-done.1), channel_id=1, source_target_pairs={{0,4},{4,0},{8,12},{12,8},{16,20},{20,16},{24,28},{28,24},{32,36},... | collective-permute-start | bytes 1572872 | tf_op jit(solution)/shard_map/ppermute | solution.py:10
  63.2 1.1 constant_dynamic-update-slice_fusion.7
  64.3 1.2 constant_dynamic-update-slice_fusion
  85.5 3.3 %collective-permute-start.10 = (bf16[256,1024]{0,1:T(8,128)(2,1)S(1)}, bf16[256,1024]{0,1:T(8,128)(2,1)S(1)}, u32[]{:S(2)}, u32[]{:S(2)}) collective-permute-start(bf16[256,1024]{0,1:T(8,128)(2,1)S(1)} %fusion.36), channel_id=1, source_target_pairs={{0,1},{1,2},{2,3},{3,0},{4,5},{5,6},{6,7},{7,4},{8,9},{9,10},{10,1... | collective-permute-start | bytes 1572872 | tf_op jit(solution)/shard_map/ppermute | solution.py:15
  90.2 9.6 %collective-permute-done.8 = bf16[256,1024]{0,1:T(8,128)(2,1)S(1)} collective-permute-done((bf16[256,1024]{0,1:T(8,128)(2,1)S(1)}, bf16[256,1024]{0,1:T(8,128)(2,1)S(1)}, u32[]{:S(2)}, u32[]{:S(2)}) %collective-permute-start.8) | collective-permute-done | bytes 524320 | tf_op jit(solution)/shard_map/ppermute | solution.py:15
  99.8 11.6 %collective-permute-done.10 = bf16[256,1024]{0,1:T(8,128)(2,1)S(1)} collective-permute-done((bf16[256,1024]{0,1:T(8,128)(2,1)S(1)}, bf16[256,1024]{0,1:T(8,128)(2,1)S(1)}, u32[]{:S(2)}, u32[]{:S(2)}) %collective-permute-start.10) | collective-permute-done | bytes 524320 | tf_op jit(solution)/shard_map/ppermute | solution.py:15
  113.0 1.0 copy.20
  114.0 6.5 %all-to-all-start.1 = ((bf16[2,64,4,512]{3,2,0,1:T(4,128)(2,1)}), bf16[2,64,4,512]{3,2,0,1:T(4,128)(2,1)S(1)}, u32[]{:S(2)}, u32[]{:S(2)}) async-start(bf16[2,64,4,512]{3,2,0,1:T(4,128)(2,1)} %copy.20), calls=%async_computation.1 | async-start | bytes 1048576 | tf_op jit(solution)/shard_map/all_to_all | solution.py:144
  120.5 1.5 %broadcast_in_dim.42.clone = bf16[1,2048,512]{2,1,0:T(8,128)(2,1)} broadcast(bf16[]{:T(256)} %constant.101.clone.1), dimensions={} | broadcast | bytes 2097154 | tf_op jit(solution)/shard_map/broadcast_in_dim | solution.py:124
  122.1 1.3 fusion.4
  123.4 1.3 fusion.6
  124.7 1.3 fusion.8
  126.0 1.3 fusion.10
  127.2 10.6 %all-to-all-done.1 = bf16[2,64,4,512]{3,2,0,1:T(4,128)(2,1)S(1)} async-done(((bf16[2,64,4,512]{3,2,0,1:T(4,128)(2,1)}), bf16[2,64,4,512]{3,2,0,1:T(4,128)(2,1)S(1)}, u32[]{:S(2)}, u32[]{:S(2)}) %all-to-all-start.1) | async-done | bytes 524320 | tf_op jit(solution)/shard_map/all_to_all | solution.py:144
  138.1 0.9 convolution_convert_fusion.13
  139.1 0.9 convolution_convert_fusion.14
  (107 shorter events, 25.9 us)
Async XLA Ops:
  0.6 66.8 %copy-start = (bf16[1,2048,512]{2,1,0:T(8,128)(2,1)S(1)}, bf16[1,2048,512]{2,1,0:T(8,128)(2,1)}, u32[]{:S(2)}) copy-start(bf16[1,2048,512]{2,1,0:T(8,128)(2,1)} %param.14) | copy-start | bytes 6291460
  37.0 24.6 %collective-permute-start.1 = (bf16[256,1024]{1,0:T(8,128)(2,1)S(1)}, bf16[256,1024]{1,0:T(8,128)(2,1)S(1)}, u32[]{:S(2)}, u32[]{:S(2)}) collective-permute-start(bf16[256,1024]{1,0:T(8,128)(2,1)S(1)} %reshape.84), channel_id=1, source_target_pairs={{0,3},{1,0},{2,1},{3,2},{4,7},{5,4},{6,5},{7,6},{8,11},{9,8},{10,9... | collective-permute-start | bytes 1572872 | tf_op jit(solution)/shard_map/ppermute | solution.py:15
  39.6 23.5 %collective-permute-start.5 = (bf16[256,1024]{1,0:T(8,128)(2,1)S(1)}, bf16[256,1024]{1,0:T(8,128)(2,1)}, u32[]{:S(2)}, u32[]{:S(2)}) collective-permute-start(bf16[256,1024]{1,0:T(8,128)(2,1)S(1)} %reshape.84), channel_id=1, source_target_pairs={{0,2},{1,3},{2,0},{3,1},{4,6},{5,7},{6,4},{7,5},{8,10},{9,11},{10,... | collective-permute-start | bytes 1572872 | tf_op jit(solution)/shard_map/ppermute | solution.py:15
  40.1 24.2 %collective-permute-start = (bf16[256,1024]{1,0:T(8,128)(2,1)S(1)}, bf16[256,1024]{1,0:T(8,128)(2,1)}, u32[]{:S(2)}, u32[]{:S(2)}) collective-permute-start(bf16[256,1024]{1,0:T(8,128)(2,1)S(1)} %reshape.84), channel_id=1, source_target_pairs={{0,4},{4,0},{8,12},{12,8},{16,20},{20,16},{24,28},{28,24},{32,36},... | collective-permute-start | bytes 1572872 | tf_op jit(solution)/shard_map/ppermute | solution.py:10
  41.0 24.6 %copy-start.2 = (bf16[1,512,2048]{2,1,0:T(8,128)(2,1)S(1)}, bf16[1,512,2048]{2,1,0:T(8,128)(2,1)}, u32[]{:S(2)}) copy-start(bf16[1,512,2048]{2,1,0:T(8,128)(2,1)} %param.15) | copy-start | bytes 6291460
  41.0 25.2 %collective-permute-start.3 = (bf16[256,1024]{1,0:T(8,128)(2,1)S(1)}, bf16[256,1024]{1,0:T(8,128)(2,1)S(1)}, u32[]{:S(2)}, u32[]{:S(2)}) collective-permute-start(bf16[256,1024]{1,0:T(8,128)(2,1)S(1)} %reshape.84), channel_id=1, source_target_pairs={{0,1},{1,2},{2,3},{3,0},{4,5},{5,6},{6,7},{7,4},{8,9},{9,10},{10,1... | collective-permute-start | bytes 1572872 | tf_op jit(solution)/shard_map/ppermute | solution.py:15
  61.7 7.2 %collective-permute-start.2 = (bf16[256,1024]{1,0:T(8,128)(2,1)S(1)}, bf16[256,1024]{1,0:T(8,128)(2,1)S(1)}, u32[]{:S(2)}, u32[]{:S(2)}) collective-permute-start(bf16[256,1024]{1,0:T(8,128)(2,1)S(1)} %collective-permute-done.1), channel_id=1, source_target_pairs={{0,4},{4,0},{8,12},{12,8},{16,20},{20,16},{24,28},{28,24},{32,36},... | collective-permute-start | bytes 1572872 | tf_op jit(solution)/shard_map/ppermute | solution.py:10
  63.1 4.8 %collective-permute-start.6 = (bf16[256,1024]{1,0:T(8,128)(2,1)}, bf16[256,1024]{1,0:T(8,128)(2,1)S(1)}, u32[]{:S(2)}, u32[]{:S(2)}) collective-permute-start(bf16[256,1024]{1,0:T(8,128)(2,1)} %collective-permute-done.5), channel_id=1, source_target_pairs={{0,4},{4,0},{8,12},{12,8},{16,20},{20,16},{24,28},{28,24},{32,36},... | collective-permute-start | bytes 1572872 | tf_op jit(solution)/shard_map/ppermute | solution.py:10
  64.3 2.7 %copy-start.1 = (bf16[1,2048,512]{2,1,0:T(8,128)(2,1)S(1)}, bf16[1,2048,512]{2,1,0:T(8,128)(2,1)}, u32[]{:S(2)}) copy-start(bf16[1,2048,512]{2,1,0:T(8,128)(2,1)} %param.13) | copy-start | bytes 6291460
  65.5 17.3 %copy-start.5 = (bf16[512,1024]{1,0:T(8,128)(2,1)}, bf16[512,1024]{1,0:T(8,128)(2,1)S(1)}, u32[]{:S(2)}) copy-start(bf16[512,1024]{1,0:T(8,128)(2,1)S(1)} %constant_dynamic-update-slice_fusion) | copy-start | bytes 3145732
  66.2 4.5 %collective-permute-start.4 = (bf16[256,1024]{1,0:T(8,128)(2,1)S(1)}, bf16[256,1024]{1,0:T(8,128)(2,1)S(1)}, u32[]{:S(2)}, u32[]{:S(2)}) collective-permute-start(bf16[256,1024]{1,0:T(8,128)(2,1)S(1)} %collective-permute-done.3), channel_id=1, source_target_pairs={{0,4},{4,0},{8,12},{12,8},{16,20},{20,16},{24,28},{28,24},{32,36},... | collective-permute-start | bytes 1572872 | tf_op jit(solution)/shard_map/ppermute | solution.py:10
  67.9 21.8 %copy-start.3 = (bf16[512,1024]{1,0:T(8,128)(2,1)}, bf16[512,1024]{1,0:T(8,128)(2,1)S(1)}, u32[]{:S(2)}) copy-start(bf16[512,1024]{1,0:T(8,128)(2,1)S(1)} %constant_dynamic-update-slice_fusion.6) | copy-start | bytes 3145732
  68.9 14.4 %copy-start.7 = (bf16[512,1024]{1,0:T(8,128)(2,1)}, bf16[512,1024]{1,0:T(8,128)(2,1)S(1)}, u32[]{:S(2)}) copy-start(bf16[512,1024]{1,0:T(8,128)(2,1)S(1)} %constant_dynamic-update-slice_fusion.2) | copy-start | bytes 3145732
  70.8 18.4 %copy-start.9 = (bf16[512,1024]{1,0:T(8,128)(2,1)}, bf16[512,1024]{1,0:T(8,128)(2,1)S(1)}, u32[]{:S(2)}) copy-start(bf16[512,1024]{1,0:T(8,128)(2,1)S(1)} %constant_dynamic-update-slice_fusion.4) | copy-start | bytes 3145732
  78.4 6.1 %collective-permute-start.7 = (f32[256,1024]{0,1:T(8,128)S(1)}, f32[256,1024]{0,1:T(8,128)S(1)}, u32[]{:S(2)}, u32[]{:S(2)}) collective-permute-start(f32[256,1024]{0,1:T(8,128)S(1)} %pad_maximum_fusion.3), channel_id=1, source_target_pairs={{0,4},{4,0},{8,12},{12,8},{16,20},{20,16},{24,28},{28,24},{32,36},... | collective-permute-start | bytes 3145736 | tf_op jit(solution)/shard_map/ppermute | solution.py:10
  79.1 6.2 %collective-permute-start.9 = (f32[256,1024]{0,1:T(8,128)S(1)}, f32[256,1024]{0,1:T(8,128)S(1)}, u32[]{:S(2)}, u32[]{:S(2)}) collective-permute-start(f32[256,1024]{0,1:T(8,128)S(1)} %pad_maximum_fusion.2), channel_id=1, source_target_pairs={{0,4},{4,0},{8,12},{12,8},{16,20},{20,16},{24,28},{28,24},{32,36},... | collective-permute-start | bytes 3145736 | tf_op jit(solution)/shard_map/ppermute | solution.py:10
  80.2 8.7 %collective-permute-start.11 = (f32[256,1024]{0,1:T(8,128)S(1)}, f32[256,1024]{0,1:T(8,128)S(1)}, u32[]{:S(2)}, u32[]{:S(2)}) collective-permute-start(f32[256,1024]{0,1:T(8,128)S(1)} %pad_maximum_fusion.1), channel_id=1, source_target_pairs={{0,4},{4,0},{8,12},{12,8},{16,20},{20,16},{24,28},{28,24},{32,36},... | collective-permute-start | bytes 3145736 | tf_op jit(solution)/shard_map/ppermute | solution.py:10
  81.0 9.2 %collective-permute-start.13 = (f32[256,1024]{0,1:T(8,128)S(1)}, f32[256,1024]{0,1:T(8,128)S(1)}, u32[]{:S(2)}, u32[]{:S(2)}) collective-permute-start(f32[256,1024]{0,1:T(8,128)S(1)} %pad_maximum_fusion), channel_id=1, source_target_pairs={{0,4},{4,0},{8,12},{12,8},{16,20},{20,16},{24,28},{28,24},{32,36},... | collective-permute-start | bytes 3145736 | tf_op jit(solution)/shard_map/ppermute | solution.py:10
  84.7 15.1 %collective-permute-start.8 = (bf16[256,1024]{0,1:T(8,128)(2,1)S(1)}, bf16[256,1024]{0,1:T(8,128)(2,1)S(1)}, u32[]{:S(2)}, u32[]{:S(2)}) collective-permute-start(bf16[256,1024]{0,1:T(8,128)(2,1)S(1)} %fusion.39), channel_id=1, source_target_pairs={{0,2},{1,3},{2,0},{3,1},{4,6},{5,7},{6,4},{7,5},{8,10},{9,11},{10,... | collective-permute-start | bytes 1572872 | tf_op jit(solution)/shard_map/ppermute | solution.py:15
  85.5 25.8 %collective-permute-start.10 = (bf16[256,1024]{0,1:T(8,128)(2,1)S(1)}, bf16[256,1024]{0,1:T(8,128)(2,1)S(1)}, u32[]{:S(2)}, u32[]{:S(2)}) collective-permute-start(bf16[256,1024]{0,1:T(8,128)(2,1)S(1)} %fusion.36), channel_id=1, source_target_pairs={{0,1},{1,2},{2,3},{3,0},{4,5},{5,6},{6,7},{7,4},{8,9},{9,10},{10,1... | collective-permute-start | bytes 1572872 | tf_op jit(solution)/shard_map/ppermute | solution.py:15
  89.1 22.7 %collective-permute-start.12 = (bf16[256,1024]{0,1:T(8,128)(2,1)S(1)}, bf16[256,1024]{0,1:T(8,128)(2,1)S(1)}, u32[]{:S(2)}, u32[]{:S(2)}) collective-permute-start(bf16[256,1024]{0,1:T(8,128)(2,1)S(1)} %fusion.33), channel_id=1, source_target_pairs={{0,3},{1,0},{2,1},{3,2},{4,7},{5,4},{6,5},{7,6},{8,11},{9,8},{10,9... | collective-permute-start | bytes 1572872 | tf_op jit(solution)/shard_map/ppermute | solution.py:15
  90.2 22.0 %copy-start.12 = (bf16[1,2048,512]{2,1,0:T(8,128)(2,1)}, bf16[1,2048,512]{2,1,0:T(8,128)(2,1)S(1)}, u32[]{:S(2)}) copy-start(bf16[1,2048,512]{2,1,0:T(8,128)(2,1)S(1)} %fusion.18) | copy-start | bytes 6291460
  114.0 23.8 %all-to-all-start.1 = ((bf16[2,64,4,512]{3,2,0,1:T(4,128)(2,1)}), bf16[2,64,4,512]{3,2,0,1:T(4,128)(2,1)S(1)}, u32[]{:S(2)}, u32[]{:S(2)}) async-start(bf16[2,64,4,512]{3,2,0,1:T(4,128)(2,1)} %copy.20), calls=%async_computation.1 | async-start | bytes 1048576 | tf_op jit(solution)/shard_map/all_to_all | solution.py:144
  120.5 2.9 %copy-start.8 = (bf16[512,1024]{1,0:T(8,128)(2,1)S(1)}, bf16[512,1024]{1,0:T(8,128)(2,1)}, u32[]{:S(2)}) copy-start(bf16[512,1024]{1,0:T(8,128)(2,1)} %copy-done.7) | copy-start | bytes 3145732
  (4 other events, 8.0 us)

commit v13 on v11

--- a/solution.py
+++ b/solution.py
@@ -46,16 +46,17 @@
     slot_pos = jnp.sum(before * lab_hot, axis=1).astype(jnp.int32)
     target_row = lang_label * capacity + slot_pos
     rows_out = n_expert * half_cap
-    sources = jnp.concatenate((tokens, grad_rows), axis=1)
+    stacked = jnp.stack((tokens, grad_rows))
     dispatch_map = (
         jnp.arange(rows_out, dtype=jnp.int32)[:, None] == target_row[None, :]
     ).astype(jnp.bfloat16)
-    outbound = jnp.dot(dispatch_map, sources, preferred_element_type=jnp.float32).astype(
-        jnp.bfloat16
-    )
-    outbound = outbound.reshape(n_expert, half_cap, 2 * feat_slice)
-    arrived = lax.all_to_all(outbound, "expert", split_axis=0, concat_axis=0, tiled=True)
-    own_piece = arrived.reshape(rows_out, 2 * feat_slice)
+    outbound = jnp.einsum(
+        "rt,ktw->krw", dispatch_map, stacked, preferred_element_type=jnp.float32
+    ).astype(jnp.bfloat16)
+    outbound = outbound.reshape(2, n_expert, half_cap, feat_slice)
+    arrived = lax.all_to_all(outbound, "expert", split_axis=1, concat_axis=1, tiled=True)
+    arrived = arrived.reshape(2, rows_out, feat_slice)
+    own_piece = jnp.concatenate((arrived[0], arrived[1]), axis=1)
     order = sorted(range(n_tensor), key=lambda k: -min(k, n_tensor - k))
     received = {k: shifted(own_piece, "tensor", k) for k in order if k}
     order = [0] + [k for k in reversed(order) if k]

time: 140 us -> 152 us (1.086)
  local copies, waits for them, and re-layouts: 8.29 us -> 13.4 us
  waiting for transfers between devices: 52.5 us -> 55.6 us
  matrix products: 24.4 us -> 26.5 us
  other arithmetic: 4.2 us -> 6.26 us
    ppermute x6, waiting for transfers between devices: 41.9 us -> 44.9 us  [shifted(): lax.ppermute(value, axis, [(i, (i + step) % size) for i in range(size)])]
    slice x3, local copies, waits for them, and re-layouts: 0.32 us -> 3.02 us  [body(): going_back = jnp.stack((acc[:, :feat_slice], acc[:, feat_slice:]))]
    unnamed x30, local copies, waits for them, and re-layouts: 2.01 us -> 3.94 us
  transfers between devices with their start and end apart: 15 -> 15, of which waited for: 6 -> 5; matrix products, arithmetic and copies ran while one was open for 13% -> 14% of each run, Pallas kernels for 0% -> 0%
where the time goes in v13:
time: 152 us; the launch traced here: 151 us
  waiting for transfers between devices  55.6 us (37%)
  blocking collectives  30.3 us (20%)
  matrix products  26.5 us (17%)
  starting transfers between devices  18 us (12%)
  local copies, waits for them, and re-layouts  13.4 us (9%)
  other arithmetic  6.26 us (4%)
    ppermute x6, waiting for transfers between devices, shifted(): lax.ppermute(value, axis, [(i, (i + step) % size) for i in range(size)])  44.9 us
    all_to_all x1, blocking collectives, body(): lax.all_to_all(outbound, 'expert', split_axis=1, concat_axis=1, tiled=True)  30.3 us
    all_to_all x1, waiting for transfers between devices, body(): lax.all_to_all(going_back, 'expert', split_axis=1, concat_axis=1, tiled=T...  10.7 us
    ppermute x6, starting transfers between devices, shifted(): lax.ppermute(value, axis, [(i, (i + step) % size) for i in range(size)])  7.12 us
    all_to_all x1, starting transfers between devices, body(): lax.all_to_all(going_back, 'expert', split_axis=1, concat_axis=1, tiled=T...  6.27 us
    dot_general x4, matrix products, body(): lax.dot_general(b[0], grad_gate_pre, contract_rows, preferred_element_typ...  5.06 us
    ppermute x8, starting transfers between devices, partner(): lax.ppermute(value, axis, [(i, i ^ 1 << stride) for i in range(lax.axis_s...  4.58 us
    unnamed x30, local copies, waits for them, and re-layouts  3.94 us
  transfers between devices with their start and end apart: 15, of which 5 were waited for; matrix products, arithmetic and copies ran while one was open for 14% of the time, Pallas kernels for 0%

profile of v13, /device:TPU:1, one launch (start us, length us, event | category | flops | bytes accessed | tf_op | source)
XLA Modules:
  0.0 151.2 jit_solution(18092828701676814368)
XLA Ops:
  4.0 1.2 fusion.3
  5.6 30.3 %all_to_all.10 = bf16[2,64,4,512]{3,2,0,1:T(4,128)(2,1)S(1)} all-to-all(bf16[2,64,4,512]{3,2,0,1:T(4,128)(2,1)S(1)} %copy.19), channel_id=1, replica_groups=mesh['expert'=64,'tensor'=4] {'expert'}, dimensions={1} | all-to-all | bytes 1048576 | tf_op jit(solution)/shard_map/all_to_all | solution.py:57
  36.3 2.6 %collective-permute-start.1 = (bf16[256,1024]{1,0:T(8,128)(2,1)S(1)}, bf16[256,1024]{1,0:T(8,128)(2,1)}, u32[]{:S(2)}, u32[]{:S(2)}) collective-permute-start(bf16[256,1024]{1,0:T(8,128)(2,1)S(1)} %constant_dynamic-update-slice_fusion), channel_id=1, source_target_pairs={{0,3},{1,0},{2,1},{3,2},{4,7},{5,4},{6,5},{7,6},{8,11},{9,8},{10,9... | collective-permute-start | bytes 1572872 | tf_op jit(solution)/shard_map/ppermute | solution.py:15
  39.9 1.2 collective-permute-start
  41.1 19.8 %collective-permute-done.1 = bf16[256,1024]{1,0:T(8,128)(2,1)} collective-permute-done((bf16[256,1024]{1,0:T(8,128)(2,1)S(1)}, bf16[256,1024]{1,0:T(8,128)(2,1)}, u32[]{:S(2)}, u32[]{:S(2)}) %collective-permute-start.1) | collective-permute-done | bytes 524320 | tf_op jit(solution)/shard_map/ppermute | solution.py:15
  60.9 1.3 collective-permute-start.2
  62.2 3.3 %collective-permute-done.3 = bf16[256,1024]{1,0:T(8,128)(2,1)} collective-permute-done((bf16[256,1024]{1,0:T(8,128)(2,1)S(1)}, bf16[256,1024]{1,0:T(8,128)(2,1)}, u32[]{:S(2)}, u32[]{:S(2)}) %collective-permute-start.3) | collective-permute-done | bytes 524320 | tf_op jit(solution)/shard_map/ppermute | solution.py:15
  67.1 1.2 constant_dynamic-update-slice_fusion.7
  70.4 1.6 %fusion.63 = f32[512,512]{1,0:T(8,128)S(1)} fusion(bf16[1,512,2048]{2,1,0:T(8,128)(2,1)S(1)} %copy-done.2, s32[]{:T(128)S(6)} %select_n.84, bf16[256,1024]{1,0:T(8,128)(2,1)} %collective-permute-done, bf16[256,1024]{1,0:T(8,128)(2,1)S(1)} %constant_dynamic-update-slice_fusion), kind=kOutput, calls=%fused_computation.109 | convolution fusion | flops 269484032 | bytes 2621444 | tf_op jit(solution)/shard_map/dot_general | solution.py:101
  82.2 1.4 fusion.21
  92.1 2.4 %collective-permute-start.12 = (bf16[256,1024]{0,1:T(8,128)(2,1)S(1)}, bf16[256,1024]{0,1:T(8,128)(2,1)S(1)}, u32[]{:S(2)}, u32[]{:S(2)}) collective-permute-start(bf16[256,1024]{0,1:T(8,128)(2,1)S(1)} %fusion.35), channel_id=1, source_target_pairs={{0,3},{1,0},{2,1},{3,2},{4,7},{5,4},{6,5},{7,6},{8,11},{9,8},{10,9... | collective-permute-start | bytes 1572872 | tf_op jit(solution)/shard_map/ppermute | solution.py:15
  95.4 10.3 %collective-permute-done.8 = bf16[256,1024]{0,1:T(8,128)(2,1)S(1)} collective-permute-done((bf16[256,1024]{0,1:T(8,128)(2,1)S(1)}, bf16[256,1024]{0,1:T(8,128)(2,1)S(1)}, u32[]{:S(2)}, u32[]{:S(2)}) %collective-permute-start.8) | collective-permute-done | bytes 524320 | tf_op jit(solution)/shard_map/ppermute | solution.py:15
  105.7 11.5 %collective-permute-done.10 = bf16[256,1024]{0,1:T(8,128)(2,1)S(1)} collective-permute-done((bf16[256,1024]{0,1:T(8,128)(2,1)S(1)}, bf16[256,1024]{0,1:T(8,128)(2,1)S(1)}, u32[]{:S(2)}, u32[]{:S(2)}) %collective-permute-start.10) | collective-permute-done | bytes 524320 | tf_op jit(solution)/shard_map/ppermute | solution.py:15
  118.4 1.1 copy.20
  120.3 1.1 copy.21
  122.2 1.4 pad_maximum_fusion.5
  124.6 6.3 %all-to-all-start.1 = ((bf16[2,64,4,512]{3,2,0,1:T(4,128)(2,1)}), bf16[2,64,4,512]{3,2,0,1:T(4,128)(2,1)}, u32[]{:S(2)}, u32[]{:S(2)}) async-start(bf16[2,64,4,512]{3,2,0,1:T(4,128)(2,1)} %copy.22), calls=%async_computation.1 | async-start | bytes 1048576 | tf_op jit(solution)/shard_map/all_to_all | solution.py:149
  130.9 1.5 broadcast_in_dim.43.clone
  132.3 1.3 fusion.5
  133.6 1.3 fusion.7
  134.9 1.3 fusion.9
  136.1 1.3 fusion.11
  137.4 10.7 %all-to-all-done.1 = bf16[2,64,4,512]{3,2,0,1:T(4,128)(2,1)} async-done(((bf16[2,64,4,512]{3,2,0,1:T(4,128)(2,1)}), bf16[2,64,4,512]{3,2,0,1:T(4,128)(2,1)}, u32[]{:S(2)}, u32[]{:S(2)}) %all-to-all-start.1) | async-done | bytes 524320 | tf_op jit(solution)/shard_map/all_to_all | solution.py:149
  148.1 1.2 fusion.161
  (111 shorter events, 33.7 us)
Async XLA Ops:
  0.6 71.4 %copy-start = (bf16[1,2048,512]{2,1,0:T(8,128)(2,1)S(1)}, bf16[1,2048,512]{2,1,0:T(8,128)(2,1)}, u32[]{:S(2)}) copy-start(bf16[1,2048,512]{2,1,0:T(8,128)(2,1)} %param.14) | copy-start | bytes 6291460
  36.2 34.2 %copy-start.7 = (bf16[256,1024]{1,0:T(8,128)(2,1)}, bf16[256,1024]{1,0:T(8,128)(2,1)S(1)}, u32[]{:S(2)}) copy-start(bf16[256,1024]{1,0:T(8,128)(2,1)S(1)} %constant_dynamic-update-slice_fusion) | copy-start | bytes 1572868
  36.3 24.6 %collective-permute-start.1 = (bf16[256,1024]{1,0:T(8,128)(2,1)S(1)}, bf16[256,1024]{1,0:T(8,128)(2,1)}, u32[]{:S(2)}, u32[]{:S(2)}) collective-permute-start(bf16[256,1024]{1,0:T(8,128)(2,1)S(1)} %constant_dynamic-update-slice_fusion), channel_id=1, source_target_pairs={{0,3},{1,0},{2,1},{3,2},{4,7},{5,4},{6,5},{7,6},{8,11},{9,8},{10,9... | collective-permute-start | bytes 1572872 | tf_op jit(solution)/shard_map/ppermute | solution.py:15
  38.8 23.4 %collective-permute-start.5 = (bf16[256,1024]{1,0:T(8,128)(2,1)S(1)}, bf16[256,1024]{1,0:T(8,128)(2,1)}, u32[]{:S(2)}, u32[]{:S(2)}) collective-permute-start(bf16[256,1024]{1,0:T(8,128)(2,1)S(1)} %constant_dynamic-update-slice_fusion), channel_id=1, source_target_pairs={{0,2},{1,3},{2,0},{3,1},{4,6},{5,7},{6,4},{7,5},{8,10},{9,11},{10,... | collective-permute-start | bytes 1572872 | tf_op jit(solution)/shard_map/ppermute | solution.py:15
  39.3 26.2 %collective-permute-start.3 = (bf16[256,1024]{1,0:T(8,128)(2,1)S(1)}, bf16[256,1024]{1,0:T(8,128)(2,1)}, u32[]{:S(2)}, u32[]{:S(2)}) collective-permute-start(bf16[256,1024]{1,0:T(8,128)(2,1)S(1)} %constant_dynamic-update-slice_fusion), channel_id=1, source_target_pairs={{0,1},{1,2},{2,3},{3,0},{4,5},{5,6},{6,7},{7,4},{8,9},{9,10},{10,1... | collective-permute-start | bytes 1572872 | tf_op jit(solution)/shard_map/ppermute | solution.py:15
  39.9 29.5 %collective-permute-start = (bf16[256,1024]{1,0:T(8,128)(2,1)S(1)}, bf16[256,1024]{1,0:T(8,128)(2,1)}, u32[]{:S(2)}, u32[]{:S(2)}) collective-permute-start(bf16[256,1024]{1,0:T(8,128)(2,1)S(1)} %constant_dynamic-update-slice_fusion), channel_id=1, source_target_pairs={{0,4},{4,0},{8,12},{12,8},{16,20},{20,16},{24,28},{28,24},{32,36},... | collective-permute-start | bytes 1572872 | tf_op jit(solution)/shard_map/ppermute | solution.py:10
  60.9 13.0 %collective-permute-start.2 = (bf16[256,1024]{1,0:T(8,128)(2,1)}, bf16[256,1024]{1,0:T(8,128)(2,1)S(1)}, u32[]{:S(2)}, u32[]{:S(2)}) collective-permute-start(bf16[256,1024]{1,0:T(8,128)(2,1)} %collective-permute-done.1), channel_id=1, source_target_pairs={{0,4},{4,0},{8,12},{12,8},{16,20},{20,16},{24,28},{28,24},{32,36},... | collective-permute-start | bytes 1572872 | tf_op jit(solution)/shard_map/ppermute | solution.py:10
  62.2 10.7 %collective-permute-start.6 = (bf16[256,1024]{1,0:T(8,128)(2,1)}, bf16[256,1024]{1,0:T(8,128)(2,1)S(1)}, u32[]{:S(2)}, u32[]{:S(2)}) collective-permute-start(bf16[256,1024]{1,0:T(8,128)(2,1)} %collective-permute-done.5), channel_id=1, source_target_pairs={{0,4},{4,0},{8,12},{12,8},{16,20},{20,16},{24,28},{28,24},{32,36},... | collective-permute-start | bytes 1572872 | tf_op jit(solution)/shard_map/ppermute | solution.py:10
  65.5 10.3 %collective-permute-start.4 = (bf16[256,1024]{1,0:T(8,128)(2,1)}, bf16[256,1024]{1,0:T(8,128)(2,1)S(1)}, u32[]{:S(2)}, u32[]{:S(2)}) collective-permute-start(bf16[256,1024]{1,0:T(8,128)(2,1)} %collective-permute-done.3), channel_id=1, source_target_pairs={{0,4},{4,0},{8,12},{12,8},{16,20},{20,16},{24,28},{28,24},{32,36},... | collective-permute-start | bytes 1572872 | tf_op jit(solution)/shard_map/ppermute | solution.py:10
  67.1 3.3 %copy-start.2 = (bf16[1,512,2048]{2,1,0:T(8,128)(2,1)S(1)}, bf16[1,512,2048]{2,1,0:T(8,128)(2,1)}, u32[]{:S(2)}) copy-start(bf16[1,512,2048]{2,1,0:T(8,128)(2,1)} %param.15) | copy-start | bytes 6291460
  73.0 21.9 %copy-start.3 = (bf16[512,1024]{1,0:T(8,128)(2,1)}, bf16[512,1024]{1,0:T(8,128)(2,1)S(1)}, u32[]{:S(2)}) copy-start(bf16[512,1024]{1,0:T(8,128)(2,1)S(1)} %constant_dynamic-update-slice_fusion.6) | copy-start | bytes 3145732
  74.0 15.6 %copy-start.5 = (bf16[512,1024]{1,0:T(8,128)(2,1)}, bf16[512,1024]{1,0:T(8,128)(2,1)S(1)}, u32[]{:S(2)}) copy-start(bf16[512,1024]{1,0:T(8,128)(2,1)S(1)} %constant_dynamic-update-slice_fusion.2) | copy-start | bytes 3145732
  75.9 18.5 %copy-start.9 = (bf16[512,1024]{1,0:T(8,128)(2,1)}, bf16[512,1024]{1,0:T(8,128)(2,1)S(1)}, u32[]{:S(2)}) copy-start(bf16[512,1024]{1,0:T(8,128)(2,1)S(1)} %constant_dynamic-update-slice_fusion.4) | copy-start | bytes 3145732
  84.7 5.6 %collective-permute-start.7 = (f32[256,1024]{0,1:T(8,128)S(1)}, f32[256,1024]{0,1:T(8,128)S(1)}, u32[]{:S(2)}, u32[]{:S(2)}) collective-permute-start(f32[256,1024]{0,1:T(8,128)S(1)} %pad_maximum_fusion.3), channel_id=1, source_target_pairs={{0,4},{4,0},{8,12},{12,8},{16,20},{20,16},{24,28},{28,24},{32,36},... | collective-permute-start | bytes 3145736 | tf_op jit(solution)/shard_map/ppermute | solution.py:10
  85.4 5.8 %collective-permute-start.9 = (f32[256,1024]{0,1:T(8,128)S(1)}, f32[256,1024]{0,1:T(8,128)S(1)}, u32[]{:S(2)}, u32[]{:S(2)}) collective-permute-start(f32[256,1024]{0,1:T(8,128)S(1)} %pad_maximum_fusion.2), channel_id=1, source_target_pairs={{0,4},{4,0},{8,12},{12,8},{16,20},{20,16},{24,28},{28,24},{32,36},... | collective-permute-start | bytes 3145736 | tf_op jit(solution)/shard_map/ppermute | solution.py:10
  86.5 5.3 %collective-permute-start.11 = (f32[256,1024]{0,1:T(8,128)S(1)}, f32[256,1024]{0,1:T(8,128)S(1)}, u32[]{:S(2)}, u32[]{:S(2)}) collective-permute-start(f32[256,1024]{0,1:T(8,128)S(1)} %pad_maximum_fusion.1), channel_id=1, source_target_pairs={{0,4},{4,0},{8,12},{12,8},{16,20},{20,16},{24,28},{28,24},{32,36},... | collective-permute-start | bytes 3145736 | tf_op jit(solution)/shard_map/ppermute | solution.py:10
  87.2 8.2 %collective-permute-start.13 = (f32[256,1024]{0,1:T(8,128)S(1)}, f32[256,1024]{0,1:T(8,128)S(1)}, u32[]{:S(2)}, u32[]{:S(2)}) collective-permute-start(f32[256,1024]{0,1:T(8,128)S(1)} %pad_maximum_fusion), channel_id=1, source_target_pairs={{0,4},{4,0},{8,12},{12,8},{16,20},{20,16},{24,28},{28,24},{32,36},... | collective-permute-start | bytes 3145736 | tf_op jit(solution)/shard_map/ppermute | solution.py:10
  90.5 15.2 %collective-permute-start.8 = (bf16[256,1024]{0,1:T(8,128)(2,1)S(1)}, bf16[256,1024]{0,1:T(8,128)(2,1)S(1)}, u32[]{:S(2)}, u32[]{:S(2)}) collective-permute-start(bf16[256,1024]{0,1:T(8,128)(2,1)S(1)} %fusion.41), channel_id=1, source_target_pairs={{0,2},{1,3},{2,0},{3,1},{4,6},{5,7},{6,4},{7,5},{8,10},{9,11},{10,... | collective-permute-start | bytes 1572872 | tf_op jit(solution)/shard_map/ppermute | solution.py:15
  91.4 25.9 %collective-permute-start.10 = (bf16[256,1024]{0,1:T(8,128)(2,1)S(1)}, bf16[256,1024]{0,1:T(8,128)(2,1)S(1)}, u32[]{:S(2)}, u32[]{:S(2)}) collective-permute-start(bf16[256,1024]{0,1:T(8,128)(2,1)S(1)} %fusion.38), channel_id=1, source_target_pairs={{0,1},{1,2},{2,3},{3,0},{4,5},{5,6},{6,7},{7,4},{8,9},{9,10},{10,1... | collective-permute-start | bytes 1572872 | tf_op jit(solution)/shard_map/ppermute | solution.py:15
  92.1 25.2 %collective-permute-start.12 = (bf16[256,1024]{0,1:T(8,128)(2,1)S(1)}, bf16[256,1024]{0,1:T(8,128)(2,1)S(1)}, u32[]{:S(2)}, u32[]{:S(2)}) collective-permute-start(bf16[256,1024]{0,1:T(8,128)(2,1)S(1)} %fusion.35), channel_id=1, source_target_pairs={{0,3},{1,0},{2,1},{3,2},{4,7},{5,4},{6,5},{7,6},{8,11},{9,8},{10,9... | collective-permute-start | bytes 1572872 | tf_op jit(solution)/shard_map/ppermute | solution.py:15
  95.4 22.2 %copy-start.12 = (bf16[1,2048,512]{2,1,0:T(8,128)(2,1)}, bf16[1,2048,512]{2,1,0:T(8,128)(2,1)S(1)}, u32[]{:S(2)}) copy-start(bf16[1,2048,512]{2,1,0:T(8,128)(2,1)S(1)} %fusion.19) | copy-start | bytes 6291460
  124.6 23.5 %all-to-all-start.1 = ((bf16[2,64,4,512]{3,2,0,1:T(4,128)(2,1)}), bf16[2,64,4,512]{3,2,0,1:T(4,128)(2,1)}, u32[]{:S(2)}, u32[]{:S(2)}) async-start(bf16[2,64,4,512]{3,2,0,1:T(4,128)(2,1)} %copy.22), calls=%async_computation.1 | async-start | bytes 1048576 | tf_op jit(solution)/shard_map/all_to_all | solution.py:149
  130.9 2.7 %copy-start.6 = (bf16[512,1024]{1,0:T(8,128)(2,1)S(1)}, bf16[512,1024]{1,0:T(8,128)(2,1)}, u32[]{:S(2)}) copy-start(bf16[512,1024]{1,0:T(8,128)(2,1)} %copy-done.5) | copy-start | bytes 3145732
  133.6 2.6 %copy-start.4 = (bf16[512,1024]{1,0:T(8,128)(2,1)S(1)}, bf16[512,1024]{1,0:T(8,128)(2,1)}, u32[]{:S(2)}) copy-start(bf16[512,1024]{1,0:T(8,128)(2,1)} %copy-done.3) | copy-start | bytes 3145732
  (4 other events, 7.0 us)
